TPU v7x, 256 devices: a whole 4x4x8 slice. The times are simulated.
256 devices in a mesh: blk: 8 (over x, y_hi), batch: 32 (over y_lo, z, core).
Axes of the slice: x: 4, y: 4 (y_hi: 2, y_lo: 2; y = y_hi * 2 + y_lo), z: 8, core: 2. Of those that a mesh axis runs over, the one named last changes fastest.
Arguments:
- frame_one: bfloat16 [32, 4096, 128], P('batch', 'blk'), may hold values from -40 to 40
- frame_two: bfloat16 [32, 4096, 128], P('batch', 'blk'), may hold values from -40 to 40
- encoder_weight: bfloat16 [128, 256], replicated, may hold values from -0.5 to 0.5
- flow_grad: float32 [32, 2, 4096], P('batch', None, 'blk'), may hold values from -6 to 6
Outputs:
- flow: float32 [32, 2, 4096], P('batch', None, 'blk')
- grad_w: float32 [128, 256], replicated
All inputs are finite; a program needn't handle non-finite values.
Results may differ from a plain program's by a relative error of at most 0.01.
Values may be sent and summed in bfloat16 or wider, within the bound.
No kernel may reach another device: no remote copies, remote signals or barrier semaphores. Data moves between devices by JAX's collectives and lax.ppermute only.
A program may use at most 64 MiB of HBM per device.

v0:
```python
import jax
import jax.numpy as jnp
from jax import lax
from jax.sharding import PartitionSpec as P

WIDTH = 240


def grid_coords(start, count):
    position = start + jnp.arange(count, dtype=jnp.int32)
    col_coord = (position % WIDTH).astype(jnp.float32) / 64.0
    row_coord = (position // WIDTH).astype(jnp.float32) / 8.0
    return (col_coord, row_coord)


def body(frame_one, frame_two, encoder_weight, flow_grad):
    first_in = frame_one[0]
    second_in = frame_two[0]
    grad_col = flow_grad[0, 0]
    grad_row = flow_grad[0, 1]
    query_count = first_in.shape[0]
    channels = encoder_weight.shape[1]
    scaling = channels ** (-0.5)
    first_feat = jnp.dot(first_in, encoder_weight, preferred_element_type=jnp.float32).astype(
        jnp.bfloat16
    )
    second_feat = jnp.dot(second_in, encoder_weight, preferred_element_type=jnp.float32).astype(
        jnp.bfloat16
    )
    own_col, own_row = grid_coords(lax.axis_index("blk") * query_count, query_count)
    zero_rows = jnp.zeros((query_count,), jnp.float32)
    forward_run_max = jnp.full((query_count,), -jnp.inf, jnp.float32)
    forward_run_sum = zero_rows
    sum_col = zero_rows
    sum_row = zero_rows
    key_feat = lax.all_gather(second_feat, "blk", axis=0, tiled=True)
    logits = scaling * jnp.dot(first_feat, key_feat.T, preferred_element_type=jnp.float32)
    key_col, key_row = grid_coords(jnp.int32(0), key_feat.shape[0])
    new_max = jnp.max(logits, axis=1)
    rescale = jnp.exp(forward_run_max - new_max)
    expo = jnp.exp(logits - new_max[:, None])
    forward_run_sum = forward_run_sum * rescale + jnp.sum(expo, axis=1)
    sum_col = sum_col * rescale + jnp.sum(expo * key_col[None, :], axis=1)
    sum_row = sum_row * rescale + jnp.sum(expo * key_row[None, :], axis=1)
    stats = (new_max, forward_run_sum, sum_col, sum_row)
    run_max, run_sum, sum_col, sum_row = stats
    mean_col = sum_col / run_sum
    mean_row = sum_row / run_sum
    inner = grad_col * mean_col + grad_row * mean_row
    flow = jnp.stack([mean_col - own_col, mean_row - own_row])[None]
    key_feat = lax.all_gather(second_feat, "blk", axis=0, tiled=True)
    logits = scaling * jnp.dot(first_feat, key_feat.T, preferred_element_type=jnp.float32)
    probs = jnp.exp(logits - run_max[:, None]) / run_sum[:, None]
    key_col, key_row = grid_coords(jnp.int32(0), key_feat.shape[0])
    slope = (
        probs
        * (
            grad_col[:, None] * key_col[None, :]
            + grad_row[:, None] * key_row[None, :]
            - inner[:, None]
        )
    ).astype(jnp.bfloat16)
    first_accum = jnp.dot(slope, key_feat, preferred_element_type=jnp.float32)
    first_accum, slope_store = (first_accum, slope)
    delta_one = (scaling * first_accum).astype(jnp.bfloat16)
    local_grad = jnp.dot(first_in.T, delta_one, preferred_element_type=jnp.float32)
    delta_two = lax.psum_scatter(
        scaling * jnp.dot(slope_store.T, first_feat, preferred_element_type=jnp.float32),
        "blk",
        scatter_dimension=0,
        tiled=True,
    )
    second_term = jnp.dot(
        second_in.astype(jnp.float32).T,
        delta_two,
        precision=lax.Precision.HIGHEST,
        preferred_element_type=jnp.float32,
    )
    local_grad = local_grad + second_term
    grad_w = lax.psum(local_grad, ("blk", "batch"))
    return (flow, grad_w)


def solution(mesh):
    placed = (P("batch", "blk", None), P("batch", "blk", None), P(), P("batch", None, "blk"))
    return jax.shard_map(
        body, mesh=mesh, in_specs=placed, out_specs=(P("batch", None, "blk"), P()), check_vma=False
    )
```

profile of v0, /device:TPU:1, one launch (start us, length us, event | category | flops | bytes accessed | tf_op | source)
XLA Modules:
  0.0 437.2 jit_solution(4563758125745906845)
XLA Ops:
  7.2 0.0 copy-start
  7.2 0.0 all-gather.2.cloned.1.call-start
  7.2 1.8 convolution_convert_fusion
  9.1 0.0 all-gather.2.cloned.1.call-update
  9.1 0.0 reduce-scatter.2.cloned.1.call-start
  9.2 0.8 fusion.24
  9.9 0.0 copy-done
  9.9 1.0 convolution_convert_fusion.1
  11.0 62.1 %all-gather.2.cloned.1.call-done = bf16[4096,256]{1,0:T(8,128)(2,1)} async-done(((bf16[512,256]{1,0:T(8,128)(2,1)}), bf16[4096,256]{1,0:T(8,128)(2,1)}) %all-gather.2.cloned.1.call-update) | async-done | bytes 2097168 | tf_op jit(solution)/shard_map/all_gather | solution.py:36
  73.1 3.0 multiply_reduce_fusion.2
  76.0 3.1 multiply_reduce_fusion.1
  79.1 4.2 multiply_convert_fusion
  83.3 0.0 copy-start.1
  83.4 1.9 copy-done.1
  85.3 3.3 convolution_multiply_fusion
  88.5 0.0 reduce-scatter.2.cloned.1.call-update
  88.6 0.0 all-reduce.2.cloned.1.call-start
  88.7 3.7 fusion.2
  92.4 85.6 %reduce-scatter.2.cloned.1.call-done = f32[512,256]{1,0:T(8,128)} async-done(((f32[4096,256]{1,0:T(8,128)}), f32[512,256]{1,0:T(8,128)}) %reduce-scatter.2.cloned.1.call-update) | async-done | bytes 524304 | tf_op jit(solution)/shard_map/reduce_scatter | solution.py:67
  178.0 2.3 fusion.1
  180.3 0.0 all-reduce.2.cloned.1.call-update
  180.3 0.6 maximum_bitcast_fusion
  180.9 248.1 %all-reduce.2.cloned.1.call-done = f32[128,256]{0,1:T(8,128)} async-done(((f32[128,256]{0,1:T(8,128)}), f32[128,256]{0,1:T(8,128)}) %all-reduce.2.cloned.1.call-update) | async-done | bytes 131088 | tf_op jit(solution)/shard_map/psum | solution.py:80
  429.1 1.7 copy.6
  (8 shorter events, 0.1 us)
Async XLA Ops:
  7.2 2.8 copy-start
  7.2 65.9 %all-gather.2.cloned.1.call-start = ((), (), s32[]{:S(2)}) async-start(), calls=%async_computation.1 | async-start | bytes 2359296 | tf_op jit(solution)/shard_map/all_gather | solution.py:36
  9.1 168.9 %reduce-scatter.2.cloned.1.call-start = ((), (), s32[]{:S(2)}) async-start(), calls=%async_computation.2 | async-start | bytes 4718592 | tf_op jit(solution)/shard_map/reduce_scatter | solution.py:67
  83.3 1.9 copy-start.1
  85.3 3.4 copy-start.2
  88.5 89.4 %copy-start.3 = (bf16[1,512,128]{2,1,0:T(8,128)(2,1)S(1)}, bf16[1,512,128]{2,1,0:T(8,128)(2,1)}, u32[]{:S(2)}) copy-start(bf16[1,512,128]{2,1,0:T(8,128)(2,1)} %param.5) | copy-start | bytes 393220
  88.6 340.5 %all-reduce.2.cloned.1.call-start = ((), (), s32[]{:S(2)}) async-start(), calls=%async_computation.3 | async-start | bytes 262144 | tf_op jit(solution)/shard_map/psum | solution.py:80
Sparse Core Ops, SparseCore 0:
  10.6 62.4 all-gather.1
  88.7 89.2 reduce-scatter.1
  184.1 244.9 all-reduce.1
where the time goes:
time: 438 us; the launch traced here: 437 us
  waiting for transfers between devices  396 us (90%)
  matrix products  15.1 us (3%)
  between operations  13.8 us (3%)
  other arithmetic  7.96 us (2%)
  local copies, waits for them, and re-layouts  4.38 us (1%)
    psum x1, waiting for transfers between devices, body(): grad_w = lax.psum(local_grad, ('blk', 'batch'))  248 us
    reduce_scatter x1, waiting for transfers between devices, body(): lax.psum_scatter(scaling * jnp.dot(slope_store.T, first_feat, preferred_e...  85.6 us
    all_gather x1, waiting for transfers between devices, body(): key_feat = lax.all_gather(second_feat, 'blk', axis=0, tiled=True)  62.1 us
  transfers between devices with their start and end apart: 3, of which 3 were waited for; matrix products, arithmetic and copies ran while one was open for 1% of the time, Pallas kernels for 0%

commit v1 on v0

v1 whole, which is shorter than its diff:
```python
import jax
import jax.numpy as jnp
from jax import lax
from jax.sharding import PartitionSpec as P

WIDTH = 240


def coords_of(position):
    col_coord = (position % WIDTH).astype(jnp.float32) / 64.0
    row_coord = (position // WIDTH).astype(jnp.float32) / 8.0
    return (col_coord, row_coord)


def butterfly_sum(x, axis, n):
    k = 1
    while k < n:
        x = x + lax.ppermute(x, axis, [(i, i ^ k) for i in range(n)])
        k *= 2
    return x


def body(frame_one, frame_two, encoder_weight, flow_grad, n_blk, n_batch):
    first_in = frame_one[0]
    second_in = frame_two[0]
    grad_col = flow_grad[0, 0]
    grad_row = flow_grad[0, 1]
    query_count = first_in.shape[0]
    channels = encoder_weight.shape[1]
    scaling = channels ** (-0.5)
    blk = lax.axis_index("blk")

    parts = [second_in] + [
        lax.ppermute(second_in, "blk", [(i, (i + k) % n_blk) for i in range(n_blk)])
        for k in range(1, n_blk)
    ]
    key_in = jnp.concatenate(parts, axis=0)
    source = (blk - jnp.arange(n_blk, dtype=jnp.int32)) % n_blk
    key_pos = (source[:, None] * query_count + jnp.arange(query_count, dtype=jnp.int32)[None, :]).reshape(-1)
    key_col, key_row = coords_of(key_pos)
    own_col, own_row = coords_of(blk * query_count + jnp.arange(query_count, dtype=jnp.int32))

    first_feat = jnp.dot(first_in, encoder_weight, preferred_element_type=jnp.float32).astype(jnp.bfloat16)
    key_feat = jnp.dot(key_in, encoder_weight, preferred_element_type=jnp.float32).astype(jnp.bfloat16)

    logits = scaling * jnp.dot(first_feat, key_feat.T, preferred_element_type=jnp.float32)
    top = jnp.max(logits, axis=1, keepdims=True)
    expo = jnp.exp(logits - top)
    total = jnp.sum(expo, axis=1, keepdims=True)
    probs = expo / total
    mean_col = jnp.sum(probs * key_col[None, :], axis=1)
    mean_row = jnp.sum(probs * key_row[None, :], axis=1)
    flow = jnp.stack([mean_col - own_col, mean_row - own_row])[None]

    inner = grad_col * mean_col + grad_row * mean_row
    slope = (
        probs * (grad_col[:, None] * key_col[None, :] + grad_row[:, None] * key_row[None, :] - inner[:, None])
    ).astype(jnp.bfloat16)
    delta_one = (scaling * jnp.dot(slope, key_feat, preferred_element_type=jnp.float32)).astype(jnp.bfloat16)
    key_term = scaling * jnp.dot(slope.T, first_feat, preferred_element_type=jnp.float32)
    local_grad = jnp.dot(first_in.T, delta_one, preferred_element_type=jnp.float32)
    local_grad = local_grad + jnp.dot(
        key_in.astype(jnp.float32).T,
        key_term,
        precision=lax.Precision.HIGHEST,
        preferred_element_type=jnp.float32,
    )
    grad_w = butterfly_sum(butterfly_sum(local_grad, "blk", n_blk), "batch", n_batch)
    return (flow, grad_w)


def solution(mesh):
    placed = (P("batch", "blk", None), P("batch", "blk", None), P(), P("batch", None, "blk"))
    n_blk = mesh.shape["blk"]
    n_batch = mesh.shape["batch"]

    def step(frame_one, frame_two, encoder_weight, flow_grad):
        return body(frame_one, frame_two, encoder_weight, flow_grad, n_blk, n_batch)

    return jax.shard_map(
        step, mesh=mesh, in_specs=placed, out_specs=(P("batch", None, "blk"), P()), check_vma=False
    )
```

time: 438 us -> 103 us (0.24)
  the two profiles are of different devices: /device:TPU:1 before, /device:TPU:2 now
where the time goes in v1:
time: 103 us
  waiting for transfers between devices  41.5 us (40%)
  starting transfers between devices  31.8 us (31%)
  matrix products  16.5 us (16%)
  other arithmetic  7.86 us (8%)
  local copies, waits for them, and re-layouts  4.58 us (4%)
    ppermute x8, waiting for transfers between devices, butterfly_sum(): x = x + lax.ppermute(x, axis, [(i, i ^ k) for i in range(n)])  35.5 us
    ppermute x8, starting transfers between devices, butterfly_sum(): x = x + lax.ppermute(x, axis, [(i, i ^ k) for i in range(n)])  17.1 us
    ppermute x7, starting transfers between devices, body(): lax.ppermute(second_in, 'blk', [(i, (i + k) % n_blk) for i in range(n_blk)])  14.6 us
    ppermute x7, waiting for transfers between devices, body(): lax.ppermute(second_in, 'blk', [(i, (i + k) % n_blk) for i in range(n_blk)])  6.03 us
    dot_general x1, matrix products, body(): jnp.dot(key_in.astype(jnp.float32).T, key_term, precision=lax.Precision.H...  5.62 us
    unnamed x15, local copies, waits for them, and re-layouts  3.79 us
    dot_general x1, matrix products, body(): jnp.dot(first_in.T, delta_one, preferred_element_type=jnp.float32)  3.72 us
    dot_general x1, matrix products, body(): jnp.dot(slope.T, first_feat, preferred_element_type=jnp.float32)  3.26 us
  transfers between devices with their start and end apart: 15, of which 11 were waited for; matrix products, arithmetic and copies ran while one was open for 4% of the time, Pallas kernels for 0%

profile of v1, /device:TPU:2, one launch (start us, length us, event | category | flops | bytes accessed | tf_op | source)
XLA Modules:
  0.0 103.1 jit_solution(798704255785991040)
XLA Ops:
  0.6 3.3 %collective-permute-start = (bf16[512,128]{1,0:T(8,128)(2,1)}, bf16[512,128]{1,0:T(8,128)(2,1)S(1)}, u32[]{:S(2)}, u32[]{:S(2)}) collective-permute-start(bf16[512,128]{1,0:T(8,128)(2,1)} %bitcast.35), channel_id=1, source_target_pairs={{0,32},{32,64},{64,96},{96,128},{128,160},{160,192},{192,224},{224... | collective-permute-start | bytes 393224 | tf_op jit(solution)/shard_map/ppermute | solution.py:34
  5.4 2.6 %collective-permute-start.2 = (bf16[512,128]{1,0:T(8,128)(2,1)}, bf16[512,128]{1,0:T(8,128)(2,1)S(1)}, u32[]{:S(2)}, u32[]{:S(2)}) collective-permute-start(bf16[512,128]{1,0:T(8,128)(2,1)} %bitcast.37), channel_id=1, source_target_pairs={{0,96},{32,128},{64,160},{96,192},{128,224},{160,0},{192,32},{224,... | collective-permute-start | bytes 393224 | tf_op jit(solution)/shard_map/ppermute | solution.py:34
  8.7 3.7 %collective-permute-start.4 = (bf16[512,128]{1,0:T(8,128)(2,1)}, bf16[512,128]{1,0:T(8,128)(2,1)S(1)}, u32[]{:S(2)}, u32[]{:S(2)}) collective-permute-start(bf16[512,128]{1,0:T(8,128)(2,1)} %bitcast.39), channel_id=1, source_target_pairs={{0,160},{32,192},{64,224},{96,0},{128,32},{160,64},{192,96},{224,1... | collective-permute-start | bytes 393224 | tf_op jit(solution)/shard_map/ppermute | solution.py:34
  15.5 2.2 %collective-permute-start.5 = (bf16[512,128]{1,0:T(8,128)(2,1)}, bf16[512,128]{1,0:T(8,128)(2,1)S(1)}, u32[]{:S(2)}, u32[]{:S(2)}) collective-permute-start(bf16[512,128]{1,0:T(8,128)(2,1)} %bitcast.40), channel_id=1, source_target_pairs={{0,192},{32,224},{64,0},{96,32},{128,64},{160,96},{192,128},{224,1... | collective-permute-start | bytes 393224 | tf_op jit(solution)/shard_map/ppermute | solution.py:34
  19.9 2.2 %collective-permute-done.5 = bf16[512,128]{1,0:T(8,128)(2,1)S(1)} collective-permute-done((bf16[512,128]{1,0:T(8,128)(2,1)}, bf16[512,128]{1,0:T(8,128)(2,1)S(1)}, u32[]{:S(2)}, u32[]{:S(2)}) %collective-permute-start.5) | collective-permute-done | bytes 131104 | tf_op jit(solution)/shard_map/ppermute | solution.py:34
  22.1 2.3 %collective-permute-done.6 = bf16[512,128]{1,0:T(8,128)(2,1)S(1)} collective-permute-done((bf16[512,128]{1,0:T(8,128)(2,1)}, bf16[512,128]{1,0:T(8,128)(2,1)S(1)}, u32[]{:S(2)}, u32[]{:S(2)}) %collective-permute-start.6) | collective-permute-done | bytes 131104 | tf_op jit(solution)/shard_map/ppermute | solution.py:34
  28.9 3.1 %multiply_reduce_fusion.1 = (f32[512]{0:T(512)S(1)}, f32[512]{0:T(512)S(1)}, f32[512,4096]{1,0:T(8,128)S(1)}) fusion(f32[4096]{0:T(1024)S(1)} %get-tuple-element.8, f32[4096]{0:T(1024)S(1)} %get-tuple-element.7, f32[512]{0:T(512)S(1)} %fusion.1, f32[512]{0:T(512)S(1)} %get-tuple-element.13, f32[512,4096]{1,0:T(8,128)S(1)} %get-tuple-element.14), kind=kLoop, calls=%fused_computation.2 | loop fusion | flops 14679040 | bytes 16818176 | tf_op jit(solution)/shard_map/reduce_sum | solution.py:51
  32.1 2.3 %multiply_convert_fusion = bf16[512,4096]{1,0:T(8,128)(2,1)S(1)} fusion(f32[512,4096]{1,0:T(8,128)S(1)} %get-tuple-element.6, f32[512]{0:T(512)S(1)} %multiply_add_fusion, f32[512]{0:T(512)S(1)} %bitcast.47, f32[512]{0:T(512)S(1)} %bitcast.45, f32[4096]{0:T(1024)S(1)} %get-tuple-element.7, f32[4096]{0:T(1024)S(1)} %get-tuple-element.8), kind=kLoop, calls=%fused_computation | loop fusion | flops 12582912 | bytes 12621824 | tf_op jit(solution)/shard_map/convert_element_type | solution.py:58
  34.4 1.9 %copy-done.1 = bf16[512,4096]{1,0:T(8,128)(2,1)} copy-done((bf16[512,4096]{1,0:T(8,128)(2,1)}, bf16[512,4096]{1,0:T(8,128)(2,1)S(1)}, u32[]{:S(2)}) %copy-start.1) | copy-done | bytes 4194328
  36.3 3.3 %convolution_multiply_fusion = f32[4096,256]{1,0:T(8,128)} fusion(bf16[512,4096]{1,0:T(8,128)(2,1)S(1)} %multiply_convert_fusion, bf16[512,256]{1,0:T(8,128)(2,1)S(1)} %convolution_convert_fusion.1), kind=kOutput, calls=%fused_computation.7 | convolution fusion | flops 1074790400 | bytes 8650752 | tf_op jit(solution)/shard_map/dot_general | solution.py:60
  39.6 3.7 %convolution_bitcast_fusion = f32[128,256]{0,1:T(8,128)S(1)} fusion(bf16[512,4096]{1,0:T(8,128)(2,1)} %copy-done.1, bf16[4096,256]{1,0:T(8,128)(2,1)S(1)} %convolution_convert_fusion, bf16[1,512,128]{2,1,0:T(8,128)(2,1)S(1)} %copy-done), kind=kOutput, calls=%fused_computation.12 | convolution fusion | flops 1107558400 | bytes 6553600 | tf_op jit(solution)/shard_map/dot_general | solution.py:61
  43.3 5.6 %convolution_add_fusion = f32[128,256]{0,1:T(8,128)S(1)} fusion(f32[128,256]{0,1:T(8,128)S(1)} %convolution_bitcast_fusion, bf16[4096,128]{1,0:T(8,128)(2,1)S(1)} %constant_dynamic-update-slice_fusion, f32[4096,256]{1,0:T(8,128)} %convolution_multiply_fusion), kind=kOutput, calls=%fused_computation.13 | convolution fusion | flops 1610645504 | bytes 5505024 | tf_op jit(solution)/shard_map/dot_general | solution.py:62
  48.9 2.2 %collective-permute-start.7 = (f32[128,256]{0,1:T(8,128)S(1)}, f32[128,256]{0,1:T(8,128)S(1)}, u32[]{:S(2)}, u32[]{:S(2)}) collective-permute-start(f32[128,256]{0,1:T(8,128)S(1)} %convolution_add_fusion), channel_id=1, source_target_pairs={{0,32},{32,0},{64,96},{96,64},{128,160},{160,128},{192,224},{224,1... | collective-permute-start | bytes 393224 | tf_op jit(solution)/shard_map/ppermute | solution.py:18
  51.1 4.4 %collective-permute-done.7 = f32[128,256]{0,1:T(8,128)S(1)} collective-permute-done((f32[128,256]{0,1:T(8,128)S(1)}, f32[128,256]{0,1:T(8,128)S(1)}, u32[]{:S(2)}, u32[]{:S(2)}) %collective-permute-start.7) | collective-permute-done | bytes 131104 | tf_op jit(solution)/shard_map/ppermute | solution.py:18
  55.5 1.5 %collective-permute-start.8 = (f32[128,256]{0,1:T(8,128)S(1)}, f32[128,256]{0,1:T(8,128)S(1)}, u32[]{:S(2)}, u32[]{:S(2)}) collective-permute-start(f32[128,256]{0,1:T(8,128)S(1)} %add.133), channel_id=1, source_target_pairs={{0,64},{32,96},{64,0},{96,32},{128,192},{160,224},{192,128},{224,1... | collective-permute-start | bytes 393224 | tf_op jit(solution)/shard_map/ppermute | solution.py:18
  57.0 4.7 %collective-permute-done.8 = f32[128,256]{0,1:T(8,128)S(1)} collective-permute-done((f32[128,256]{0,1:T(8,128)S(1)}, f32[128,256]{0,1:T(8,128)S(1)}, u32[]{:S(2)}, u32[]{:S(2)}) %collective-permute-start.8) | collective-permute-done | bytes 131104 | tf_op jit(solution)/shard_map/ppermute | solution.py:18
  62.6 5.7 %collective-permute-done.9 = f32[128,256]{0,1:T(8,128)S(1)} collective-permute-done((f32[128,256]{0,1:T(8,128)S(1)}, f32[128,256]{0,1:T(8,128)S(1)}, u32[]{:S(2)}, u32[]{:S(2)}) %collective-permute-start.9) | collective-permute-done | bytes 131104 | tf_op jit(solution)/shard_map/ppermute | solution.py:18
  69.7 2.0 %collective-permute-start.11 = (f32[128,256]{0,1:T(8,128)S(1)}, f32[128,256]{0,1:T(8,128)S(1)}, u32[]{:S(2)}, u32[]{:S(2)}) collective-permute-start(f32[128,256]{0,1:T(8,128)S(1)} %add.136), channel_id=1, source_target_pairs={{0,2},{1,3},{2,0},{3,1},{4,6},{5,7},{6,4},{7,5},{8,10},{9,11},{10,... | collective-permute-start | bytes 393224 | tf_op jit(solution)/shard_map/ppermute | solution.py:18
  71.7 3.8 %collective-permute-done.11 = f32[128,256]{0,1:T(8,128)S(1)} collective-permute-done((f32[128,256]{0,1:T(8,128)S(1)}, f32[128,256]{0,1:T(8,128)S(1)}, u32[]{:S(2)}, u32[]{:S(2)}) %collective-permute-start.11) | collective-permute-done | bytes 131104 | tf_op jit(solution)/shard_map/ppermute | solution.py:18
  75.6 3.4 %collective-permute-start.12 = (f32[128,256]{0,1:T(8,128)S(1)}, f32[128,256]{0,1:T(8,128)S(1)}, u32[]{:S(2)}, u32[]{:S(2)}) collective-permute-start(f32[128,256]{0,1:T(8,128)S(1)} %add.137), channel_id=1, source_target_pairs={{0,4},{1,5},{2,6},{3,7},{4,0},{5,1},{6,2},{7,3},{8,12},{9,13},{10,... | collective-permute-start | bytes 393224 | tf_op jit(solution)/shard_map/ppermute | solution.py:18
  78.9 5.9 %collective-permute-done.12 = f32[128,256]{0,1:T(8,128)S(1)} collective-permute-done((f32[128,256]{0,1:T(8,128)S(1)}, f32[128,256]{0,1:T(8,128)S(1)}, u32[]{:S(2)}, u32[]{:S(2)}) %collective-permute-start.12) | collective-permute-done | bytes 131104 | tf_op jit(solution)/shard_map/ppermute | solution.py:18
  84.9 6.3 %collective-permute-start.13 = (f32[128,256]{0,1:T(8,128)S(1)}, f32[128,256]{0,1:T(8,128)S(1)}, u32[]{:S(2)}, u32[]{:S(2)}) collective-permute-start(f32[128,256]{0,1:T(8,128)S(1)} %add.138), channel_id=1, source_target_pairs={{0,8},{1,9},{2,10},{3,11},{4,12},{5,13},{6,14},{7,15},{8,0},{9,1},... | collective-permute-start | bytes 393224 | tf_op jit(solution)/shard_map/ppermute | solution.py:18
  91.2 6.1 %collective-permute-done.13 = f32[128,256]{0,1:T(8,128)S(1)} collective-permute-done((f32[128,256]{0,1:T(8,128)S(1)}, f32[128,256]{0,1:T(8,128)S(1)}, u32[]{:S(2)}, u32[]{:S(2)}) %collective-permute-start.13) | collective-permute-done | bytes 131104 | tf_op jit(solution)/shard_map/ppermute | solution.py:18
  98.7 3.7 %collective-permute-done.14 = f32[128,256]{0,1:T(8,128)S(1)} collective-permute-done((f32[128,256]{0,1:T(8,128)S(1)}, f32[128,256]{0,1:T(8,128)S(1)}, u32[]{:S(2)}, u32[]{:S(2)}) %collective-permute-start.14) | collective-permute-done | bytes 131104 | tf_op jit(solution)/shard_map/ppermute | solution.py:18
  (47 shorter events, 16.4 us)
Async XLA Ops:
  0.6 13.0 %copy-start = (bf16[1,512,128]{2,1,0:T(8,128)(2,1)S(1)}, bf16[1,512,128]{2,1,0:T(8,128)(2,1)}, u32[]{:S(2)}) copy-start(bf16[1,512,128]{2,1,0:T(8,128)(2,1)} %param.4) | copy-start | bytes 393220
  0.6 14.8 %collective-permute-start = (bf16[512,128]{1,0:T(8,128)(2,1)}, bf16[512,128]{1,0:T(8,128)(2,1)S(1)}, u32[]{:S(2)}, u32[]{:S(2)}) collective-permute-start(bf16[512,128]{1,0:T(8,128)(2,1)} %bitcast.35), channel_id=1, source_target_pairs={{0,32},{32,64},{64,96},{96,128},{128,160},{160,192},{192,224},{224... | collective-permute-start | bytes 393224 | tf_op jit(solution)/shard_map/ppermute | solution.py:34
  3.9 13.8 %collective-permute-start.1 = (bf16[512,128]{1,0:T(8,128)(2,1)}, bf16[512,128]{1,0:T(8,128)(2,1)S(1)}, u32[]{:S(2)}, u32[]{:S(2)}) collective-permute-start(bf16[512,128]{1,0:T(8,128)(2,1)} %bitcast.36), channel_id=1, source_target_pairs={{0,64},{32,96},{64,128},{96,160},{128,192},{160,224},{192,0},{224,... | collective-permute-start | bytes 393224 | tf_op jit(solution)/shard_map/ppermute | solution.py:34
  5.4 13.0 %collective-permute-start.2 = (bf16[512,128]{1,0:T(8,128)(2,1)}, bf16[512,128]{1,0:T(8,128)(2,1)S(1)}, u32[]{:S(2)}, u32[]{:S(2)}) collective-permute-start(bf16[512,128]{1,0:T(8,128)(2,1)} %bitcast.37), channel_id=1, source_target_pairs={{0,96},{32,128},{64,160},{96,192},{128,224},{160,0},{192,32},{224,... | collective-permute-start | bytes 393224 | tf_op jit(solution)/shard_map/ppermute | solution.py:34
  8.0 10.4 %collective-permute-start.3 = (bf16[512,128]{1,0:T(8,128)(2,1)}, bf16[512,128]{1,0:T(8,128)(2,1)S(1)}, u32[]{:S(2)}, u32[]{:S(2)}) collective-permute-start(bf16[512,128]{1,0:T(8,128)(2,1)} %bitcast.38), channel_id=1, source_target_pairs={{0,128},{32,160},{64,192},{96,224},{128,0},{160,32},{192,64},{224,... | collective-permute-start | bytes 393224 | tf_op jit(solution)/shard_map/ppermute | solution.py:34
  8.7 11.2 %collective-permute-start.4 = (bf16[512,128]{1,0:T(8,128)(2,1)}, bf16[512,128]{1,0:T(8,128)(2,1)S(1)}, u32[]{:S(2)}, u32[]{:S(2)}) collective-permute-start(bf16[512,128]{1,0:T(8,128)(2,1)} %bitcast.39), channel_id=1, source_target_pairs={{0,160},{32,192},{64,224},{96,0},{128,32},{160,64},{192,96},{224,1... | collective-permute-start | bytes 393224 | tf_op jit(solution)/shard_map/ppermute | solution.py:34
  15.5 6.7 %collective-permute-start.5 = (bf16[512,128]{1,0:T(8,128)(2,1)}, bf16[512,128]{1,0:T(8,128)(2,1)S(1)}, u32[]{:S(2)}, u32[]{:S(2)}) collective-permute-start(bf16[512,128]{1,0:T(8,128)(2,1)} %bitcast.40), channel_id=1, source_target_pairs={{0,192},{32,224},{64,0},{96,32},{128,64},{160,96},{192,128},{224,1... | collective-permute-start | bytes 393224 | tf_op jit(solution)/shard_map/ppermute | solution.py:34
  17.7 6.8 %collective-permute-start.6 = (bf16[512,128]{1,0:T(8,128)(2,1)}, bf16[512,128]{1,0:T(8,128)(2,1)S(1)}, u32[]{:S(2)}, u32[]{:S(2)}) collective-permute-start(bf16[512,128]{1,0:T(8,128)(2,1)} %bitcast.41), channel_id=1, source_target_pairs={{0,224},{32,0},{64,32},{96,64},{128,96},{160,128},{192,160},{224,1... | collective-permute-start | bytes 393224 | tf_op jit(solution)/shard_map/ppermute | solution.py:34
  34.4 2.0 %copy-start.1 = (bf16[512,4096]{1,0:T(8,128)(2,1)}, bf16[512,4096]{1,0:T(8,128)(2,1)S(1)}, u32[]{:S(2)}) copy-start(bf16[512,4096]{1,0:T(8,128)(2,1)S(1)} %multiply_convert_fusion) | copy-start | bytes 12582916
  48.9 6.6 %collective-permute-start.7 = (f32[128,256]{0,1:T(8,128)S(1)}, f32[128,256]{0,1:T(8,128)S(1)}, u32[]{:S(2)}, u32[]{:S(2)}) collective-permute-start(f32[128,256]{0,1:T(8,128)S(1)} %convolution_add_fusion), channel_id=1, source_target_pairs={{0,32},{32,0},{64,96},{96,64},{128,160},{160,128},{192,224},{224,1... | collective-permute-start | bytes 393224 | tf_op jit(solution)/shard_map/ppermute | solution.py:18
  55.5 6.2 %collective-permute-start.8 = (f32[128,256]{0,1:T(8,128)S(1)}, f32[128,256]{0,1:T(8,128)S(1)}, u32[]{:S(2)}, u32[]{:S(2)}) collective-permute-start(f32[128,256]{0,1:T(8,128)S(1)} %add.133), channel_id=1, source_target_pairs={{0,64},{32,96},{64,0},{96,32},{128,192},{160,224},{192,128},{224,1... | collective-permute-start | bytes 393224 | tf_op jit(solution)/shard_map/ppermute | solution.py:18
  61.7 6.6 %collective-permute-start.9 = (f32[128,256]{0,1:T(8,128)S(1)}, f32[128,256]{0,1:T(8,128)S(1)}, u32[]{:S(2)}, u32[]{:S(2)}) collective-permute-start(f32[128,256]{0,1:T(8,128)S(1)} %add.134), channel_id=1, source_target_pairs={{0,128},{32,160},{64,192},{96,224},{128,0},{160,32},{192,64},{224,... | collective-permute-start | bytes 393224 | tf_op jit(solution)/shard_map/ppermute | solution.py:18
  68.3 1.4 %collective-permute-start.10 = (f32[128,256]{0,1:T(8,128)S(1)}, f32[128,256]{0,1:T(8,128)S(1)}, u32[]{:S(2)}, u32[]{:S(2)}) collective-permute-start(f32[128,256]{0,1:T(8,128)S(1)} %add.135), channel_id=1, source_target_pairs={{0,1},{1,0},{2,3},{3,2},{4,5},{5,4},{6,7},{7,6},{8,9},{9,8},{10,11... | collective-permute-start | bytes 393224 | tf_op jit(solution)/shard_map/ppermute | solution.py:18
  69.7 5.8 %collective-permute-start.11 = (f32[128,256]{0,1:T(8,128)S(1)}, f32[128,256]{0,1:T(8,128)S(1)}, u32[]{:S(2)}, u32[]{:S(2)}) collective-permute-start(f32[128,256]{0,1:T(8,128)S(1)} %add.136), channel_id=1, source_target_pairs={{0,2},{1,3},{2,0},{3,1},{4,6},{5,7},{6,4},{7,5},{8,10},{9,11},{10,... | collective-permute-start | bytes 393224 | tf_op jit(solution)/shard_map/ppermute | solution.py:18
  75.6 9.3 %collective-permute-start.12 = (f32[128,256]{0,1:T(8,128)S(1)}, f32[128,256]{0,1:T(8,128)S(1)}, u32[]{:S(2)}, u32[]{:S(2)}) collective-permute-start(f32[128,256]{0,1:T(8,128)S(1)} %add.137), channel_id=1, source_target_pairs={{0,4},{1,5},{2,6},{3,7},{4,0},{5,1},{6,2},{7,3},{8,12},{9,13},{10,... | collective-permute-start | bytes 393224 | tf_op jit(solution)/shard_map/ppermute | solution.py:18
  84.9 12.4 %collective-permute-start.13 = (f32[128,256]{0,1:T(8,128)S(1)}, f32[128,256]{0,1:T(8,128)S(1)}, u32[]{:S(2)}, u32[]{:S(2)}) collective-permute-start(f32[128,256]{0,1:T(8,128)S(1)} %add.138), channel_id=1, source_target_pairs={{0,8},{1,9},{2,10},{3,11},{4,12},{5,13},{6,14},{7,15},{8,0},{9,1},... | collective-permute-start | bytes 393224 | tf_op jit(solution)/shard_map/ppermute | solution.py:18
  97.3 5.1 %collective-permute-start.14 = (f32[128,256]{0,1:T(8,128)S(1)}, f32[128,256]{0,1:T(8,128)S(1)}, u32[]{:S(2)}, u32[]{:S(2)}) collective-permute-start(f32[128,256]{0,1:T(8,128)S(1)} %add.139), channel_id=1, source_target_pairs={{0,16},{1,17},{2,18},{3,19},{4,20},{5,21},{6,22},{7,23},{8,24},{9,... | collective-permute-start | bytes 393224 | tf_op jit(solution)/shard_map/ppermute | solution.py:18

commit v2 on v1

--- a/solution.py
+++ b/solution.py
@@ -12,12 +12,11 @@
     return (col_coord, row_coord)
 
 
-def butterfly_sum(x, axis, n):
-    k = 1
-    while k < n:
-        x = x + lax.ppermute(x, axis, [(i, i ^ k) for i in range(n)])
-        k *= 2
-    return x
+def all_sum(x, axes, n):
+    chunks = x.reshape(n, -1)
+    mine = lax.all_to_all(chunks, axes, 0, 0, tiled=True).sum(axis=0)
+    spread = jnp.broadcast_to(mine[None], chunks.shape)
+    return lax.all_to_all(spread, axes, 0, 0, tiled=True).reshape(x.shape)
 
 
 def body(frame_one, frame_two, encoder_weight, flow_grad, n_blk, n_batch):
@@ -30,14 +29,9 @@
     scaling = channels ** (-0.5)
     blk = lax.axis_index("blk")
 
-    parts = [second_in] + [
-        lax.ppermute(second_in, "blk", [(i, (i + k) % n_blk) for i in range(n_blk)])
-        for k in range(1, n_blk)
-    ]
-    key_in = jnp.concatenate(parts, axis=0)
-    source = (blk - jnp.arange(n_blk, dtype=jnp.int32)) % n_blk
-    key_pos = (source[:, None] * query_count + jnp.arange(query_count, dtype=jnp.int32)[None, :]).reshape(-1)
-    key_col, key_row = coords_of(key_pos)
+    spread = jnp.broadcast_to(second_in[None], (n_blk,) + second_in.shape)
+    key_in = lax.all_to_all(spread, "blk", 0, 0, tiled=True).reshape(-1, second_in.shape[1])
+    key_col, key_row = coords_of(jnp.arange(key_in.shape[0], dtype=jnp.int32))
     own_col, own_row = coords_of(blk * query_count + jnp.arange(query_count, dtype=jnp.int32))
 
     first_feat = jnp.dot(first_in, encoder_weight, preferred_element_type=jnp.float32).astype(jnp.bfloat16)
@@ -56,16 +50,16 @@
     slope = (
         probs * (grad_col[:, None] * key_col[None, :] + grad_row[:, None] * key_row[None, :] - inner[:, None])
     ).astype(jnp.bfloat16)
-    delta_one = (scaling * jnp.dot(slope, key_feat, preferred_element_type=jnp.float32)).astype(jnp.bfloat16)
-    key_term = scaling * jnp.dot(slope.T, first_feat, preferred_element_type=jnp.float32)
+    both = jnp.dot(slope, jnp.concatenate([key_feat, key_in], axis=1), preferred_element_type=jnp.float32)
+    delta_one = (scaling * both[:, :channels]).astype(jnp.bfloat16)
     local_grad = jnp.dot(first_in.T, delta_one, preferred_element_type=jnp.float32)
-    local_grad = local_grad + jnp.dot(
-        key_in.astype(jnp.float32).T,
-        key_term,
+    local_grad = local_grad + scaling * jnp.dot(
+        both[:, channels:].T,
+        first_feat.astype(jnp.float32),
         precision=lax.Precision.HIGHEST,
         preferred_element_type=jnp.float32,
     )
-    grad_w = butterfly_sum(butterfly_sum(local_grad, "blk", n_blk), "batch", n_batch)
+    grad_w = all_sum(local_grad, ("blk", "batch"), n_blk * n_batch)
     return (flow, grad_w)
 
 

time: 103 us -> 85.5 us (0.83)
  the two profiles are of different devices: /device:TPU:2 before, /device:TPU:1 now
where the time goes in v2:
time: 85.5 us; the launch traced here: 85.1 us
  waiting for transfers between devices  39 us (46%)
  starting transfers between devices  25.9 us (30%)
  matrix products  7.37 us (9%)
  other arithmetic  6.45 us (8%)
  local copies, waits for them, and re-layouts  5.68 us (7%)
    all_to_all x1, waiting for transfers between devices, body(): lax.all_to_all(spread, 'blk', 0, 0, tiled=True)  13.8 us
    all_to_all x1, waiting for transfers between devices, all_sum(): mine = lax.all_to_all(chunks, axes, 0, 0, tiled=True).sum(axis=0)  12.8 us
    all_to_all x1, starting transfers between devices, all_sum(): mine = lax.all_to_all(chunks, axes, 0, 0, tiled=True).sum(axis=0)  12.6 us
    all_to_all x1, waiting for transfers between devices, all_sum(): return lax.all_to_all(spread, axes, 0, 0, tiled=True).reshape(x.shape)  12.4 us
    all_to_all x1, starting transfers between devices, body(): lax.all_to_all(spread, 'blk', 0, 0, tiled=True)  7.47 us
    all_to_all x1, starting transfers between devices, all_sum(): return lax.all_to_all(spread, axes, 0, 0, tiled=True).reshape(x.shape)  5.84 us
    reduce_sum x1, other arithmetic, body(): mean_col = jnp.sum(probs * key_col[None, :], axis=1)  3.05 us
    dot_general x1, matrix products, body(): jnp.dot(slope, jnp.concatenate([key_feat, key_in], axis=1), preferred_ele...  2.67 us
  transfers between devices with their start and end apart: 3, of which 3 were waited for; matrix products, arithmetic and copies ran while one was open for 3% of the time, Pallas kernels for 0%

profile of v2, /device:TPU:1, one launch (start us, length us, event | category | flops | bytes accessed | tf_op | source)
XLA Modules:
  0.0 85.1 jit_solution(11131981423684475440)
XLA Ops:
  0.6 1.0 %copy.11 = bf16[512,128]{0,1:T(8,128)(2,1)S(1)} copy(bf16[512,128]{1,0:T(8,128)(2,1)} %bitcast.26) | data formatting | bytes 262144 | tf_op jit(solution)/shard_map/broadcast_in_dim | solution.py:32
  1.7 1.1 %broadcast_in_dim.9 = bf16[8,512,128]{1,2,0:T(8,128)(2,1)} broadcast(bf16[512,128]{0,1:T(8,128)(2,1)S(1)} %copy.11), dimensions={1,2} | broadcast | bytes 1179648 | tf_op jit(solution)/shard_map/broadcast_in_dim | solution.py:32
  2.8 7.5 %all-to-all-start = ((bf16[8,512,128]{1,2,0:T(8,128)(2,1)}), bf16[8,512,128]{1,2,0:T(8,128)(2,1)S(1)}, u32[]{:S(2)}, u32[]{:S(2)}) async-start(bf16[8,512,128]{1,2,0:T(8,128)(2,1)} %broadcast_in_dim.9), calls=%async_computation | async-start | bytes 2097152 | tf_op jit(solution)/shard_map/all_to_all | solution.py:33
  10.3 0.8 fusion.29
  11.0 1.0 %convolution_convert_fusion.1 = bf16[512,256]{1,0:T(8,128)(2,1)S(1)} fusion(bf16[128,256]{1,0:T(8,128)(2,1)} %param.6, bf16[1,512,128]{2,1,0:T(8,128)(2,1)S(1)} %copy-done), kind=kOutput, calls=%fused_computation.12 | convolution fusion | flops 33685504 | bytes 458752 | tf_op jit(solution)/shard_map/dot_general | solution.py:37
  12.1 13.8 %all-to-all-done = bf16[8,512,128]{1,2,0:T(8,128)(2,1)S(1)} async-done(((bf16[8,512,128]{1,2,0:T(8,128)(2,1)}), bf16[8,512,128]{1,2,0:T(8,128)(2,1)S(1)}, u32[]{:S(2)}, u32[]{:S(2)}) %all-to-all-start) | async-done | bytes 1048608 | tf_op jit(solution)/shard_map/all_to_all | solution.py:33
  26.0 1.6 %convolution_convert_fusion = bf16[4096,256]{0,1:T(8,128)(2,1)S(1)} fusion(bf16[4096,128]{0,1:T(8,128)(2,1)S(1)} %bitcast.23, bf16[128,256]{1,0:T(8,128)(2,1)} %param.6), kind=kOutput, calls=%fused_computation.7 | convolution fusion | flops 269484032 | bytes 3211264 | tf_op jit(solution)/shard_map/dot_general | solution.py:38
  27.5 1.4 %multiply_reduce_fusion.2 = (f32[512]{0:T(512)S(1)}, f32[512,4096]{1,0:T(8,128)S(1)}) fusion(bf16[512,256]{1,0:T(8,128)(2,1)S(1)} %convolution_convert_fusion.1, bf16[4096,256]{0,1:T(8,128)(2,1)S(1)} %convolution_convert_fusion), kind=kOutput, calls=%fused_computation.4 | convolution fusion | flops 1077935616 | bytes 10749952 | tf_op jit(solution)/shard_map/dot_general | solution.py:40
  28.9 1.5 %fusion.1 = f32[512]{0:T(512)S(1)} fusion(f32[512,4096]{1,0:T(8,128)S(1)} %get-tuple-element.8, f32[512]{0:T(512)S(1)} %get-tuple-element.7), kind=kLoop, calls=%fused_computation.6 | loop fusion | flops 6290944 | bytes 8392704 | tf_op jit(solution)/shard_map/reduce_sum | solution.py:43
  30.4 3.0 %multiply_reduce_fusion.1 = (f32[512]{0:T(512)S(1)}, f32[512]{0:T(512)S(1)}, f32[512,4096]{1,0:T(8,128)S(1)}) fusion(f32[4096]{0:T(1024)S(1)} %get-tuple-element.10, f32[4096]{0:T(1024)S(1)} %get-tuple-element.9, f32[512]{0:T(512)S(1)} %fusion.1, f32[512]{0:T(512)S(1)} %get-tuple-element.7, f32[512,4096]{1,0:T(8,128)S(1)} %get-tuple-element.8), kind=kLoop, calls=%fused_computation.2 | loop fusion | flops 14679040 | bytes 16818176 | tf_op jit(solution)/shard_map/reduce_sum | solution.py:45
  33.5 2.7 %fusion.2 = f32[512,384]{1,0:T(8,128)S(1)} fusion(f32[512,4096]{1,0:T(8,128)S(1)} %get-tuple-element.4, f32[512]{0:T(512)S(1)} %multiply_add_fusion, f32[512]{0:T(512)S(1)} %bitcast.32, f32[512]{0:T(512)S(1)} %bitcast.30, f32[4096]{0:T(1024)S(1)} %get-tuple-element.9, f32[4096]{0:T(1024)S(1)} %get-tuple-element.10, bf16[4096,128]{0,1:T(8,128)(2,1)S(1)} %bitcast.24, ...), kind=kOutput, calls=%fused_computation.8 | convolution fusion | flops 1629487104 | bytes 12359680 | tf_op jit(solution)/shard_map/dot_general | solution.py:53
  36.2 0.3 convolution_bitcast_fusion
  36.4 0.4 fusion.6
  37.0 0.7 all_to_all.14
  37.6 12.6 %all-to-all-start.1 = ((f32[256,1,128]{2,1,0:T(1,128)}), f32[256,1,128]{2,1,0:T(1,128)S(1)}, u32[]{:S(2)}, u32[]{:S(2)}) async-start(f32[256,1,128]{2,1,0:T(1,128)} %bitcast.8), calls=%async_computation.1 | async-start | bytes 262144 | tf_op jit(solution)/shard_map/all_to_all | solution.py:17
  50.2 12.8 %all-to-all-done.1 = f32[256,1,128]{2,1,0:T(1,128)S(1)} async-done(((f32[256,1,128]{2,1,0:T(1,128)}), f32[256,1,128]{2,1,0:T(1,128)S(1)}, u32[]{:S(2)}, u32[]{:S(2)}) %all-to-all-start.1) | async-done | bytes 131104 | tf_op jit(solution)/shard_map/all_to_all | solution.py:17
  63.1 0.3 reduce_sum.45
  63.4 0.7 broadcast_in_dim.11
  64.1 5.8 %all-to-all-start.2 = ((f32[256,1,128]{2,1,0:T(1,128)}), f32[256,1,128]{2,1,0:T(1,128)S(1)}, u32[]{:S(2)}, u32[]{:S(2)}) async-start(f32[256,1,128]{2,1,0:T(1,128)} %broadcast_in_dim.11), calls=%async_computation.2 | async-start | bytes 262144 | tf_op jit(solution)/shard_map/all_to_all | solution.py:19
  70.0 0.6 maximum_bitcast_fusion
  70.6 12.4 %all-to-all-done.2 = f32[256,1,128]{2,1,0:T(1,128)S(1)} async-done(((f32[256,1,128]{2,1,0:T(1,128)}), f32[256,1,128]{2,1,0:T(1,128)S(1)}, u32[]{:S(2)}, u32[]{:S(2)}) %all-to-all-start.2) | async-done | bytes 131104 | tf_op jit(solution)/shard_map/all_to_all | solution.py:19
  82.9 0.5 broadcast.142
  83.4 0.9 %reduce.4 = f32[256,128]{1,0:T(8,128)S(1)} reduce(f32[256,1,128]{2,1,0:T(1,128)S(1)} %all-to-all-done.2, f32[]{:T(128)} %broadcast.142), dimensions={1}, to_apply=%all_to_all.16.reduce_sub_computation.3 | reduce | bytes 262148 | tf_op jit(solution)/shard_map/all_to_all | solution.py:19
  84.4 0.7 reshape.135
  (8 shorter events, 0.3 us)
Async XLA Ops:
  0.6 10.4 %copy-start = (bf16[1,512,128]{2,1,0:T(8,128)(2,1)S(1)}, bf16[1,512,128]{2,1,0:T(8,128)(2,1)}, u32[]{:S(2)}) copy-start(bf16[1,512,128]{2,1,0:T(8,128)(2,1)} %param.4) | copy-start | bytes 393220
  2.8 23.1 %all-to-all-start = ((bf16[8,512,128]{1,2,0:T(8,128)(2,1)}), bf16[8,512,128]{1,2,0:T(8,128)(2,1)S(1)}, u32[]{:S(2)}, u32[]{:S(2)}) async-start(bf16[8,512,128]{1,2,0:T(8,128)(2,1)} %broadcast_in_dim.9), calls=%async_computation | async-start | bytes 2097152 | tf_op jit(solution)/shard_map/all_to_all | solution.py:33
  37.6 25.4 %all-to-all-start.1 = ((f32[256,1,128]{2,1,0:T(1,128)}), f32[256,1,128]{2,1,0:T(1,128)S(1)}, u32[]{:S(2)}, u32[]{:S(2)}) async-start(f32[256,1,128]{2,1,0:T(1,128)} %bitcast.8), calls=%async_computation.1 | async-start | bytes 262144 | tf_op jit(solution)/shard_map/all_to_all | solution.py:17
  64.1 18.8 %all-to-all-start.2 = ((f32[256,1,128]{2,1,0:T(1,128)}), f32[256,1,128]{2,1,0:T(1,128)S(1)}, u32[]{:S(2)}, u32[]{:S(2)}) async-start(f32[256,1,128]{2,1,0:T(1,128)} %broadcast_in_dim.11), calls=%async_computation.2 | async-start | bytes 262144 | tf_op jit(solution)/shard_map/all_to_all | solution.py:19

commit v3 on v2

--- a/solution.py
+++ b/solution.py
@@ -1,7 +1,7 @@
 import jax
 import jax.numpy as jnp
 from jax import lax
-from jax.sharding import PartitionSpec as P
+from jax.sharding import Mesh, PartitionSpec as P
 
 WIDTH = 240
 
@@ -59,18 +59,21 @@
         precision=lax.Precision.HIGHEST,
         preferred_element_type=jnp.float32,
     )
-    grad_w = all_sum(local_grad, ("blk", "batch"), n_blk * n_batch)
+    local_grad = local_grad + lax.ppermute(local_grad, "core", [(0, 1), (1, 0)])
+    grad_w = all_sum(local_grad, ("blk", "chip"), n_blk * n_batch // 2)
     return (flow, grad_w)
 
 
 def solution(mesh):
-    placed = (P("batch", "blk", None), P("batch", "blk", None), P(), P("batch", None, "blk"))
     n_blk = mesh.shape["blk"]
     n_batch = mesh.shape["batch"]
+    mesh = Mesh(mesh.devices.reshape(n_blk, n_batch // 2, 2), ("blk", "chip", "core"))
+    batch = ("chip", "core")
+    placed = (P(batch, "blk", None), P(batch, "blk", None), P(), P(batch, None, "blk"))
 
     def step(frame_one, frame_two, encoder_weight, flow_grad):
         return body(frame_one, frame_two, encoder_weight, flow_grad, n_blk, n_batch)
 
     return jax.shard_map(
-        step, mesh=mesh, in_specs=placed, out_specs=(P("batch", None, "blk"), P()), check_vma=False
+        step, mesh=mesh, in_specs=placed, out_specs=(P(batch, None, "blk"), P()), check_vma=False
     )

time: 85.5 us -> 83.8 us (0.980)
  waiting for transfers between devices: 39 us -> 37 us
  starting transfers between devices: 25.9 us -> 27.8 us
  other arithmetic: 6.45 us -> 5.39 us
    all_to_all x1, waiting for transfers between devices: 12.4 us -> 10.8 us  [all_sum(): return lax.all_to_all(spread, axes, 0, 0, tiled=True).reshape(x.shape)]
    all_to_all x1, waiting for transfers between devices: 12.8 us -> 11.4 us  [all_sum(): mine = lax.all_to_all(chunks, axes, 0, 0, tiled=True).sum(axis=0)]
    ppermute x0 -> x1, starting transfers between devices: none -> 1.35 us  [body(): local_grad = local_grad + lax.ppermute(local_grad, 'core', [(0, 1), (1, 0)])]
    ppermute x0 -> x1, waiting for transfers between devices: none -> 0.99 us  [body(): local_grad = local_grad + lax.ppermute(local_grad, 'core', [(0, 1), (1, 0)])]
    all_to_all x1, other arithmetic: 0.95 us -> 0.02 us  [all_sum(): mine = lax.all_to_all(chunks, axes, 0, 0, tiled=True).sum(axis=0)]
  transfers between devices with their start and end apart: 3 -> 4, of which waited for: 3 -> 4; matrix products, arithmetic and copies ran while one was open for 3% -> 3% of each run, Pallas kernels for 0% -> 0%
where the time goes in v3:
time: 83.8 us; the launch traced here: 83.4 us
  waiting for transfers between devices  37 us (44%)
  starting transfers between devices  27.8 us (33%)
  matrix products  7.37 us (9%)
  other arithmetic  5.39 us (6%)
  local copies, waits for them, and re-layouts  5.14 us (6%)
    all_to_all x1, waiting for transfers between devices, body(): lax.all_to_all(spread, 'blk', 0, 0, tiled=True)  13.8 us
    all_to_all x1, starting transfers between devices, all_sum(): mine = lax.all_to_all(chunks, axes, 0, 0, tiled=True).sum(axis=0)  12.6 us
    all_to_all x1, waiting for transfers between devices, all_sum(): mine = lax.all_to_all(chunks, axes, 0, 0, tiled=True).sum(axis=0)  11.4 us
    all_to_all x1, waiting for transfers between devices, all_sum(): return lax.all_to_all(spread, axes, 0, 0, tiled=True).reshape(x.shape)  10.8 us
    all_to_all x1, starting transfers between devices, body(): lax.all_to_all(spread, 'blk', 0, 0, tiled=True)  7.47 us
    all_to_all x1, starting transfers between devices, all_sum(): return lax.all_to_all(spread, axes, 0, 0, tiled=True).reshape(x.shape)  6.34 us
    reduce_sum x1, other arithmetic, body(): mean_col = jnp.sum(probs * key_col[None, :], axis=1)  3.05 us
    dot_general x1, matrix products, body(): jnp.dot(slope, jnp.concatenate([key_feat, key_in], axis=1), preferred_ele...  2.67 us
  transfers between devices with their start and end apart: 4, of which 4 were waited for; matrix products, arithmetic and copies ran while one was open for 3% of the time, Pallas kernels for 0%

profile of v3, /device:TPU:1, one launch (start us, length us, event | category | flops | bytes accessed | tf_op | source)
XLA Modules:
  0.0 83.4 jit_solution(9346966016288332757)
XLA Ops:
  0.6 1.0 %copy.8 = bf16[512,128]{0,1:T(8,128)(2,1)S(1)} copy(bf16[512,128]{1,0:T(8,128)(2,1)} %bitcast.30) | data formatting | bytes 262144 | tf_op jit(solution)/shard_map/broadcast_in_dim | solution.py:32
  1.7 1.1 %broadcast_in_dim.9 = bf16[8,512,128]{1,2,0:T(8,128)(2,1)} broadcast(bf16[512,128]{0,1:T(8,128)(2,1)S(1)} %copy.8), dimensions={1,2} | broadcast | bytes 1179648 | tf_op jit(solution)/shard_map/broadcast_in_dim | solution.py:32
  2.8 7.5 %all-to-all-start = ((bf16[8,512,128]{1,2,0:T(8,128)(2,1)}), bf16[8,512,128]{1,2,0:T(8,128)(2,1)S(1)}, u32[]{:S(2)}, u32[]{:S(2)}) async-start(bf16[8,512,128]{1,2,0:T(8,128)(2,1)} %broadcast_in_dim.9), calls=%async_computation | async-start | bytes 2097152 | tf_op jit(solution)/shard_map/all_to_all | solution.py:33
  10.3 0.8 fusion.29
  11.0 1.0 %convolution_convert_fusion.1 = bf16[512,256]{1,0:T(8,128)(2,1)S(1)} fusion(bf16[128,256]{1,0:T(8,128)(2,1)} %param.6, bf16[1,512,128]{2,1,0:T(8,128)(2,1)S(1)} %copy-done), kind=kOutput, calls=%fused_computation.12 | convolution fusion | flops 33685504 | bytes 458752 | tf_op jit(solution)/shard_map/dot_general | solution.py:37
  12.1 13.8 %all-to-all-done = bf16[8,512,128]{1,2,0:T(8,128)(2,1)S(1)} async-done(((bf16[8,512,128]{1,2,0:T(8,128)(2,1)}), bf16[8,512,128]{1,2,0:T(8,128)(2,1)S(1)}, u32[]{:S(2)}, u32[]{:S(2)}) %all-to-all-start) | async-done | bytes 1048608 | tf_op jit(solution)/shard_map/all_to_all | solution.py:33
  26.0 1.6 %convolution_convert_fusion = bf16[4096,256]{0,1:T(8,128)(2,1)S(1)} fusion(bf16[4096,128]{0,1:T(8,128)(2,1)S(1)} %bitcast.27, bf16[128,256]{1,0:T(8,128)(2,1)} %param.6), kind=kOutput, calls=%fused_computation.7 | convolution fusion | flops 269484032 | bytes 3211264 | tf_op jit(solution)/shard_map/dot_general | solution.py:38
  27.5 1.4 %multiply_reduce_fusion.2 = (f32[512]{0:T(512)S(1)}, f32[512,4096]{1,0:T(8,128)S(1)}) fusion(bf16[512,256]{1,0:T(8,128)(2,1)S(1)} %convolution_convert_fusion.1, bf16[4096,256]{0,1:T(8,128)(2,1)S(1)} %convolution_convert_fusion), kind=kOutput, calls=%fused_computation.4 | convolution fusion | flops 1077935616 | bytes 10749952 | tf_op jit(solution)/shard_map/dot_general | solution.py:40
  28.9 1.5 %fusion.1 = f32[512]{0:T(512)S(1)} fusion(f32[512,4096]{1,0:T(8,128)S(1)} %get-tuple-element.8, f32[512]{0:T(512)S(1)} %get-tuple-element.7), kind=kLoop, calls=%fused_computation.6 | loop fusion | flops 6290944 | bytes 8392704 | tf_op jit(solution)/shard_map/reduce_sum | solution.py:43
  30.4 3.0 %multiply_reduce_fusion.1 = (f32[512]{0:T(512)S(1)}, f32[512]{0:T(512)S(1)}, f32[512,4096]{1,0:T(8,128)S(1)}) fusion(f32[4096]{0:T(1024)S(1)} %get-tuple-element.10, f32[4096]{0:T(1024)S(1)} %get-tuple-element.9, f32[512]{0:T(512)S(1)} %fusion.1, f32[512]{0:T(512)S(1)} %get-tuple-element.7, f32[512,4096]{1,0:T(8,128)S(1)} %get-tuple-element.8), kind=kLoop, calls=%fused_computation.2 | loop fusion | flops 14679040 | bytes 16818176 | tf_op jit(solution)/shard_map/reduce_sum | solution.py:45
  33.5 2.7 %fusion.2 = f32[512,384]{1,0:T(8,128)S(1)} fusion(f32[512,4096]{1,0:T(8,128)S(1)} %get-tuple-element.4, f32[512]{0:T(512)S(1)} %multiply_add_fusion, f32[512]{0:T(512)S(1)} %bitcast.37, f32[512]{0:T(512)S(1)} %bitcast.35, f32[4096]{0:T(1024)S(1)} %get-tuple-element.9, f32[4096]{0:T(1024)S(1)} %get-tuple-element.10, bf16[4096,128]{0,1:T(8,128)(2,1)S(1)} %bitcast.28, ...), kind=kOutput, calls=%fused_computation.8 | convolution fusion | flops 1629487104 | bytes 12359680 | tf_op jit(solution)/shard_map/dot_general | solution.py:53
  36.2 0.3 convolution_bitcast_fusion
  36.4 0.4 fusion.6
  36.9 1.3 %collective-permute-start = (f32[128,256]{0,1:T(8,128)S(1)}, f32[128,256]{0,1:T(8,128)S(1)}, u32[]{:S(2)}, u32[]{:S(2)}) collective-permute-start(f32[128,256]{0,1:T(8,128)S(1)} %fusion.6), channel_id=1, source_target_pairs={{0,1},{1,0},{2,3},{3,2},{4,5},{5,4},{6,7},{7,6},{8,9},{9,8},{10,11... | collective-permute-start | bytes 393224 | tf_op jit(solution)/shard_map/ppermute | solution.py:62
  38.2 1.0 %collective-permute-done = f32[128,256]{0,1:T(8,128)S(1)} collective-permute-done((f32[128,256]{0,1:T(8,128)S(1)}, f32[128,256]{0,1:T(8,128)S(1)}, u32[]{:S(2)}, u32[]{:S(2)}) %collective-permute-start) | collective-permute-done | bytes 131104 | tf_op jit(solution)/shard_map/ppermute | solution.py:62
  39.2 0.8 copy.11
  40.0 12.6 %all-to-all-start.1 = ((f32[128,1,256]{2,1,0:T(1,128)}), f32[128,1,256]{2,1,0:T(1,128)S(1)}, u32[]{:S(2)}, u32[]{:S(2)}) async-start(f32[128,1,256]{2,1,0:T(1,128)} %copy.11), calls=%async_computation.1 | async-start | bytes 262144 | tf_op jit(solution)/shard_map/all_to_all | solution.py:17
  52.7 11.4 %all-to-all-done.1 = f32[128,1,256]{2,1,0:T(1,128)S(1)} async-done(((f32[128,1,256]{2,1,0:T(1,128)}), f32[128,1,256]{2,1,0:T(1,128)S(1)}, u32[]{:S(2)}, u32[]{:S(2)}) %all-to-all-start.1) | async-done | bytes 131104 | tf_op jit(solution)/shard_map/all_to_all | solution.py:17
  64.1 0.2 reduce_sum.45
  64.3 0.7 broadcast_in_dim.11
  65.0 6.3 %all-to-all-start.2 = ((f32[128,1,256]{2,1,0:T(1,128)}), f32[128,1,256]{2,1,0:T(1,128)S(1)}, u32[]{:S(2)}, u32[]{:S(2)}) async-start(f32[128,1,256]{2,1,0:T(1,128)} %broadcast_in_dim.11), calls=%async_computation.2 | async-start | bytes 262144 | tf_op jit(solution)/shard_map/all_to_all | solution.py:19
  71.4 0.6 maximum_bitcast_fusion
  72.0 10.8 %all-to-all-done.2 = f32[128,1,256]{2,1,0:T(1,128)S(1)} async-done(((f32[128,1,256]{2,1,0:T(1,128)}), f32[128,1,256]{2,1,0:T(1,128)S(1)}, u32[]{:S(2)}, u32[]{:S(2)}) %all-to-all-start.2) | async-done | bytes 131104 | tf_op jit(solution)/shard_map/all_to_all | solution.py:19
  82.7 0.7 copy.16
  (8 shorter events, 0.2 us)
Async XLA Ops:
  0.6 10.4 %copy-start = (bf16[1,512,128]{2,1,0:T(8,128)(2,1)S(1)}, bf16[1,512,128]{2,1,0:T(8,128)(2,1)}, u32[]{:S(2)}) copy-start(bf16[1,512,128]{2,1,0:T(8,128)(2,1)} %param.4) | copy-start | bytes 393220
  2.8 23.1 %all-to-all-start = ((bf16[8,512,128]{1,2,0:T(8,128)(2,1)}), bf16[8,512,128]{1,2,0:T(8,128)(2,1)S(1)}, u32[]{:S(2)}, u32[]{:S(2)}) async-start(bf16[8,512,128]{1,2,0:T(8,128)(2,1)} %broadcast_in_dim.9), calls=%async_computation | async-start | bytes 2097152 | tf_op jit(solution)/shard_map/all_to_all | solution.py:33
  36.9 2.3 %collective-permute-start = (f32[128,256]{0,1:T(8,128)S(1)}, f32[128,256]{0,1:T(8,128)S(1)}, u32[]{:S(2)}, u32[]{:S(2)}) collective-permute-start(f32[128,256]{0,1:T(8,128)S(1)} %fusion.6), channel_id=1, source_target_pairs={{0,1},{1,0},{2,3},{3,2},{4,5},{5,4},{6,7},{7,6},{8,9},{9,8},{10,11... | collective-permute-start | bytes 393224 | tf_op jit(solution)/shard_map/ppermute | solution.py:62
  40.0 24.1 %all-to-all-start.1 = ((f32[128,1,256]{2,1,0:T(1,128)}), f32[128,1,256]{2,1,0:T(1,128)S(1)}, u32[]{:S(2)}, u32[]{:S(2)}) async-start(f32[128,1,256]{2,1,0:T(1,128)} %copy.11), calls=%async_computation.1 | async-start | bytes 262144 | tf_op jit(solution)/shard_map/all_to_all | solution.py:17
  65.0 17.8 %all-to-all-start.2 = ((f32[128,1,256]{2,1,0:T(1,128)}), f32[128,1,256]{2,1,0:T(1,128)S(1)}, u32[]{:S(2)}, u32[]{:S(2)}) async-start(f32[128,1,256]{2,1,0:T(1,128)} %broadcast_in_dim.11), calls=%async_computation.2 | async-start | bytes 262144 | tf_op jit(solution)/shard_map/all_to_all | solution.py:19

commit v4 on v3

--- a/solution.py
+++ b/solution.py
@@ -1,6 +1,10 @@
+import functools
+
 import jax
 import jax.numpy as jnp
 from jax import lax
+from jax.experimental import pallas as pl
+from jax.experimental.pallas import tpu as pltpu
 from jax.sharding import Mesh, PartitionSpec as P
 
 WIDTH = 240
@@ -17,6 +21,58 @@
     mine = lax.all_to_all(chunks, axes, 0, 0, tiled=True).sum(axis=0)
     spread = jnp.broadcast_to(mine[None], chunks.shape)
     return lax.all_to_all(spread, axes, 0, 0, tiled=True).reshape(x.shape)
+
+
+def corr_kernel(ff_ref, kcat_ref, coord_ref, grad_ref, mean_ref, d1_ref, g2_ref, *, scaling, channels):
+    ff = ff_ref[...]
+    keys = kcat_ref[...]
+    logits = scaling * lax.dot_general(
+        ff, keys[:, :channels], (((1,), (1,)), ((), ())), preferred_element_type=jnp.float32
+    )
+    top = jnp.max(logits, axis=1, keepdims=True)
+    expo = jnp.exp(logits - top)
+    total = jnp.sum(expo, axis=1, keepdims=True)
+    probs = expo / total
+    key_col = coord_ref[0:1, :]
+    key_row = coord_ref[1:2, :]
+    mean_col = jnp.sum(probs * key_col, axis=1, keepdims=True)
+    mean_row = jnp.sum(probs * key_row, axis=1, keepdims=True)
+    grad_col = grad_ref[:, 0:1]
+    grad_row = grad_ref[:, 1:2]
+    inner = grad_col * mean_col + grad_row * mean_row
+    slope = (probs * (grad_col * key_col + grad_row * key_row - inner)).astype(jnp.bfloat16)
+    both = jnp.dot(slope, keys, preferred_element_type=jnp.float32)
+    mean_ref[...] = jnp.concatenate([mean_col, mean_row], axis=1)
+    d1_ref[...] = (scaling * both[:, :channels]).astype(jnp.bfloat16)
+    g2_ref[...] = both[:, channels:]
+
+
+def corr_call(first_feat, key_cat, coords, grads, scaling, channels, tile=128):
+    rows = first_feat.shape[0]
+    keys, width = key_cat.shape
+    extra = width - channels
+    kernel = functools.partial(corr_kernel, scaling=scaling, channels=channels)
+    return pl.pallas_call(
+        kernel,
+        grid=(rows // tile,),
+        in_specs=[
+            pl.BlockSpec((tile, channels), lambda i: (i, 0)),
+            pl.BlockSpec((keys, width), lambda i: (0, 0)),
+            pl.BlockSpec(coords.shape, lambda i: (0, 0)),
+            pl.BlockSpec((tile, grads.shape[1]), lambda i: (i, 0)),
+        ],
+        out_specs=[
+            pl.BlockSpec((tile, 2), lambda i: (i, 0)),
+            pl.BlockSpec((tile, channels), lambda i: (i, 0)),
+            pl.BlockSpec((tile, extra), lambda i: (i, 0)),
+        ],
+        out_shape=[
+            jax.ShapeDtypeStruct((rows, 2), jnp.float32),
+            jax.ShapeDtypeStruct((rows, channels), jnp.bfloat16),
+            jax.ShapeDtypeStruct((rows, extra), jnp.float32),
+        ],
+        compiler_params=pltpu.CompilerParams(vmem_limit_bytes=48 * 1024 * 1024),
+    )(first_feat, key_cat, coords, grads)
 
 
 def body(frame_one, frame_two, encoder_weight, flow_grad, n_blk, n_batch):
@@ -37,24 +93,14 @@
     first_feat = jnp.dot(first_in, encoder_weight, preferred_element_type=jnp.float32).astype(jnp.bfloat16)
     key_feat = jnp.dot(key_in, encoder_weight, preferred_element_type=jnp.float32).astype(jnp.bfloat16)
 
-    logits = scaling * jnp.dot(first_feat, key_feat.T, preferred_element_type=jnp.float32)
-    top = jnp.max(logits, axis=1, keepdims=True)
-    expo = jnp.exp(logits - top)
-    total = jnp.sum(expo, axis=1, keepdims=True)
-    probs = expo / total
-    mean_col = jnp.sum(probs * key_col[None, :], axis=1)
-    mean_row = jnp.sum(probs * key_row[None, :], axis=1)
-    flow = jnp.stack([mean_col - own_col, mean_row - own_row])[None]
-
-    inner = grad_col * mean_col + grad_row * mean_row
-    slope = (
-        probs * (grad_col[:, None] * key_col[None, :] + grad_row[:, None] * key_row[None, :] - inner[:, None])
-    ).astype(jnp.bfloat16)
-    both = jnp.dot(slope, jnp.concatenate([key_feat, key_in], axis=1), preferred_element_type=jnp.float32)
-    delta_one = (scaling * both[:, :channels]).astype(jnp.bfloat16)
+    key_cat = jnp.concatenate([key_feat, key_in], axis=1)
+    coords = jnp.stack([key_col, key_row])
+    grads = jnp.stack([grad_col, grad_row], axis=1)
+    means, delta_one, slope_two = corr_call(first_feat, key_cat, coords, grads, scaling, channels)
+    flow = jnp.stack([means[:, 0] - own_col, means[:, 1] - own_row])[None]
     local_grad = jnp.dot(first_in.T, delta_one, preferred_element_type=jnp.float32)
     local_grad = local_grad + scaling * jnp.dot(
-        both[:, channels:].T,
+        slope_two.T,
         first_feat.astype(jnp.float32),
         precision=lax.Precision.HIGHEST,
         preferred_element_type=jnp.float32,

time: 83.8 us -> 84.3 us (level)
  Pallas kernels: 0 us -> 9.97 us
  matrix products: 7.37 us -> 1.58 us
  other arithmetic: 5.39 us -> 1.25 us
  waiting for transfers between devices: 37 us -> 38 us
    pallas_call x0 -> x1, Pallas kernels: none -> 9.97 us  [corr_call(): pl.pallas_call(kernel, grid=(rows // tile,), in_specs=[pl.BlockSpec((tile...]
    reduce_sum x2 -> x0, other arithmetic: 4.55 us -> none  [the longest x1 3.05 us: body(): mean_col = jnp.sum(probs * key_col[None, :], axis=1)]
    dot_general x3 -> x1, matrix products: 4.47 us -> 0.43 us  [body(): jnp.dot(slope_two.T, first_feat.astype(jnp.float32), precision=lax.Precis...]
    all_to_all x1, waiting for transfers between devices: 13.8 us -> 15.1 us  [body(): lax.all_to_all(spread, 'blk', 0, 0, tiled=True)]
    dot_general x1, matrix products: 1.59 us -> 0.68 us  [body(): jnp.dot(key_in, encoder_weight, preferred_element_type=jnp.float32)]
    broadcast_in_dim x2 -> x1, local copies, waits for them, and re-layouts: 2.12 us -> 2.07 us  [body(): spread = jnp.broadcast_to(second_in[None], (n_blk,) + second_in.shape)]
  transfers between devices with their start and end apart: 4 -> 4, of which waited for: 4 -> 4; matrix products, arithmetic and copies ran while one was open for 3% -> 2% of each run, Pallas kernels for 0% -> 0%
where the time goes in v4:
time: 84.3 us; the launch traced here: 84 us
  waiting for transfers between devices  38 us (45%)
  starting transfers between devices  27.8 us (33%)
  Pallas kernels  9.97 us (12%)
  local copies, waits for them, and re-layouts  4.69 us (6%)
  matrix products  1.58 us (2%)
  other arithmetic  1.25 us (1%)
    all_to_all x1, waiting for transfers between devices, body(): lax.all_to_all(spread, 'blk', 0, 0, tiled=True)  15.1 us
    all_to_all x1, starting transfers between devices, all_sum(): mine = lax.all_to_all(chunks, axes, 0, 0, tiled=True).sum(axis=0)  12.6 us
    all_to_all x1, waiting for transfers between devices, all_sum(): mine = lax.all_to_all(chunks, axes, 0, 0, tiled=True).sum(axis=0)  11.1 us
    all_to_all x1, waiting for transfers between devices, all_sum(): return lax.all_to_all(spread, axes, 0, 0, tiled=True).reshape(x.shape)  10.8 us
    pallas_call x1, Pallas kernels, corr_call(): pl.pallas_call(kernel, grid=(rows // tile,), in_specs=[pl.BlockSpec((tile...  9.97 us
    all_to_all x1, starting transfers between devices, body(): lax.all_to_all(spread, 'blk', 0, 0, tiled=True)  7.47 us
    all_to_all x1, starting transfers between devices, all_sum(): return lax.all_to_all(spread, axes, 0, 0, tiled=True).reshape(x.shape)  6.34 us
    broadcast_in_dim x1, local copies, waits for them, and re-layouts, body(): spread = jnp.broadcast_to(second_in[None], (n_blk,) + second_in.shape)  2.07 us
  transfers between devices with their start and end apart: 4, of which 4 were waited for; matrix products, arithmetic and copies ran while one was open for 2% of the time, Pallas kernels for 0%

profile of v4, /device:TPU:1, one launch (start us, length us, event | category | flops | bytes accessed | tf_op | source)
XLA Modules:
  0.0 84.0 jit_solution(14011726183168164069)
XLA Ops:
  0.6 0.0 copy-start
  0.7 2.1 %broadcast_in_dim.17 = bf16[8,512,128]{2,1,0:T(8,128)(2,1)} broadcast(bf16[512,128]{1,0:T(8,128)(2,1)} %bitcast.30), dimensions={1,2} | broadcast | bytes 1179648 | tf_op jit(solution)/shard_map/broadcast_in_dim | solution.py:88
  2.7 7.5 %all-to-all-start = ((bf16[8,512,128]{2,1,0:T(8,128)(2,1)}), bf16[8,512,128]{2,1,0:T(8,128)(2,1)S(1)}, u32[]{:S(2)}, u32[]{:S(2)}) async-start(bf16[8,512,128]{2,1,0:T(8,128)(2,1)} %broadcast_in_dim.17), calls=%async_computation | async-start | bytes 2097152 | tf_op jit(solution)/shard_map/all_to_all | solution.py:89
  10.2 0.2 convolution_convert_fusion.1.ff_ref
  10.5 0.1 copy.13.grad_ref
  10.6 0.1 fusion.4
  10.7 15.1 %all-to-all-done = bf16[8,512,128]{2,1,0:T(8,128)(2,1)S(1)} async-done(((bf16[8,512,128]{2,1,0:T(8,128)(2,1)}), bf16[8,512,128]{2,1,0:T(8,128)(2,1)S(1)}, u32[]{:S(2)}, u32[]{:S(2)}) %all-to-all-start) | async-done | bytes 1048608 | tf_op jit(solution)/shard_map/all_to_all | solution.py:89
  25.8 0.7 convolution_convert_fusion
  26.5 0.3 pad_maximum_fusion.kcat_ref
  26.8 10.0 %shard_map.59 = (f32[512,2]{1,0:T(8,128)S(1)}, bf16[512,256]{1,0:T(8,128)(2,1)S(1)}, f32[512,128]{1,0:T(8,128)S(1)}) custom-call(bf16[512,256]{1,0:T(8,128)(2,1)S(1)} %convolution_convert_fusion.1.ff_ref, bf16[4096,384]{1,0:T(8,128)(2,1)S(1)} %pad_maximum_fusion.kcat_ref, f32[2,4096]{1,0:T(2,128)S(1)} %pad_maximum_fusion.1.coord_ref, f32[512,2]{1,0:T(8,128)S(1)} %copy.13.grad_ref), custom_call_target="tpu_custom_call" | custom-call | tf_op jit(solution)/shard_map/pallas_call | solution.py:55
  36.8 0.3 convolution_bitcast_fusion
  37.1 0.4 fusion
  37.5 1.3 %collective-permute-start = (f32[128,256]{0,1:T(8,128)S(1)}, f32[128,256]{0,1:T(8,128)S(1)}, u32[]{:S(2)}, u32[]{:S(2)}) collective-permute-start(f32[128,256]{0,1:T(8,128)S(1)} %fusion), channel_id=1, source_target_pairs={{0,1},{1,0},{2,3},{3,2},{4,5},{5,4},{6,7},{7,6},{8,9},{9,8},{10,11... | collective-permute-start | bytes 393224 | tf_op jit(solution)/shard_map/ppermute | solution.py:108
  38.9 1.0 %collective-permute-done = f32[128,256]{0,1:T(8,128)S(1)} collective-permute-done((f32[128,256]{0,1:T(8,128)S(1)}, f32[128,256]{0,1:T(8,128)S(1)}, u32[]{:S(2)}, u32[]{:S(2)}) %collective-permute-start) | collective-permute-done | bytes 131104 | tf_op jit(solution)/shard_map/ppermute | solution.py:108
  39.9 0.8 copy.15
  40.6 12.6 %all-to-all-start.1 = ((f32[128,1,256]{2,1,0:T(1,128)}), f32[128,1,256]{2,1,0:T(1,128)S(1)}, u32[]{:S(2)}, u32[]{:S(2)}) async-start(f32[128,1,256]{2,1,0:T(1,128)} %copy.15), calls=%async_computation.1 | async-start | bytes 262144 | tf_op jit(solution)/shard_map/all_to_all | solution.py:21
  53.3 0.3 slice_reduce_fusion.1
  53.6 11.1 %all-to-all-done.1 = f32[128,1,256]{2,1,0:T(1,128)S(1)} async-done(((f32[128,1,256]{2,1,0:T(1,128)}), f32[128,1,256]{2,1,0:T(1,128)S(1)}, u32[]{:S(2)}, u32[]{:S(2)}) %all-to-all-start.1) | async-done | bytes 131104 | tf_op jit(solution)/shard_map/all_to_all | solution.py:21
  64.7 0.2 reduce_sum.9
  64.9 0.7 broadcast_in_dim.19
  65.6 6.3 %all-to-all-start.2 = ((f32[128,1,256]{2,1,0:T(1,128)}), f32[128,1,256]{2,1,0:T(1,128)S(1)}, u32[]{:S(2)}, u32[]{:S(2)}) async-start(f32[128,1,256]{2,1,0:T(1,128)} %broadcast_in_dim.19), calls=%async_computation.2 | async-start | bytes 262144 | tf_op jit(solution)/shard_map/all_to_all | solution.py:23
  72.0 0.6 maximum_bitcast_fusion
  72.6 10.8 %all-to-all-done.2 = f32[128,1,256]{2,1,0:T(1,128)S(1)} async-done(((f32[128,1,256]{2,1,0:T(1,128)}), f32[128,1,256]{2,1,0:T(1,128)S(1)}, u32[]{:S(2)}, u32[]{:S(2)}) %all-to-all-start.2) | async-done | bytes 131104 | tf_op jit(solution)/shard_map/all_to_all | solution.py:23
  83.4 0.7 copy.20
  (11 shorter events, 0.1 us)
Async XLA Ops:
  0.6 9.6 %copy-start = (bf16[1,512,128]{2,1,0:T(8,128)(2,1)S(1)}, bf16[1,512,128]{2,1,0:T(8,128)(2,1)}, u32[]{:S(2)}) copy-start(bf16[1,512,128]{2,1,0:T(8,128)(2,1)} %param.4) | copy-start | bytes 393220
  0.6 9.6 %copy-start.2 = (f32[1,2,512]{2,1,0:T(2,128)S(1)}, f32[1,2,512]{2,1,0:T(2,128)}, u32[]{:S(2)}) copy-start(f32[1,2,512]{2,1,0:T(2,128)} %param.7) | copy-start | bytes 12292
  0.7 9.6 %copy-start.1 = (bf16[128,256]{1,0:T(8,128)(2,1)S(1)}, bf16[128,256]{1,0:T(8,128)(2,1)}, u32[]{:S(2)}) copy-start(bf16[128,256]{1,0:T(8,128)(2,1)} %param.6) | copy-start | bytes 196612
  2.7 23.1 %all-to-all-start = ((bf16[8,512,128]{2,1,0:T(8,128)(2,1)}), bf16[8,512,128]{2,1,0:T(8,128)(2,1)S(1)}, u32[]{:S(2)}, u32[]{:S(2)}) async-start(bf16[8,512,128]{2,1,0:T(8,128)(2,1)} %broadcast_in_dim.17), calls=%async_computation | async-start | bytes 2097152 | tf_op jit(solution)/shard_map/all_to_all | solution.py:89
  37.5 2.3 %collective-permute-start = (f32[128,256]{0,1:T(8,128)S(1)}, f32[128,256]{0,1:T(8,128)S(1)}, u32[]{:S(2)}, u32[]{:S(2)}) collective-permute-start(f32[128,256]{0,1:T(8,128)S(1)} %fusion), channel_id=1, source_target_pairs={{0,1},{1,0},{2,3},{3,2},{4,5},{5,4},{6,7},{7,6},{8,9},{9,8},{10,11... | collective-permute-start | bytes 393224 | tf_op jit(solution)/shard_map/ppermute | solution.py:108
  40.6 24.1 %all-to-all-start.1 = ((f32[128,1,256]{2,1,0:T(1,128)}), f32[128,1,256]{2,1,0:T(1,128)S(1)}, u32[]{:S(2)}, u32[]{:S(2)}) async-start(f32[128,1,256]{2,1,0:T(1,128)} %copy.15), calls=%async_computation.1 | async-start | bytes 262144 | tf_op jit(solution)/shard_map/all_to_all | solution.py:21
  65.6 17.8 %all-to-all-start.2 = ((f32[128,1,256]{2,1,0:T(1,128)}), f32[128,1,256]{2,1,0:T(1,128)S(1)}, u32[]{:S(2)}, u32[]{:S(2)}) async-start(f32[128,1,256]{2,1,0:T(1,128)} %broadcast_in_dim.19), calls=%async_computation.2 | async-start | bytes 262144 | tf_op jit(solution)/shard_map/all_to_all | solution.py:23

commit v5 on v4

--- a/solution.py
+++ b/solution.py
@@ -1,4 +1,5 @@
 import functools
+import math
 
 import jax
 import jax.numpy as jnp
@@ -24,23 +25,23 @@
 
 
 def corr_kernel(ff_ref, kcat_ref, coord_ref, grad_ref, mean_ref, d1_ref, g2_ref, *, scaling, channels):
-    ff = ff_ref[...]
     keys = kcat_ref[...]
-    logits = scaling * lax.dot_general(
-        ff, keys[:, :channels], (((1,), (1,)), ((), ())), preferred_element_type=jnp.float32
+    logits = lax.dot_general(
+        ff_ref[...], keys[:, :channels], (((1,), (1,)), ((), ())), preferred_element_type=jnp.float32
     )
     top = jnp.max(logits, axis=1, keepdims=True)
     expo = jnp.exp(logits - top)
-    total = jnp.sum(expo, axis=1, keepdims=True)
-    probs = expo / total
+    inv_total = 1.0 / jnp.sum(expo, axis=1, keepdims=True)
     key_col = coord_ref[0:1, :]
     key_row = coord_ref[1:2, :]
-    mean_col = jnp.sum(probs * key_col, axis=1, keepdims=True)
-    mean_row = jnp.sum(probs * key_row, axis=1, keepdims=True)
+    mean_col = jnp.sum(expo * key_col, axis=1, keepdims=True) * inv_total
+    mean_row = jnp.sum(expo * key_row, axis=1, keepdims=True) * inv_total
     grad_col = grad_ref[:, 0:1]
     grad_row = grad_ref[:, 1:2]
     inner = grad_col * mean_col + grad_row * mean_row
-    slope = (probs * (grad_col * key_col + grad_row * key_row - inner)).astype(jnp.bfloat16)
+    slope = (expo * ((grad_col * inv_total) * key_col + (grad_row * inv_total) * key_row - inner * inv_total)).astype(
+        jnp.bfloat16
+    )
     both = jnp.dot(slope, keys, preferred_element_type=jnp.float32)
     mean_ref[...] = jnp.concatenate([mean_col, mean_row], axis=1)
     d1_ref[...] = (scaling * both[:, :channels]).astype(jnp.bfloat16)
@@ -48,6 +49,7 @@
 
 
 def corr_call(first_feat, key_cat, coords, grads, scaling, channels, tile=128):
+    assert scaling == 2.0 ** round(math.log2(scaling))
     rows = first_feat.shape[0]
     keys, width = key_cat.shape
     extra = width - channels
@@ -72,7 +74,7 @@
             jax.ShapeDtypeStruct((rows, extra), jnp.float32),
         ],
         compiler_params=pltpu.CompilerParams(vmem_limit_bytes=48 * 1024 * 1024),
-    )(first_feat, key_cat, coords, grads)
+    )(first_feat * jnp.asarray(scaling, first_feat.dtype), key_cat, coords, grads)
 
 
 def body(frame_one, frame_two, encoder_weight, flow_grad, n_blk, n_batch):

time: 84.3 us -> 83.7 us (level)
  no operation moved by 1% of the time
where the time goes in v5:
time: 83.7 us; the launch traced here: 83.5 us
  waiting for transfers between devices  38 us (45%)
  starting transfers between devices  27.8 us (33%)
  Pallas kernels  9.38 us (11%)
  local copies, waits for them, and re-layouts  4.68 us (6%)
  matrix products  1.6 us (2%)
  other arithmetic  1.25 us (1%)
    all_to_all x1, waiting for transfers between devices, body(): lax.all_to_all(spread, 'blk', 0, 0, tiled=True)  15.1 us
    all_to_all x1, starting transfers between devices, all_sum(): mine = lax.all_to_all(chunks, axes, 0, 0, tiled=True).sum(axis=0)  12.6 us
    all_to_all x1, waiting for transfers between devices, all_sum(): mine = lax.all_to_all(chunks, axes, 0, 0, tiled=True).sum(axis=0)  11.1 us
    all_to_all x1, waiting for transfers between devices, all_sum(): return lax.all_to_all(spread, axes, 0, 0, tiled=True).reshape(x.shape)  10.8 us
    pallas_call x1, Pallas kernels, corr_call(): pl.pallas_call(kernel, grid=(rows // tile,), in_specs=[pl.BlockSpec((tile...  9.38 us
    all_to_all x1, starting transfers between devices, body(): lax.all_to_all(spread, 'blk', 0, 0, tiled=True)  7.47 us
    all_to_all x1, starting transfers between devices, all_sum(): return lax.all_to_all(spread, axes, 0, 0, tiled=True).reshape(x.shape)  6.34 us
    broadcast_in_dim x1, local copies, waits for them, and re-layouts, body(): spread = jnp.broadcast_to(second_in[None], (n_blk,) + second_in.shape)  2.07 us
  transfers between devices with their start and end apart: 4, of which 4 were waited for; matrix products, arithmetic and copies ran while one was open for 2% of the time, Pallas kernels for 0%

profile of v5, /device:TPU:1, one launch (start us, length us, event | category | flops | bytes accessed | tf_op | source)
XLA Modules:
  0.0 83.5 jit_solution(11296766809049247118)
XLA Ops:
  0.6 0.0 copy-start
  0.7 2.1 %broadcast_in_dim.17 = bf16[8,512,128]{2,1,0:T(8,128)(2,1)} broadcast(bf16[512,128]{1,0:T(8,128)(2,1)} %bitcast.32), dimensions={1,2} | broadcast | bytes 1179648 | tf_op jit(solution)/shard_map/broadcast_in_dim | solution.py:90
  2.7 7.5 %all-to-all-start = ((bf16[8,512,128]{2,1,0:T(8,128)(2,1)}), bf16[8,512,128]{2,1,0:T(8,128)(2,1)S(1)}, u32[]{:S(2)}, u32[]{:S(2)}) async-start(bf16[8,512,128]{2,1,0:T(8,128)(2,1)} %broadcast_in_dim.17), calls=%async_computation | async-start | bytes 2097152 | tf_op jit(solution)/shard_map/all_to_all | solution.py:91
  10.2 0.2 broadcast_multiply_fusion
  10.5 0.1 copy.13.grad_ref
  10.6 0.1 fusion.4
  10.7 15.1 %all-to-all-done = bf16[8,512,128]{2,1,0:T(8,128)(2,1)S(1)} async-done(((bf16[8,512,128]{2,1,0:T(8,128)(2,1)}), bf16[8,512,128]{2,1,0:T(8,128)(2,1)S(1)}, u32[]{:S(2)}, u32[]{:S(2)}) %all-to-all-start) | async-done | bytes 1048608 | tf_op jit(solution)/shard_map/all_to_all | solution.py:91
  25.8 0.7 convolution_convert_fusion
  26.5 0.3 pad_maximum_fusion.kcat_ref
  26.8 9.4 %shard_map.59 = (f32[512,2]{1,0:T(8,128)S(1)}, bf16[512,256]{1,0:T(8,128)(2,1)S(1)}, f32[512,128]{1,0:T(8,128)S(1)}) custom-call(bf16[512,256]{1,0:T(8,128)(2,1)S(1)} %get-tuple-element.12.ff_ref, bf16[4096,384]{1,0:T(8,128)(2,1)S(1)} %pad_maximum_fusion.kcat_ref, f32[2,4096]{1,0:T(2,128)S(1)} %pad_maximum_fusion.1.coord_ref, f32[512,2]{1,0:T(8,128)S(1)} %copy.13.grad_ref), custom_call_target="tpu_custom_call" | custom-call | tf_op jit(solution)/shard_map/pallas_call | solution.py:57
  36.2 0.3 convolution_bitcast_fusion
  36.5 0.4 fusion
  36.9 1.3 %collective-permute-start = (f32[128,256]{0,1:T(8,128)S(1)}, f32[128,256]{0,1:T(8,128)S(1)}, u32[]{:S(2)}, u32[]{:S(2)}) collective-permute-start(f32[128,256]{0,1:T(8,128)S(1)} %fusion), channel_id=1, source_target_pairs={{0,1},{1,0},{2,3},{3,2},{4,5},{5,4},{6,7},{7,6},{8,9},{9,8},{10,11... | collective-permute-start | bytes 393224 | tf_op jit(solution)/shard_map/ppermute | solution.py:110
  38.3 1.0 %collective-permute-done = f32[128,256]{0,1:T(8,128)S(1)} collective-permute-done((f32[128,256]{0,1:T(8,128)S(1)}, f32[128,256]{0,1:T(8,128)S(1)}, u32[]{:S(2)}, u32[]{:S(2)}) %collective-permute-start) | collective-permute-done | bytes 131104 | tf_op jit(solution)/shard_map/ppermute | solution.py:110
  39.3 0.8 copy.15
  40.0 12.6 %all-to-all-start.1 = ((f32[128,1,256]{2,1,0:T(1,128)}), f32[128,1,256]{2,1,0:T(1,128)S(1)}, u32[]{:S(2)}, u32[]{:S(2)}) async-start(f32[128,1,256]{2,1,0:T(1,128)} %copy.15), calls=%async_computation.1 | async-start | bytes 262144 | tf_op jit(solution)/shard_map/all_to_all | solution.py:22
  52.7 0.3 slice_reduce_fusion.1
  53.0 11.1 %all-to-all-done.1 = f32[128,1,256]{2,1,0:T(1,128)S(1)} async-done(((f32[128,1,256]{2,1,0:T(1,128)}), f32[128,1,256]{2,1,0:T(1,128)S(1)}, u32[]{:S(2)}, u32[]{:S(2)}) %all-to-all-start.1) | async-done | bytes 131104 | tf_op jit(solution)/shard_map/all_to_all | solution.py:22
  64.1 0.2 reduce_sum.9
  64.3 0.7 broadcast_in_dim.19
  65.0 6.3 %all-to-all-start.2 = ((f32[128,1,256]{2,1,0:T(1,128)}), f32[128,1,256]{2,1,0:T(1,128)S(1)}, u32[]{:S(2)}, u32[]{:S(2)}) async-start(f32[128,1,256]{2,1,0:T(1,128)} %broadcast_in_dim.19), calls=%async_computation.2 | async-start | bytes 262144 | tf_op jit(solution)/shard_map/all_to_all | solution.py:24
  71.4 0.6 maximum_bitcast_fusion
  72.0 10.8 %all-to-all-done.2 = f32[128,1,256]{2,1,0:T(1,128)S(1)} async-done(((f32[128,1,256]{2,1,0:T(1,128)}), f32[128,1,256]{2,1,0:T(1,128)S(1)}, u32[]{:S(2)}, u32[]{:S(2)}) %all-to-all-start.2) | async-done | bytes 131104 | tf_op jit(solution)/shard_map/all_to_all | solution.py:24
  82.8 0.7 copy.20
  (11 shorter events, 0.1 us)
Async XLA Ops:
  0.6 9.6 %copy-start = (bf16[1,512,128]{2,1,0:T(8,128)(2,1)S(1)}, bf16[1,512,128]{2,1,0:T(8,128)(2,1)}, u32[]{:S(2)}) copy-start(bf16[1,512,128]{2,1,0:T(8,128)(2,1)} %param.4) | copy-start | bytes 393220
  0.6 9.6 %copy-start.2 = (f32[1,2,512]{2,1,0:T(2,128)S(1)}, f32[1,2,512]{2,1,0:T(2,128)}, u32[]{:S(2)}) copy-start(f32[1,2,512]{2,1,0:T(2,128)} %param.7) | copy-start | bytes 12292
  0.7 9.6 %copy-start.1 = (bf16[128,256]{1,0:T(8,128)(2,1)S(1)}, bf16[128,256]{1,0:T(8,128)(2,1)}, u32[]{:S(2)}) copy-start(bf16[128,256]{1,0:T(8,128)(2,1)} %param.6) | copy-start | bytes 196612
  2.7 23.1 %all-to-all-start = ((bf16[8,512,128]{2,1,0:T(8,128)(2,1)}), bf16[8,512,128]{2,1,0:T(8,128)(2,1)S(1)}, u32[]{:S(2)}, u32[]{:S(2)}) async-start(bf16[8,512,128]{2,1,0:T(8,128)(2,1)} %broadcast_in_dim.17), calls=%async_computation | async-start | bytes 2097152 | tf_op jit(solution)/shard_map/all_to_all | solution.py:91
  36.9 2.3 %collective-permute-start = (f32[128,256]{0,1:T(8,128)S(1)}, f32[128,256]{0,1:T(8,128)S(1)}, u32[]{:S(2)}, u32[]{:S(2)}) collective-permute-start(f32[128,256]{0,1:T(8,128)S(1)} %fusion), channel_id=1, source_target_pairs={{0,1},{1,0},{2,3},{3,2},{4,5},{5,4},{6,7},{7,6},{8,9},{9,8},{10,11... | collective-permute-start | bytes 393224 | tf_op jit(solution)/shard_map/ppermute | solution.py:110
  40.0 24.1 %all-to-all-start.1 = ((f32[128,1,256]{2,1,0:T(1,128)}), f32[128,1,256]{2,1,0:T(1,128)S(1)}, u32[]{:S(2)}, u32[]{:S(2)}) async-start(f32[128,1,256]{2,1,0:T(1,128)} %copy.15), calls=%async_computation.1 | async-start | bytes 262144 | tf_op jit(solution)/shard_map/all_to_all | solution.py:22
  65.0 17.8 %all-to-all-start.2 = ((f32[128,1,256]{2,1,0:T(1,128)}), f32[128,1,256]{2,1,0:T(1,128)S(1)}, u32[]{:S(2)}, u32[]{:S(2)}) async-start(f32[128,1,256]{2,1,0:T(1,128)} %broadcast_in_dim.19), calls=%async_computation.2 | async-start | bytes 262144 | tf_op jit(solution)/shard_map/all_to_all | solution.py:24

commit v6 on v3

v6 whole, which is shorter than its diff:
```python
import functools
import math

import jax
import jax.numpy as jnp
from jax import lax
from jax.experimental import pallas as pl
from jax.experimental.pallas import tpu as pltpu
from jax.sharding import Mesh, PartitionSpec as P

WIDTH = 240


def coords_of(position):
    col_coord = (position % WIDTH).astype(jnp.float32) / 64.0
    row_coord = (position // WIDTH).astype(jnp.float32) / 8.0
    return (col_coord, row_coord)


def all_sum(x, axes, n):
    chunks = x.reshape(n, -1)
    mine = lax.all_to_all(chunks, axes, 0, 0, tiled=True).sum(axis=0)
    spread = jnp.broadcast_to(mine[None], chunks.shape)
    return lax.all_to_all(spread, axes, 0, 0, tiled=True).reshape(x.shape)


def stats_kernel(ff_ref, kcat_ref, coord_ref, stat_ref, *, channels):
    logits = lax.dot_general(
        ff_ref[...], kcat_ref[:, :channels], (((1,), (1,)), ((), ())), preferred_element_type=jnp.float32
    )
    top = jnp.max(logits, axis=1, keepdims=True)
    expo = jnp.exp(logits - top)
    total = jnp.sum(expo, axis=1, keepdims=True)
    sum_col = jnp.sum(expo * coord_ref[0:1, :], axis=1, keepdims=True)
    sum_row = jnp.sum(expo * coord_ref[1:2, :], axis=1, keepdims=True)
    stat_ref[...] = jnp.concatenate([top, total, sum_col, sum_row], axis=1)


def slope_kernel(ff_ref, kcat_ref, coord_ref, coef_ref, both_ref, *, channels):
    keys = kcat_ref[...]
    logits = lax.dot_general(
        ff_ref[...], keys[:, :channels], (((1,), (1,)), ((), ())), preferred_element_type=jnp.float32
    )
    top = coef_ref[:, 0:1]
    factor = coef_ref[:, 1:2] * coord_ref[0:1, :] + coef_ref[:, 2:3] * coord_ref[1:2, :] + coef_ref[:, 3:4]
    slope = (jnp.exp(logits - top) * factor).astype(jnp.bfloat16)
    both_ref[...] = jnp.dot(slope, keys, preferred_element_type=jnp.float32)


def row_call(kernel, ff, kcat, coords, rows_in, out_width, channels, tile=128):
    rows = ff.shape[0]
    keys, width = kcat.shape
    in_specs = [
        pl.BlockSpec((tile, ff.shape[1]), lambda i: (i, 0)),
        pl.BlockSpec((keys, width), lambda i: (0, 0)),
        pl.BlockSpec(coords.shape, lambda i: (0, 0)),
    ]
    operands = [ff, kcat, coords]
    if rows_in is not None:
        in_specs.append(pl.BlockSpec((tile, rows_in.shape[1]), lambda i: (i, 0)))
        operands.append(rows_in)
    return pl.pallas_call(
        functools.partial(kernel, channels=channels),
        grid=(rows // tile,),
        in_specs=in_specs,
        out_specs=pl.BlockSpec((tile, out_width), lambda i: (i, 0)),
        out_shape=jax.ShapeDtypeStruct((rows, out_width), jnp.float32),
        compiler_params=pltpu.CompilerParams(vmem_limit_bytes=48 * 1024 * 1024),
    )(*operands)


def body(frame_one, frame_two, encoder_weight, flow_grad, n_x, n_yh, n_group):
    own_in = frame_one[0]
    second_in = frame_two[0]
    own_grad = flow_grad[0]
    count = own_in.shape[0]
    channels = encoder_weight.shape[1]
    scaling = channels ** (-0.5)
    assert scaling == 2.0 ** round(math.log2(scaling))
    xi = lax.axis_index("x")
    hi = lax.axis_index("yh")
    swap = [(0, 1), (1, 0)]

    spread = jnp.broadcast_to(second_in[None], (n_x,) + second_in.shape)
    key_in = lax.all_to_all(spread, "x", 0, 0, tiled=True).reshape(-1, second_in.shape[1])
    key_blk = jnp.arange(n_x, dtype=jnp.int32) * n_yh + hi
    key_pos = (key_blk[:, None] * count + jnp.arange(count, dtype=jnp.int32)[None, :]).reshape(-1)
    key_col, key_row = coords_of(key_pos)
    coords = jnp.stack([key_col, key_row])

    other_in = lax.ppermute(own_in, "yh", swap)
    other_grad = lax.ppermute(own_grad, "yh", swap)
    query_in = jnp.concatenate([own_in, other_in], axis=0)
    query_grad = jnp.concatenate([own_grad, other_grad], axis=1)

    query_feat = jnp.dot(query_in, encoder_weight, preferred_element_type=jnp.float32).astype(jnp.bfloat16)
    key_feat = jnp.dot(key_in, encoder_weight, preferred_element_type=jnp.float32).astype(jnp.bfloat16)
    key_cat = jnp.concatenate([key_feat, key_in], axis=1)
    scaled_feat = query_feat * jnp.asarray(scaling, query_feat.dtype)

    part = row_call(stats_kernel, scaled_feat, key_cat, coords, None, 4, channels)
    recv = lax.ppermute(part, "yh", swap)
    other = jnp.concatenate([recv[count:], recv[:count]], axis=0)
    top = jnp.maximum(part[:, 0], other[:, 0])
    w_mine = jnp.exp(part[:, 0] - top)
    w_other = jnp.exp(other[:, 0] - top)
    total = part[:, 1] * w_mine + other[:, 1] * w_other
    inv_total = 1.0 / total
    mean_col = (part[:, 2] * w_mine + other[:, 2] * w_other) * inv_total
    mean_row = (part[:, 3] * w_mine + other[:, 3] * w_other) * inv_total

    own_col, own_row = coords_of((xi * n_yh + hi) * count + jnp.arange(count, dtype=jnp.int32))
    flow = jnp.stack([mean_col[:count] - own_col, mean_row[:count] - own_row])[None]

    grad_col = query_grad[0]
    grad_row = query_grad[1]
    inner = grad_col * mean_col + grad_row * mean_row
    coef = jnp.stack([top, grad_col * inv_total, grad_row * inv_total, -inner * inv_total], axis=1)
    both = row_call(slope_kernel, scaled_feat, key_cat, coords, coef, key_cat.shape[1], channels)
    delta_one = scaling * both[:, :channels]
    local_grad = jnp.dot(
        query_in.astype(jnp.float32).T, delta_one, precision=lax.Precision.HIGHEST, preferred_element_type=jnp.float32
    )
    local_grad = local_grad + scaling * jnp.dot(
        both[:, channels:].T,
        query_feat.astype(jnp.float32),
        precision=lax.Precision.HIGHEST,
        preferred_element_type=jnp.float32,
    )
    local_grad = local_grad + lax.ppermute(local_grad, "core", swap)
    grad_w = all_sum(local_grad, ("x", "yh", "chip"), n_group)
    return (flow, grad_w)


def solution(mesh):
    n_blk = mesh.shape["blk"]
    n_batch = mesh.shape["batch"]
    n_yh = 2
    n_x = n_blk // n_yh
    mesh = Mesh(mesh.devices.reshape(n_x, n_yh, n_batch // 2, 2), ("x", "yh", "chip", "core"))
    blk = ("x", "yh")
    batch = ("chip", "core")
    placed = (P(batch, blk, None), P(batch, blk, None), P(), P(batch, None, blk))

    def step(frame_one, frame_two, encoder_weight, flow_grad):
        return body(frame_one, frame_two, encoder_weight, flow_grad, n_x, n_yh, n_x * n_yh * n_batch // 2)

    return jax.shard_map(
        step, mesh=mesh, in_specs=placed, out_specs=(P(batch, None, blk), P()), check_vma=False
    )
```

time: 83.8 us -> 100 us (1.19)
  Pallas kernels: 0 us -> 13.3 us
  starting transfers between devices: 27.8 us -> 35.4 us
  matrix products: 7.37 us -> 2.66 us
  local copies, waits for them, and re-layouts: 5.14 us -> 6.35 us
  other arithmetic: 5.39 us -> 4.37 us
    pallas_call x0 -> x2, Pallas kernels: none -> 13.3 us  [row_call(): pl.pallas_call(functools.partial(kernel, channels=channels), grid=(rows /...]
    ppermute x1 -> x4, starting transfers between devices: 1.35 us -> 11.4 us  [the longest x1 3.82 us: body(): other_grad = lax.ppermute(own_grad, 'yh', swap)]
    all_to_all x1, waiting for transfers between devices: 13.8 us -> 5.58 us  [body(): lax.all_to_all(spread, 'x', 0, 0, tiled=True)]
    ppermute x1 -> x4, waiting for transfers between devices: 0.99 us -> 9.07 us  [the longest x1 8.07 us: body(): recv = lax.ppermute(part, 'yh', swap)]
    reduce_sum x2 -> x0, other arithmetic: 4.55 us -> none  [the longest x1 3.05 us: body(): mean_col = jnp.sum(probs * key_col[None, :], axis=1)]
    dot_general x5 -> x3, matrix products: 5.78 us -> 2.24 us  [the longest x1 1.07 us: body(): jnp.dot(query_in, encoder_weight, preferred_element_type=jnp.float32)]
    all_to_all x1, starting transfers between devices: 7.47 us -> 4.01 us  [body(): lax.all_to_all(spread, 'x', 0, 0, tiled=True)]
    mul x0 -> x4, other arithmetic: none -> 2.64 us  [the longest x1 1.44 us: body(): grad_row * inv_total]
  transfers between devices with their start and end apart: 4 -> 7, of which waited for: 4 -> 5; matrix products, arithmetic and copies ran while one was open for 3% -> 6% of each run, Pallas kernels for 0% -> 7%
where the time goes in v6:
time: 100 us; the launch traced here: 99.8 us
  waiting for transfers between devices  36.9 us (37%)
  starting transfers between devices  35.4 us (35%)
  Pallas kernels  13.3 us (13%)
  local copies, waits for them, and re-layouts  6.35 us (6%)
  other arithmetic  4.37 us (4%)
  matrix products  2.66 us (3%)
    all_to_all x1, starting transfers between devices, all_sum(): mine = lax.all_to_all(chunks, axes, 0, 0, tiled=True).sum(axis=0)  13.7 us
    pallas_call x2, Pallas kernels, row_call(): pl.pallas_call(functools.partial(kernel, channels=channels), grid=(rows /...  13.3 us
    all_to_all x1, waiting for transfers between devices, all_sum(): mine = lax.all_to_all(chunks, axes, 0, 0, tiled=True).sum(axis=0)  11.4 us
    all_to_all x1, waiting for transfers between devices, all_sum(): return lax.all_to_all(spread, axes, 0, 0, tiled=True).reshape(x.shape)  10.8 us
    ppermute x1, waiting for transfers between devices, body(): recv = lax.ppermute(part, 'yh', swap)  8.07 us
    all_to_all x1, starting transfers between devices, all_sum(): return lax.all_to_all(spread, axes, 0, 0, tiled=True).reshape(x.shape)  6.34 us
    all_to_all x1, waiting for transfers between devices, body(): lax.all_to_all(spread, 'x', 0, 0, tiled=True)  5.58 us
    all_to_all x1, starting transfers between devices, body(): lax.all_to_all(spread, 'x', 0, 0, tiled=True)  4.01 us
  transfers between devices with their start and end apart: 7, of which 5 were waited for; matrix products, arithmetic and copies ran while one was open for 6% of the time, Pallas kernels for 7%

profile of v6, /device:TPU:1, one launch (start us, length us, event | category | flops | bytes accessed | tf_op | source)
XLA Modules:
  0.0 99.8 jit_solution(10120188849691435905)
XLA Ops:
  0.7 3.8 %collective-permute-start.2 = (f32[2,512]{1,0:T(2,128)}, f32[2,512]{1,0:T(2,128)S(1)}, u32[]{:S(2)}, u32[]{:S(2)}) collective-permute-start(f32[2,512]{1,0:T(2,128)} %bitcast.45), channel_id=1, source_target_pairs={{0,32},{32,0},{1,33},{33,1},{2,34},{34,2},{3,35},{35,3},{4,36},{36... | collective-permute-start | bytes 12296 | tf_op jit(solution)/shard_map/ppermute | solution.py:92
  4.6 1.8 %broadcast_in_dim.9 = bf16[4,512,128]{2,1,0:T(8,128)(2,1)} broadcast(bf16[512,128]{1,0:T(8,128)(2,1)} %bitcast.38), dimensions={1,2} | broadcast | bytes 655360 | tf_op jit(solution)/shard_map/broadcast_in_dim | solution.py:84
  6.4 4.0 %all-to-all-start = ((bf16[4,512,128]{2,1,0:T(8,128)(2,1)}), bf16[4,512,128]{2,1,0:T(8,128)(2,1)S(1)}, u32[]{:S(2)}, u32[]{:S(2)}) async-start(bf16[4,512,128]{2,1,0:T(8,128)(2,1)} %broadcast_in_dim.9), calls=%async_computation | async-start | bytes 1048576 | tf_op jit(solution)/shard_map/all_to_all | solution.py:85
  10.7 1.1 %broadcast_multiply_fusion = (bf16[1024,256]{1,0:T(8,128)(2,1)S(1)}, bf16[1024,256]{1,0:T(8,128)(2,1)}) fusion(bf16[128,256]{1,0:T(8,128)(2,1)S(1)} %copy-done, bf16[512,128]{1,0:T(8,128)(2,1)S(1)} %collective-permute-done, bf16[512,128]{1,0:T(8,128)(2,1)S(1)} %bitcast.36), kind=kOutput, calls=%fused_computation.30 | convolution fusion | flops 68157440 | bytes 1376256 | tf_op jit(solution)/shard_map/dot_general | solution.py:96
  11.8 5.6 %all-to-all-done = bf16[4,512,128]{2,1,0:T(8,128)(2,1)S(1)} async-done(((bf16[4,512,128]{2,1,0:T(8,128)(2,1)}), bf16[4,512,128]{2,1,0:T(8,128)(2,1)S(1)}, u32[]{:S(2)}, u32[]{:S(2)}) %all-to-all-start) | async-done | bytes 524320 | tf_op jit(solution)/shard_map/all_to_all | solution.py:85
  17.9 6.9 %shard_map.59 = f32[1024,4]{1,0:T(8,128)S(1)} custom-call(bf16[1024,256]{1,0:T(8,128)(2,1)S(1)} %get-tuple-element.33.ff_ref, bf16[2048,384]{1,0:T(8,128)(2,1)S(1)} %pad_maximum_fusion.kcat_ref, f32[2,2048]{1,0:T(2,128)S(1)} %pad_maximum_fusion.6.coord_ref), custom_call_target="tpu_custom_call" | custom-call | tf_op jit(solution)/shard_map/pallas_call | solution.py:62
  24.9 3.7 %collective-permute-start.1 = (f32[1024,4]{1,0:T(8,128)S(1)}, f32[1024,4]{1,0:T(8,128)}, u32[]{:S(2)}, u32[]{:S(2)}) collective-permute-start(f32[1024,4]{1,0:T(8,128)S(1)} %shard_map.59), channel_id=1, source_target_pairs={{0,32},{32,0},{1,33},{33,1},{2,34},{34,2},{3,35},{35,3},{4,36},{36... | collective-permute-start | bytes 49160 | tf_op jit(solution)/shard_map/ppermute | solution.py:102
  28.6 1.0 %copy.37 = f32[1024,1]{1,0:T(8,128)} copy(f32[1024,1]{0,1:T(1,128)S(1)} %get-tuple-element.27) | data formatting | bytes 8192 | tf_op jit(solution)/shard_map/squeeze | solution.py:116
  29.9 8.1 %collective-permute-done.1 = f32[1024,4]{1,0:T(8,128)} collective-permute-done((f32[1024,4]{1,0:T(8,128)S(1)}, f32[1024,4]{1,0:T(8,128)}, u32[]{:S(2)}, u32[]{:S(2)}) %collective-permute-start.1) | collective-permute-done | bytes 16416 | tf_op jit(solution)/shard_map/ppermute | solution.py:102
  38.0 1.1 %fusion.30 = (f32[512,4]{1,0:T(8,128)S(1)}, f32[512,4]{1,0:T(8,128)S(1)}) fusion(f32[1024,4]{1,0:T(8,128)} %collective-permute-done.1), kind=kLoop, calls=%fused_computation.79 | loop fusion | bytes 32768 | tf_op jit(solution)/shard_map/slice | solution.py:103
  39.1 1.2 %fusion.28 = (f32[1024,1]{1,0:T(8,128)S(1)}, f32[1024,1]{1,0:T(8,128)S(1)}, f32[1024]{0:T(1024)S(1)}, f32[1024]{0:T(1024)S(1)}, f32[1024]{0:T(1024)S(1)}, /*index=5*/f32[1024]{0:T(1024)S(1)}) fusion(f32[1024,1]{1,0:T(8,128)S(1)} %copy.36, f32[1024,1]{1,0:T(8,128)S(1)} %get-tuple-element.10, f32[512,4]{1,0:T(8,128)S(1)} %get-tuple-element.24, ...), kind=kLoop, calls=%fused_computation.77 | loop fusion | flops 9216 | bytes 65536 | tf_op jit(solution)/shard_map/mul | solution.py:118
  40.3 1.4 %fusion.29 = (f32[1024,1]{1,0:T(8,128)S(1)}, f32[1024,1]{1,0:T(8,128)S(1)}, f32[1024]{0:T(1024)S(1)}, f32[1024]{0:T(1024)S(1)}, f32[1024]{0:T(1024)S(1)}, /*index=5*/f32[1024]{0:T(1024)S(1)}) fusion(f32[1024,1]{1,0:T(8,128)S(1)} %copy-done.1, f32[1024,1]{1,0:T(8,128)S(1)} %get-tuple-element.12, f32[512,4]{1,0:T(8,128)S(1)} %get-tuple-element.24, ...), kind=kLoop, calls=%fused_computation.78 | loop fusion | flops 21504 | bytes 69632 | tf_op jit(solution)/shard_map/mul | solution.py:118
  42.3 6.3 %shard_map.60 = f32[1024,384]{1,0:T(8,128)S(1)} custom-call(bf16[1024,256]{1,0:T(8,128)(2,1)S(1)} %get-tuple-element.33.ff_ref, bf16[2048,384]{1,0:T(8,128)(2,1)S(1)} %pad_maximum_fusion.kcat_ref, f32[2,2048]{1,0:T(2,128)S(1)} %pad_maximum_fusion.6.coord_ref, f32[1024,4]{1,0:T(8,128)S(1)} %pad_maximum_fusion.2.coef_ref), custom_call_target="tpu_custom_call" | custom-call | tf_op jit(solution)/shard_map/pallas_call | solution.py:62
  49.2 0.6 convolution_add_fusion
  49.8 3.7 %collective-permute-start.3 = (f32[128,256]{1,0:T(8,128)S(1)}, f32[128,256]{1,0:T(8,128)S(1)}, u32[]{:S(2)}, u32[]{:S(2)}) collective-permute-start(f32[128,256]{1,0:T(8,128)S(1)} %convolution_add_fusion), channel_id=1, source_target_pairs={{0,1},{1,0},{2,3},{3,2},{4,5},{5,4},{6,7},{7,6},{8,9},{9,8},{10,11... | collective-permute-start | bytes 393224 | tf_op jit(solution)/shard_map/ppermute | solution.py:130
  53.5 1.0 collective-permute-done.3
  54.5 0.8 copy.40
  55.3 13.7 %all-to-all-start.1 = ((f32[128,1,256]{2,1,0:T(1,128)}), f32[128,1,256]{2,1,0:T(1,128)S(1)}, u32[]{:S(2)}, u32[]{:S(2)}) async-start(f32[128,1,256]{2,1,0:T(1,128)} %copy.40), calls=%async_computation.1 | async-start | bytes 262144 | tf_op jit(solution)/shard_map/all_to_all | solution.py:22
  69.0 11.4 %all-to-all-done.1 = f32[128,1,256]{2,1,0:T(1,128)S(1)} async-done(((f32[128,1,256]{2,1,0:T(1,128)}), f32[128,1,256]{2,1,0:T(1,128)S(1)}, u32[]{:S(2)}, u32[]{:S(2)}) %all-to-all-start.1) | async-done | bytes 131104 | tf_op jit(solution)/shard_map/all_to_all | solution.py:22
  80.6 0.7 broadcast_in_dim.21
  81.3 6.3 %all-to-all-start.2 = ((f32[128,1,256]{2,1,0:T(1,128)}), f32[128,1,256]{2,1,0:T(1,128)S(1)}, u32[]{:S(2)}, u32[]{:S(2)}) async-start(f32[128,1,256]{2,1,0:T(1,128)} %broadcast_in_dim.21), calls=%async_computation.2 | async-start | bytes 262144 | tf_op jit(solution)/shard_map/all_to_all | solution.py:24
  87.7 0.6 maximum_bitcast_fusion
  88.3 10.8 %all-to-all-done.2 = f32[128,1,256]{2,1,0:T(1,128)S(1)} async-done(((f32[128,1,256]{2,1,0:T(1,128)}), f32[128,1,256]{2,1,0:T(1,128)S(1)}, u32[]{:S(2)}, u32[]{:S(2)}) %all-to-all-start.2) | async-done | bytes 131104 | tf_op jit(solution)/shard_map/all_to_all | solution.py:24
  99.1 0.7 copy.47
  (32 shorter events, 2.5 us)
Async XLA Ops:
  0.6 10.0 %copy-start = (bf16[128,256]{1,0:T(8,128)(2,1)S(1)}, bf16[128,256]{1,0:T(8,128)(2,1)}, u32[]{:S(2)}) copy-start(bf16[128,256]{1,0:T(8,128)(2,1)} %param.6) | copy-start | bytes 196612
  0.6 10.0 %copy-start.3 = (bf16[1,512,128]{2,1,0:T(8,128)(2,1)S(1)}, bf16[1,512,128]{2,1,0:T(8,128)(2,1)}, u32[]{:S(2)}) copy-start(bf16[1,512,128]{2,1,0:T(8,128)(2,1)} %param.4) | copy-start | bytes 393220
  0.7 28.0 %collective-permute-start.2 = (f32[2,512]{1,0:T(2,128)}, f32[2,512]{1,0:T(2,128)S(1)}, u32[]{:S(2)}, u32[]{:S(2)}) collective-permute-start(f32[2,512]{1,0:T(2,128)} %bitcast.45), channel_id=1, source_target_pairs={{0,32},{32,0},{1,33},{33,1},{2,34},{34,2},{3,35},{35,3},{4,36},{36... | collective-permute-start | bytes 12296 | tf_op jit(solution)/shard_map/ppermute | solution.py:92
  4.5 6.2 %collective-permute-start = (bf16[512,128]{1,0:T(8,128)(2,1)}, bf16[512,128]{1,0:T(8,128)(2,1)S(1)}, u32[]{:S(2)}, u32[]{:S(2)}) collective-permute-start(bf16[512,128]{1,0:T(8,128)(2,1)} %bitcast.35), channel_id=1, source_target_pairs={{0,32},{32,0},{1,33},{33,1},{2,34},{34,2},{3,35},{35,3},{4,36},{36... | collective-permute-start | bytes 393224 | tf_op jit(solution)/shard_map/ppermute | solution.py:91
  6.4 11.0 %all-to-all-start = ((bf16[4,512,128]{2,1,0:T(8,128)(2,1)}), bf16[4,512,128]{2,1,0:T(8,128)(2,1)S(1)}, u32[]{:S(2)}, u32[]{:S(2)}) async-start(bf16[4,512,128]{2,1,0:T(8,128)(2,1)} %broadcast_in_dim.9), calls=%async_computation | async-start | bytes 1048576 | tf_op jit(solution)/shard_map/all_to_all | solution.py:85
  17.9 10.7 %copy-start.4 = (f32[1,2,512]{2,1,0:T(2,128)S(1)}, f32[1,2,512]{2,1,0:T(2,128)}, u32[]{:S(2)}) copy-start(f32[1,2,512]{2,1,0:T(2,128)} %param.7) | copy-start | bytes 12292
  24.9 13.1 %collective-permute-start.1 = (f32[1024,4]{1,0:T(8,128)S(1)}, f32[1024,4]{1,0:T(8,128)}, u32[]{:S(2)}, u32[]{:S(2)}) collective-permute-start(f32[1024,4]{1,0:T(8,128)S(1)} %shard_map.59), channel_id=1, source_target_pairs={{0,32},{32,0},{1,33},{33,1},{2,34},{34,2},{3,35},{35,3},{4,36},{36... | collective-permute-start | bytes 49160 | tf_op jit(solution)/shard_map/ppermute | solution.py:102
  39.1 1.2 %copy-start.1 = (f32[1024,1]{1,0:T(8,128)S(1)}, f32[1024,1]{1,0:T(8,128)}, u32[]{:S(2)}) copy-start(f32[1024,1]{1,0:T(8,128)} %copy.37) | copy-start | bytes 12292
  42.2 6.4 %copy-start.2 = (bf16[1024,256]{1,0:T(8,128)(2,1)S(1)}, bf16[1024,256]{1,0:T(8,128)(2,1)}, u32[]{:S(2)}) copy-start(bf16[1024,256]{1,0:T(8,128)(2,1)} %get-tuple-element.34) | copy-start | bytes 1572868
  49.8 4.7 %collective-permute-start.3 = (f32[128,256]{1,0:T(8,128)S(1)}, f32[128,256]{1,0:T(8,128)S(1)}, u32[]{:S(2)}, u32[]{:S(2)}) collective-permute-start(f32[128,256]{1,0:T(8,128)S(1)} %convolution_add_fusion), channel_id=1, source_target_pairs={{0,1},{1,0},{2,3},{3,2},{4,5},{5,4},{6,7},{7,6},{8,9},{9,8},{10,11... | collective-permute-start | bytes 393224 | tf_op jit(solution)/shard_map/ppermute | solution.py:130
  55.3 25.2 %all-to-all-start.1 = ((f32[128,1,256]{2,1,0:T(1,128)}), f32[128,1,256]{2,1,0:T(1,128)S(1)}, u32[]{:S(2)}, u32[]{:S(2)}) async-start(f32[128,1,256]{2,1,0:T(1,128)} %copy.40), calls=%async_computation.1 | async-start | bytes 262144 | tf_op jit(solution)/shard_map/all_to_all | solution.py:22
  81.3 17.8 %all-to-all-start.2 = ((f32[128,1,256]{2,1,0:T(1,128)}), f32[128,1,256]{2,1,0:T(1,128)S(1)}, u32[]{:S(2)}, u32[]{:S(2)}) async-start(f32[128,1,256]{2,1,0:T(1,128)} %broadcast_in_dim.21), calls=%async_computation.2 | async-start | bytes 262144 | tf_op jit(solution)/shard_map/all_to_all | solution.py:24

commit v7 on v5

--- a/solution.py
+++ b/solution.py
@@ -48,9 +48,10 @@
     g2_ref[...] = both[:, channels:]
 
 
-def corr_call(first_feat, key_cat, coords, grads, scaling, channels, tile=128):
+def corr_call(first_feat, key_cat, coords, grads, scaling, channels, tile=512):
     assert scaling == 2.0 ** round(math.log2(scaling))
     rows = first_feat.shape[0]
+    tile = min(tile, rows)
     keys, width = key_cat.shape
     extra = width - channels
     kernel = functools.partial(corr_kernel, scaling=scaling, channels=channels)

time: 83.7 us -> 80.5 us (0.962)
  Pallas kernels: 9.38 us -> 6.13 us
    pallas_call x1, Pallas kernels: 9.38 us -> 6.13 us  [corr_call(): pl.pallas_call(kernel, grid=(rows // tile,), in_specs=[pl.BlockSpec((tile...]
where the time goes in v7:
time: 80.5 us; the launch traced here: 80.2 us
  waiting for transfers between devices  38 us (47%)
  starting transfers between devices  27.8 us (35%)
  Pallas kernels  6.13 us (8%)
  local copies, waits for them, and re-layouts  4.68 us (6%)
  matrix products  1.6 us (2%)
  other arithmetic  1.25 us (2%)
    all_to_all x1, waiting for transfers between devices, body(): lax.all_to_all(spread, 'blk', 0, 0, tiled=True)  15.1 us
    all_to_all x1, starting transfers between devices, all_sum(): mine = lax.all_to_all(chunks, axes, 0, 0, tiled=True).sum(axis=0)  12.6 us
    all_to_all x1, waiting for transfers between devices, all_sum(): mine = lax.all_to_all(chunks, axes, 0, 0, tiled=True).sum(axis=0)  11.1 us
    all_to_all x1, waiting for transfers between devices, all_sum(): return lax.all_to_all(spread, axes, 0, 0, tiled=True).reshape(x.shape)  10.8 us
    all_to_all x1, starting transfers between devices, body(): lax.all_to_all(spread, 'blk', 0, 0, tiled=True)  7.47 us
    all_to_all x1, starting transfers between devices, all_sum(): return lax.all_to_all(spread, axes, 0, 0, tiled=True).reshape(x.shape)  6.34 us
    pallas_call x1, Pallas kernels, corr_call(): pl.pallas_call(kernel, grid=(rows // tile,), in_specs=[pl.BlockSpec((tile...  6.13 us
    broadcast_in_dim x1, local copies, waits for them, and re-layouts, body(): spread = jnp.broadcast_to(second_in[None], (n_blk,) + second_in.shape)  2.07 us
  transfers between devices with their start and end apart: 4, of which 4 were waited for; matrix products, arithmetic and copies ran while one was open for 2% of the time, Pallas kernels for 0%

profile of v7, /device:TPU:1, one launch (start us, length us, event | category | flops | bytes accessed | tf_op | source)
XLA Modules:
  0.0 80.2 jit_solution(477771600200170819)
XLA Ops:
  0.6 0.0 copy-start
  0.7 2.1 %broadcast_in_dim.17 = bf16[8,512,128]{2,1,0:T(8,128)(2,1)} broadcast(bf16[512,128]{1,0:T(8,128)(2,1)} %bitcast.32), dimensions={1,2} | broadcast | bytes 1179648 | tf_op jit(solution)/shard_map/broadcast_in_dim | solution.py:91
  2.7 7.5 %all-to-all-start = ((bf16[8,512,128]{2,1,0:T(8,128)(2,1)}), bf16[8,512,128]{2,1,0:T(8,128)(2,1)S(1)}, u32[]{:S(2)}, u32[]{:S(2)}) async-start(bf16[8,512,128]{2,1,0:T(8,128)(2,1)} %broadcast_in_dim.17), calls=%async_computation | async-start | bytes 2097152 | tf_op jit(solution)/shard_map/all_to_all | solution.py:92
  10.2 0.2 broadcast_multiply_fusion
  10.5 0.1 copy.13.grad_ref
  10.6 0.1 fusion.4
  10.7 15.1 %all-to-all-done = bf16[8,512,128]{2,1,0:T(8,128)(2,1)S(1)} async-done(((bf16[8,512,128]{2,1,0:T(8,128)(2,1)}), bf16[8,512,128]{2,1,0:T(8,128)(2,1)S(1)}, u32[]{:S(2)}, u32[]{:S(2)}) %all-to-all-start) | async-done | bytes 1048608 | tf_op jit(solution)/shard_map/all_to_all | solution.py:92
  25.8 0.7 convolution_convert_fusion
  26.5 0.3 pad_maximum_fusion.kcat_ref
  26.8 6.1 %shard_map.59 = (f32[512,2]{1,0:T(8,128)S(1)}, bf16[512,256]{1,0:T(8,128)(2,1)S(1)}, f32[512,128]{1,0:T(8,128)S(1)}) custom-call(bf16[512,256]{1,0:T(8,128)(2,1)S(1)} %get-tuple-element.12.ff_ref, bf16[4096,384]{1,0:T(8,128)(2,1)S(1)} %pad_maximum_fusion.kcat_ref, f32[2,4096]{1,0:T(2,128)S(1)} %pad_maximum_fusion.1.coord_ref, f32[512,2]{1,0:T(8,128)S(1)} %copy.13.grad_ref), custom_call_target="tpu_custom_call" | custom-call | tf_op jit(solution)/shard_map/pallas_call | solution.py:58
  33.0 0.3 convolution_bitcast_fusion
  33.2 0.4 fusion
  33.7 1.3 %collective-permute-start = (f32[128,256]{0,1:T(8,128)S(1)}, f32[128,256]{0,1:T(8,128)S(1)}, u32[]{:S(2)}, u32[]{:S(2)}) collective-permute-start(f32[128,256]{0,1:T(8,128)S(1)} %fusion), channel_id=1, source_target_pairs={{0,1},{1,0},{2,3},{3,2},{4,5},{5,4},{6,7},{7,6},{8,9},{9,8},{10,11... | collective-permute-start | bytes 393224 | tf_op jit(solution)/shard_map/ppermute | solution.py:111
  35.0 1.0 %collective-permute-done = f32[128,256]{0,1:T(8,128)S(1)} collective-permute-done((f32[128,256]{0,1:T(8,128)S(1)}, f32[128,256]{0,1:T(8,128)S(1)}, u32[]{:S(2)}, u32[]{:S(2)}) %collective-permute-start) | collective-permute-done | bytes 131104 | tf_op jit(solution)/shard_map/ppermute | solution.py:111
  36.0 0.8 copy.15
  36.8 12.6 %all-to-all-start.1 = ((f32[128,1,256]{2,1,0:T(1,128)}), f32[128,1,256]{2,1,0:T(1,128)S(1)}, u32[]{:S(2)}, u32[]{:S(2)}) async-start(f32[128,1,256]{2,1,0:T(1,128)} %copy.15), calls=%async_computation.1 | async-start | bytes 262144 | tf_op jit(solution)/shard_map/all_to_all | solution.py:22
  49.4 0.3 slice_reduce_fusion.1
  49.8 11.1 %all-to-all-done.1 = f32[128,1,256]{2,1,0:T(1,128)S(1)} async-done(((f32[128,1,256]{2,1,0:T(1,128)}), f32[128,1,256]{2,1,0:T(1,128)S(1)}, u32[]{:S(2)}, u32[]{:S(2)}) %all-to-all-start.1) | async-done | bytes 131104 | tf_op jit(solution)/shard_map/all_to_all | solution.py:22
  60.9 0.2 reduce_sum.9
  61.0 0.7 broadcast_in_dim.19
  61.8 6.3 %all-to-all-start.2 = ((f32[128,1,256]{2,1,0:T(1,128)}), f32[128,1,256]{2,1,0:T(1,128)S(1)}, u32[]{:S(2)}, u32[]{:S(2)}) async-start(f32[128,1,256]{2,1,0:T(1,128)} %broadcast_in_dim.19), calls=%async_computation.2 | async-start | bytes 262144 | tf_op jit(solution)/shard_map/all_to_all | solution.py:24
  68.1 0.6 maximum_bitcast_fusion
  68.7 10.8 %all-to-all-done.2 = f32[128,1,256]{2,1,0:T(1,128)S(1)} async-done(((f32[128,1,256]{2,1,0:T(1,128)}), f32[128,1,256]{2,1,0:T(1,128)S(1)}, u32[]{:S(2)}, u32[]{:S(2)}) %all-to-all-start.2) | async-done | bytes 131104 | tf_op jit(solution)/shard_map/all_to_all | solution.py:24
  79.5 0.7 copy.20
  (11 shorter events, 0.1 us)
Async XLA Ops:
  0.6 9.6 %copy-start = (bf16[1,512,128]{2,1,0:T(8,128)(2,1)S(1)}, bf16[1,512,128]{2,1,0:T(8,128)(2,1)}, u32[]{:S(2)}) copy-start(bf16[1,512,128]{2,1,0:T(8,128)(2,1)} %param.4) | copy-start | bytes 393220
  0.6 9.6 %copy-start.2 = (f32[1,2,512]{2,1,0:T(2,128)S(1)}, f32[1,2,512]{2,1,0:T(2,128)}, u32[]{:S(2)}) copy-start(f32[1,2,512]{2,1,0:T(2,128)} %param.7) | copy-start | bytes 12292
  0.7 9.6 %copy-start.1 = (bf16[128,256]{1,0:T(8,128)(2,1)S(1)}, bf16[128,256]{1,0:T(8,128)(2,1)}, u32[]{:S(2)}) copy-start(bf16[128,256]{1,0:T(8,128)(2,1)} %param.6) | copy-start | bytes 196612
  2.7 23.1 %all-to-all-start = ((bf16[8,512,128]{2,1,0:T(8,128)(2,1)}), bf16[8,512,128]{2,1,0:T(8,128)(2,1)S(1)}, u32[]{:S(2)}, u32[]{:S(2)}) async-start(bf16[8,512,128]{2,1,0:T(8,128)(2,1)} %broadcast_in_dim.17), calls=%async_computation | async-start | bytes 2097152 | tf_op jit(solution)/shard_map/all_to_all | solution.py:92
  33.7 2.3 %collective-permute-start = (f32[128,256]{0,1:T(8,128)S(1)}, f32[128,256]{0,1:T(8,128)S(1)}, u32[]{:S(2)}, u32[]{:S(2)}) collective-permute-start(f32[128,256]{0,1:T(8,128)S(1)} %fusion), channel_id=1, source_target_pairs={{0,1},{1,0},{2,3},{3,2},{4,5},{5,4},{6,7},{7,6},{8,9},{9,8},{10,11... | collective-permute-start | bytes 393224 | tf_op jit(solution)/shard_map/ppermute | solution.py:111
  36.8 24.1 %all-to-all-start.1 = ((f32[128,1,256]{2,1,0:T(1,128)}), f32[128,1,256]{2,1,0:T(1,128)S(1)}, u32[]{:S(2)}, u32[]{:S(2)}) async-start(f32[128,1,256]{2,1,0:T(1,128)} %copy.15), calls=%async_computation.1 | async-start | bytes 262144 | tf_op jit(solution)/shard_map/all_to_all | solution.py:22
  61.8 17.8 %all-to-all-start.2 = ((f32[128,1,256]{2,1,0:T(1,128)}), f32[128,1,256]{2,1,0:T(1,128)S(1)}, u32[]{:S(2)}, u32[]{:S(2)}) async-start(f32[128,1,256]{2,1,0:T(1,128)} %broadcast_in_dim.19), calls=%async_computation.2 | async-start | bytes 262144 | tf_op jit(solution)/shard_map/all_to_all | solution.py:24

commit v8 on v7

--- a/solution.py
+++ b/solution.py
@@ -24,11 +24,10 @@
     return lax.all_to_all(spread, axes, 0, 0, tiled=True).reshape(x.shape)
 
 
-def corr_kernel(ff_ref, kcat_ref, coord_ref, grad_ref, mean_ref, d1_ref, g2_ref, *, scaling, channels):
-    keys = kcat_ref[...]
-    logits = lax.dot_general(
-        ff_ref[...], keys[:, :channels], (((1,), (1,)), ((), ())), preferred_element_type=jnp.float32
-    )
+def corr_kernel(ff_ref, kin_ref, w_ref, coord_ref, grad_ref, mean_ref, d1_ref, g2_ref, *, scaling):
+    key_in = kin_ref[...]
+    key_feat = jnp.dot(key_in, w_ref[...], preferred_element_type=jnp.float32).astype(jnp.bfloat16)
+    logits = lax.dot_general(ff_ref[...], key_feat, (((1,), (1,)), ((), ())), preferred_element_type=jnp.float32)
     top = jnp.max(logits, axis=1, keepdims=True)
     expo = jnp.exp(logits - top)
     inv_total = 1.0 / jnp.sum(expo, axis=1, keepdims=True)
@@ -42,40 +41,39 @@
     slope = (expo * ((grad_col * inv_total) * key_col + (grad_row * inv_total) * key_row - inner * inv_total)).astype(
         jnp.bfloat16
     )
-    both = jnp.dot(slope, keys, preferred_element_type=jnp.float32)
     mean_ref[...] = jnp.concatenate([mean_col, mean_row], axis=1)
-    d1_ref[...] = (scaling * both[:, :channels]).astype(jnp.bfloat16)
-    g2_ref[...] = both[:, channels:]
+    d1_ref[...] = (scaling * jnp.dot(slope, key_feat, preferred_element_type=jnp.float32)).astype(jnp.bfloat16)
+    g2_ref[...] = jnp.dot(slope, key_in, preferred_element_type=jnp.float32)
 
 
-def corr_call(first_feat, key_cat, coords, grads, scaling, channels, tile=512):
+def corr_call(first_feat, key_in, weight, coords, grads, scaling, tile=512):
     assert scaling == 2.0 ** round(math.log2(scaling))
-    rows = first_feat.shape[0]
+    rows, channels = first_feat.shape
     tile = min(tile, rows)
-    keys, width = key_cat.shape
-    extra = width - channels
-    kernel = functools.partial(corr_kernel, scaling=scaling, channels=channels)
+    keys, width = key_in.shape
+    kernel = functools.partial(corr_kernel, scaling=scaling)
     return pl.pallas_call(
         kernel,
         grid=(rows // tile,),
         in_specs=[
             pl.BlockSpec((tile, channels), lambda i: (i, 0)),
             pl.BlockSpec((keys, width), lambda i: (0, 0)),
+            pl.BlockSpec(weight.shape, lambda i: (0, 0)),
             pl.BlockSpec(coords.shape, lambda i: (0, 0)),
             pl.BlockSpec((tile, grads.shape[1]), lambda i: (i, 0)),
         ],
         out_specs=[
             pl.BlockSpec((tile, 2), lambda i: (i, 0)),
             pl.BlockSpec((tile, channels), lambda i: (i, 0)),
-            pl.BlockSpec((tile, extra), lambda i: (i, 0)),
+            pl.BlockSpec((tile, width), lambda i: (i, 0)),
         ],
         out_shape=[
             jax.ShapeDtypeStruct((rows, 2), jnp.float32),
             jax.ShapeDtypeStruct((rows, channels), jnp.bfloat16),
-            jax.ShapeDtypeStruct((rows, extra), jnp.float32),
+            jax.ShapeDtypeStruct((rows, width), jnp.float32),
         ],
         compiler_params=pltpu.CompilerParams(vmem_limit_bytes=48 * 1024 * 1024),
-    )(first_feat * jnp.asarray(scaling, first_feat.dtype), key_cat, coords, grads)
+    )(first_feat * jnp.asarray(scaling, first_feat.dtype), key_in, weight, coords, grads)
 
 
 def body(frame_one, frame_two, encoder_weight, flow_grad, n_blk, n_batch):
@@ -94,12 +92,10 @@
     own_col, own_row = coords_of(blk * query_count + jnp.arange(query_count, dtype=jnp.int32))
 
     first_feat = jnp.dot(first_in, encoder_weight, preferred_element_type=jnp.float32).astype(jnp.bfloat16)
-    key_feat = jnp.dot(key_in, encoder_weight, preferred_element_type=jnp.float32).astype(jnp.bfloat16)
 
-    key_cat = jnp.concatenate([key_feat, key_in], axis=1)
     coords = jnp.stack([key_col, key_row])
     grads = jnp.stack([grad_col, grad_row], axis=1)
-    means, delta_one, slope_two = corr_call(first_feat, key_cat, coords, grads, scaling, channels)
+    means, delta_one, slope_two = corr_call(first_feat, key_in, encoder_weight, coords, grads, scaling)
     flow = jnp.stack([means[:, 0] - own_col, means[:, 1] - own_row])[None]
     local_grad = jnp.dot(first_in.T, delta_one, preferred_element_type=jnp.float32)
     local_grad = local_grad + scaling * jnp.dot(

time: 80.5 us -> 80.3 us (level)
  no operation moved by 1% of the time
where the time goes in v8:
time: 80.3 us; the launch traced here: 80 us
  waiting for transfers between devices  38 us (47%)
  starting transfers between devices  27.9 us (35%)
  Pallas kernels  6.85 us (9%)
  local copies, waits for them, and re-layouts  4.66 us (6%)
  other arithmetic  0.93 us (1%)
  matrix products  0.9 us (1%)
    all_to_all x1, waiting for transfers between devices, body(): lax.all_to_all(spread, 'blk', 0, 0, tiled=True)  15.1 us
    all_to_all x1, starting transfers between devices, all_sum(): mine = lax.all_to_all(chunks, axes, 0, 0, tiled=True).sum(axis=0)  12.6 us
    all_to_all x1, waiting for transfers between devices, all_sum(): mine = lax.all_to_all(chunks, axes, 0, 0, tiled=True).sum(axis=0)  11.1 us
    all_to_all x1, waiting for transfers between devices, all_sum(): return lax.all_to_all(spread, axes, 0, 0, tiled=True).reshape(x.shape)  10.8 us
    all_to_all x1, starting transfers between devices, body(): lax.all_to_all(spread, 'blk', 0, 0, tiled=True)  7.6 us
    pallas_call x1, Pallas kernels, corr_call(): pl.pallas_call(kernel, grid=(rows // tile,), in_specs=[pl.BlockSpec((tile...  6.85 us
    all_to_all x1, starting transfers between devices, all_sum(): return lax.all_to_all(spread, axes, 0, 0, tiled=True).reshape(x.shape)  6.34 us
    broadcast_in_dim x1, local copies, waits for them, and re-layouts, body(): spread = jnp.broadcast_to(second_in[None], (n_blk,) + second_in.shape)  2.05 us
  transfers between devices with their start and end apart: 4, of which 4 were waited for; matrix products, arithmetic and copies ran while one was open for 2% of the time, Pallas kernels for 0%

profile of v8, /device:TPU:1, one launch (start us, length us, event | category | flops | bytes accessed | tf_op | source)
XLA Modules:
  0.0 80.0 jit_solution(17589181911779015530)
XLA Ops:
  0.6 0.0 copy-start
  0.6 2.0 %broadcast_in_dim.17 = bf16[8,512,128]{2,1,0:T(8,128)(2,1)} broadcast(bf16[512,128]{1,0:T(8,128)(2,1)} %bitcast.29), dimensions={1,2} | broadcast | bytes 1179648 | tf_op jit(solution)/shard_map/broadcast_in_dim | solution.py:89
  2.7 7.6 %all-to-all-start = ((bf16[8,512,128]{2,1,0:T(8,128)(2,1)}), bf16[8,512,128]{2,1,0:T(8,128)(2,1)S(1)}, u32[]{:S(2)}, u32[]{:S(2)}) async-start(bf16[8,512,128]{2,1,0:T(8,128)(2,1)} %broadcast_in_dim.17), calls=%async_computation | async-start | bytes 2097152 | tf_op jit(solution)/shard_map/all_to_all | solution.py:90
  10.3 0.0 copy-done.2
  10.3 0.0 copy-done
  10.3 0.2 broadcast_multiply_fusion
  10.6 0.1 copy.10.grad_ref
  10.7 0.1 fusion.4
  10.8 15.1 %all-to-all-done = bf16[8,512,128]{2,1,0:T(8,128)(2,1)S(1)} async-done(((bf16[8,512,128]{2,1,0:T(8,128)(2,1)}), bf16[8,512,128]{2,1,0:T(8,128)(2,1)S(1)}, u32[]{:S(2)}, u32[]{:S(2)}) %all-to-all-start) | async-done | bytes 1048608 | tf_op jit(solution)/shard_map/all_to_all | solution.py:90
  25.9 6.8 %shard_map.59 = (f32[512,2]{1,0:T(8,128)S(1)}, bf16[512,256]{1,0:T(8,128)(2,1)S(1)}, f32[512,128]{1,0:T(8,128)S(1)}) custom-call(bf16[512,256]{1,0:T(8,128)(2,1)S(1)} %get-tuple-element.12.ff_ref, bf16[4096,128]{1,0:T(8,128)(2,1)S(1)} %bitcast.28, bf16[128,256]{1,0:T(8,128)(2,1)S(1)} %copy-done.1, f32[2,4096]{1,0:T(2,128)S(1)} %pad_maximum_fusion.coord_ref, ...), custom_call_target="tpu_custom_call" | custom-call | tf_op jit(solution)/shard_map/pallas_call | solution.py:55
  32.8 0.3 convolution_bitcast_fusion
  33.0 0.4 fusion
  33.5 1.3 %collective-permute-start = (f32[128,256]{0,1:T(8,128)S(1)}, f32[128,256]{0,1:T(8,128)S(1)}, u32[]{:S(2)}, u32[]{:S(2)}) collective-permute-start(f32[128,256]{0,1:T(8,128)S(1)} %fusion), channel_id=1, source_target_pairs={{0,1},{1,0},{2,3},{3,2},{4,5},{5,4},{6,7},{7,6},{8,9},{9,8},{10,11... | collective-permute-start | bytes 393224 | tf_op jit(solution)/shard_map/ppermute | solution.py:107
  34.8 1.0 %collective-permute-done = f32[128,256]{0,1:T(8,128)S(1)} collective-permute-done((f32[128,256]{0,1:T(8,128)S(1)}, f32[128,256]{0,1:T(8,128)S(1)}, u32[]{:S(2)}, u32[]{:S(2)}) %collective-permute-start) | collective-permute-done | bytes 131104 | tf_op jit(solution)/shard_map/ppermute | solution.py:107
  35.8 0.8 copy.12
  36.6 12.6 %all-to-all-start.1 = ((f32[128,1,256]{2,1,0:T(1,128)}), f32[128,1,256]{2,1,0:T(1,128)S(1)}, u32[]{:S(2)}, u32[]{:S(2)}) async-start(f32[128,1,256]{2,1,0:T(1,128)} %copy.12), calls=%async_computation.1 | async-start | bytes 262144 | tf_op jit(solution)/shard_map/all_to_all | solution.py:22
  49.2 0.3 slice_reduce_fusion.1
  49.6 11.1 %all-to-all-done.1 = f32[128,1,256]{2,1,0:T(1,128)S(1)} async-done(((f32[128,1,256]{2,1,0:T(1,128)}), f32[128,1,256]{2,1,0:T(1,128)S(1)}, u32[]{:S(2)}, u32[]{:S(2)}) %all-to-all-start.1) | async-done | bytes 131104 | tf_op jit(solution)/shard_map/all_to_all | solution.py:22
  60.7 0.2 reduce_sum.9
  60.8 0.7 broadcast_in_dim.19
  61.6 6.3 %all-to-all-start.2 = ((f32[128,1,256]{2,1,0:T(1,128)}), f32[128,1,256]{2,1,0:T(1,128)S(1)}, u32[]{:S(2)}, u32[]{:S(2)}) async-start(f32[128,1,256]{2,1,0:T(1,128)} %broadcast_in_dim.19), calls=%async_computation.2 | async-start | bytes 262144 | tf_op jit(solution)/shard_map/all_to_all | solution.py:24
  67.9 0.6 maximum_bitcast_fusion
  68.5 10.8 %all-to-all-done.2 = f32[128,1,256]{2,1,0:T(1,128)S(1)} async-done(((f32[128,1,256]{2,1,0:T(1,128)}), f32[128,1,256]{2,1,0:T(1,128)S(1)}, u32[]{:S(2)}, u32[]{:S(2)}) %all-to-all-start.2) | async-done | bytes 131104 | tf_op jit(solution)/shard_map/all_to_all | solution.py:24
  79.3 0.7 copy.16
  (9 shorter events, 0.1 us)
Async XLA Ops:
  0.6 9.7 %copy-start = (bf16[1,512,128]{2,1,0:T(8,128)(2,1)S(1)}, bf16[1,512,128]{2,1,0:T(8,128)(2,1)}, u32[]{:S(2)}) copy-start(bf16[1,512,128]{2,1,0:T(8,128)(2,1)} %param.4) | copy-start | bytes 393220
  2.7 7.6 %copy-start.2 = (f32[1,2,512]{2,1,0:T(2,128)S(1)}, f32[1,2,512]{2,1,0:T(2,128)}, u32[]{:S(2)}) copy-start(f32[1,2,512]{2,1,0:T(2,128)} %param.7) | copy-start | bytes 12292
  2.7 7.6 %copy-start.1 = (bf16[128,256]{1,0:T(8,128)(2,1)S(1)}, bf16[128,256]{1,0:T(8,128)(2,1)}, u32[]{:S(2)}) copy-start(bf16[128,256]{1,0:T(8,128)(2,1)} %w_ref.1) | copy-start | bytes 196612
  2.7 23.2 %all-to-all-start = ((bf16[8,512,128]{2,1,0:T(8,128)(2,1)}), bf16[8,512,128]{2,1,0:T(8,128)(2,1)S(1)}, u32[]{:S(2)}, u32[]{:S(2)}) async-start(bf16[8,512,128]{2,1,0:T(8,128)(2,1)} %broadcast_in_dim.17), calls=%async_computation | async-start | bytes 2097152 | tf_op jit(solution)/shard_map/all_to_all | solution.py:90
  33.5 2.3 %collective-permute-start = (f32[128,256]{0,1:T(8,128)S(1)}, f32[128,256]{0,1:T(8,128)S(1)}, u32[]{:S(2)}, u32[]{:S(2)}) collective-permute-start(f32[128,256]{0,1:T(8,128)S(1)} %fusion), channel_id=1, source_target_pairs={{0,1},{1,0},{2,3},{3,2},{4,5},{5,4},{6,7},{7,6},{8,9},{9,8},{10,11... | collective-permute-start | bytes 393224 | tf_op jit(solution)/shard_map/ppermute | solution.py:107
  36.6 24.1 %all-to-all-start.1 = ((f32[128,1,256]{2,1,0:T(1,128)}), f32[128,1,256]{2,1,0:T(1,128)S(1)}, u32[]{:S(2)}, u32[]{:S(2)}) async-start(f32[128,1,256]{2,1,0:T(1,128)} %copy.12), calls=%async_computation.1 | async-start | bytes 262144 | tf_op jit(solution)/shard_map/all_to_all | solution.py:22
  61.6 17.8 %all-to-all-start.2 = ((f32[128,1,256]{2,1,0:T(1,128)}), f32[128,1,256]{2,1,0:T(1,128)S(1)}, u32[]{:S(2)}, u32[]{:S(2)}) async-start(f32[128,1,256]{2,1,0:T(1,128)} %broadcast_in_dim.19), calls=%async_computation.2 | async-start | bytes 262144 | tf_op jit(solution)/shard_map/all_to_all | solution.py:24

commit v9 on v8

--- a/solution.py
+++ b/solution.py
@@ -24,7 +24,7 @@
     return lax.all_to_all(spread, axes, 0, 0, tiled=True).reshape(x.shape)
 
 
-def corr_kernel(ff_ref, kin_ref, w_ref, coord_ref, grad_ref, mean_ref, d1_ref, g2_ref, *, scaling):
+def corr_kernel(ff_ref, qin_ref, kin_ref, w_ref, coord_ref, grad_ref, mean_ref, lg_ref, *, scaling):
     key_in = kin_ref[...]
     key_feat = jnp.dot(key_in, w_ref[...], preferred_element_type=jnp.float32).astype(jnp.bfloat16)
     logits = lax.dot_general(ff_ref[...], key_feat, (((1,), (1,)), ((), ())), preferred_element_type=jnp.float32)
@@ -42,38 +42,35 @@
         jnp.bfloat16
     )
     mean_ref[...] = jnp.concatenate([mean_col, mean_row], axis=1)
-    d1_ref[...] = (scaling * jnp.dot(slope, key_feat, preferred_element_type=jnp.float32)).astype(jnp.bfloat16)
-    g2_ref[...] = jnp.dot(slope, key_in, preferred_element_type=jnp.float32)
+    delta_one = (scaling * jnp.dot(slope, key_feat, preferred_element_type=jnp.float32)).astype(jnp.bfloat16)
+    slope_two = jnp.dot(slope, key_in, preferred_element_type=jnp.float32)
+    two_hi = slope_two.astype(jnp.bfloat16)
+    two_lo = (slope_two - two_hi.astype(jnp.float32)).astype(jnp.bfloat16)
+    tn = (((0,), (0,)), ((), ()))
+    ff = ff_ref[...]
+    local = lax.dot_general(qin_ref[...], delta_one, tn, preferred_element_type=jnp.float32)
+    local = local + lax.dot_general(two_hi, ff, tn, preferred_element_type=jnp.float32)
+    lg_ref[...] = local + lax.dot_general(two_lo, ff, tn, preferred_element_type=jnp.float32)
 
 
-def corr_call(first_feat, key_in, weight, coords, grads, scaling, tile=512):
+def corr_call(first_feat, first_in, key_in, weight, coords, grads, scaling):
     assert scaling == 2.0 ** round(math.log2(scaling))
     rows, channels = first_feat.shape
-    tile = min(tile, rows)
-    keys, width = key_in.shape
+    width = key_in.shape[1]
     kernel = functools.partial(corr_kernel, scaling=scaling)
+    whole = lambda a: pl.BlockSpec(a.shape, lambda i: (0,) * a.ndim)
+    operands = (first_feat * jnp.asarray(scaling, first_feat.dtype), first_in, key_in, weight, coords, grads)
     return pl.pallas_call(
         kernel,
-        grid=(rows // tile,),
-        in_specs=[
-            pl.BlockSpec((tile, channels), lambda i: (i, 0)),
-            pl.BlockSpec((keys, width), lambda i: (0, 0)),
-            pl.BlockSpec(weight.shape, lambda i: (0, 0)),
-            pl.BlockSpec(coords.shape, lambda i: (0, 0)),
-            pl.BlockSpec((tile, grads.shape[1]), lambda i: (i, 0)),
-        ],
-        out_specs=[
-            pl.BlockSpec((tile, 2), lambda i: (i, 0)),
-            pl.BlockSpec((tile, channels), lambda i: (i, 0)),
-            pl.BlockSpec((tile, width), lambda i: (i, 0)),
-        ],
+        grid=(1,),
+        in_specs=[whole(a) for a in operands],
+        out_specs=[pl.BlockSpec((rows, 2), lambda i: (0, 0)), pl.BlockSpec((width, channels), lambda i: (0, 0))],
         out_shape=[
             jax.ShapeDtypeStruct((rows, 2), jnp.float32),
-            jax.ShapeDtypeStruct((rows, channels), jnp.bfloat16),
-            jax.ShapeDtypeStruct((rows, width), jnp.float32),
+            jax.ShapeDtypeStruct((width, channels), jnp.float32),
         ],
         compiler_params=pltpu.CompilerParams(vmem_limit_bytes=48 * 1024 * 1024),
-    )(first_feat * jnp.asarray(scaling, first_feat.dtype), key_in, weight, coords, grads)
+    )(*operands)
 
 
 def body(frame_one, frame_two, encoder_weight, flow_grad, n_blk, n_batch):
@@ -95,15 +92,8 @@
 
     coords = jnp.stack([key_col, key_row])
     grads = jnp.stack([grad_col, grad_row], axis=1)
-    means, delta_one, slope_two = corr_call(first_feat, key_in, encoder_weight, coords, grads, scaling)
+    means, local_grad = corr_call(first_feat, first_in, key_in, encoder_weight, coords, grads, scaling)
     flow = jnp.stack([means[:, 0] - own_col, means[:, 1] - own_row])[None]
-    local_grad = jnp.dot(first_in.T, delta_one, preferred_element_type=jnp.float32)
-    local_grad = local_grad + scaling * jnp.dot(
-        slope_two.T,
-        first_feat.astype(jnp.float32),
-        precision=lax.Precision.HIGHEST,
-        preferred_element_type=jnp.float32,
-    )
     local_grad = local_grad + lax.ppermute(local_grad, "core", [(0, 1), (1, 0)])
     grad_w = all_sum(local_grad, ("blk", "chip"), n_blk * n_batch // 2)
     return (flow, grad_w)

time: 80.3 us -> 79.9 us (level)
  no operation moved by 1% of the time
where the time goes in v9:
time: 79.9 us; the launch traced here: 79.6 us
  waiting for transfers between devices  38 us (48%)
  starting transfers between devices  27.9 us (35%)
  Pallas kernels  7.17 us (9%)
  local copies, waits for them, and re-layouts  4.66 us (6%)
  other arithmetic  0.93 us (1%)
    all_to_all x1, waiting for transfers between devices, body(): lax.all_to_all(spread, 'blk', 0, 0, tiled=True)  15.1 us
    all_to_all x1, starting transfers between devices, all_sum(): mine = lax.all_to_all(chunks, axes, 0, 0, tiled=True).sum(axis=0)  12.6 us
    all_to_all x1, waiting for transfers between devices, all_sum(): mine = lax.all_to_all(chunks, axes, 0, 0, tiled=True).sum(axis=0)  11.1 us
    all_to_all x1, waiting for transfers between devices, all_sum(): return lax.all_to_all(spread, axes, 0, 0, tiled=True).reshape(x.shape)  10.8 us
    all_to_all x1, starting transfers between devices, body(): lax.all_to_all(spread, 'blk', 0, 0, tiled=True)  7.6 us
    pallas_call x1, Pallas kernels, corr_call(): pl.pallas_call(kernel, grid=(1,), in_specs=[whole(a) for a in operands],...  7.17 us
    all_to_all x1, starting transfers between devices, all_sum(): return lax.all_to_all(spread, axes, 0, 0, tiled=True).reshape(x.shape)  6.34 us
    broadcast_in_dim x1, local copies, waits for them, and re-layouts, body(): spread = jnp.broadcast_to(second_in[None], (n_blk,) + second_in.shape)  2.01 us
  transfers between devices with their start and end apart: 4, of which 4 were waited for; matrix products, arithmetic and copies ran while one was open for 2% of the time, Pallas kernels for 0%

profile of v9, /device:TPU:1, one launch (start us, length us, event | category | flops | bytes accessed | tf_op | source)
XLA Modules:
  0.0 79.6 jit_solution(14192348228760677997)
XLA Ops:
  0.6 2.0 %broadcast_in_dim.17 = bf16[8,512,128]{2,1,0:T(8,128)(2,1)} broadcast(bf16[512,128]{1,0:T(8,128)(2,1)} %bitcast.21), dimensions={1,2} | broadcast | bytes 1179648 | tf_op jit(solution)/shard_map/broadcast_in_dim | solution.py:86
  2.6 0.0 copy-start.2
  2.6 0.0 copy-start
  2.6 7.6 %all-to-all-start = ((bf16[8,512,128]{2,1,0:T(8,128)(2,1)}), bf16[8,512,128]{2,1,0:T(8,128)(2,1)S(1)}, u32[]{:S(2)}, u32[]{:S(2)}) async-start(bf16[8,512,128]{2,1,0:T(8,128)(2,1)} %broadcast_in_dim.17), calls=%async_computation | async-start | bytes 2097152 | tf_op jit(solution)/shard_map/all_to_all | solution.py:87
  10.3 0.0 copy-done.2
  10.3 0.0 copy-done
  10.3 0.0 copy-done.1
  10.3 0.2 fusion.ff_ref
  10.5 0.1 copy.8.grad_ref
  10.7 0.1 fusion.2
  10.8 15.1 %all-to-all-done = bf16[8,512,128]{2,1,0:T(8,128)(2,1)S(1)} async-done(((bf16[8,512,128]{2,1,0:T(8,128)(2,1)}), bf16[8,512,128]{2,1,0:T(8,128)(2,1)S(1)}, u32[]{:S(2)}, u32[]{:S(2)}) %all-to-all-start) | async-done | bytes 1048608 | tf_op jit(solution)/shard_map/all_to_all | solution.py:87
  25.9 7.2 %shard_map.59 = (f32[512,2]{1,0:T(8,128)S(1)}, f32[128,256]{1,0:T(8,128)S(1)}) custom-call(bf16[512,256]{1,0:T(8,128)(2,1)S(1)} %fusion.ff_ref, bf16[512,128]{1,0:T(8,128)(2,1)S(1)} %bitcast.20, bf16[4096,128]{1,0:T(8,128)(2,1)S(1)} %bitcast.19, bf16[128,256]{1,0:T(8,128)(2,1)S(1)} %copy-done.1, f32[2,4096]{1,0:T(2,128)S(1)} %pad_maximum_fusion.coord_ref, ...), custom_call_target="tpu_custom_call" | custom-call | tf_op jit(solution)/shard_map/pallas_call | solution.py:63
  33.0 1.3 %collective-permute-start = (f32[128,256]{1,0:T(8,128)S(1)}, f32[128,256]{1,0:T(8,128)S(1)}, u32[]{:S(2)}, u32[]{:S(2)}) collective-permute-start(f32[128,256]{1,0:T(8,128)S(1)} %get-tuple-element.5), channel_id=1, source_target_pairs={{0,1},{1,0},{2,3},{3,2},{4,5},{5,4},{6,7},{7,6},{8,9},{9,8},{10,11... | collective-permute-start | bytes 393224 | tf_op jit(solution)/shard_map/ppermute | solution.py:97
  34.4 1.0 %collective-permute-done = f32[128,256]{1,0:T(8,128)S(1)} collective-permute-done((f32[128,256]{1,0:T(8,128)S(1)}, f32[128,256]{1,0:T(8,128)S(1)}, u32[]{:S(2)}, u32[]{:S(2)}) %collective-permute-start) | collective-permute-done | bytes 131104 | tf_op jit(solution)/shard_map/ppermute | solution.py:97
  35.4 0.8 copy.9
  36.2 12.6 %all-to-all-start.1 = ((f32[128,1,256]{2,1,0:T(1,128)}), f32[128,1,256]{2,1,0:T(1,128)S(1)}, u32[]{:S(2)}, u32[]{:S(2)}) async-start(f32[128,1,256]{2,1,0:T(1,128)} %copy.9), calls=%async_computation.1 | async-start | bytes 262144 | tf_op jit(solution)/shard_map/all_to_all | solution.py:22
  48.8 0.3 slice_reduce_fusion.1
  49.2 11.1 %all-to-all-done.1 = f32[128,1,256]{2,1,0:T(1,128)S(1)} async-done(((f32[128,1,256]{2,1,0:T(1,128)}), f32[128,1,256]{2,1,0:T(1,128)S(1)}, u32[]{:S(2)}, u32[]{:S(2)}) %all-to-all-start.1) | async-done | bytes 131104 | tf_op jit(solution)/shard_map/all_to_all | solution.py:22
  60.3 0.2 reduce_sum.9
  60.4 0.7 broadcast_in_dim.19
  61.2 6.3 %all-to-all-start.2 = ((f32[128,1,256]{2,1,0:T(1,128)}), f32[128,1,256]{2,1,0:T(1,128)S(1)}, u32[]{:S(2)}, u32[]{:S(2)}) async-start(f32[128,1,256]{2,1,0:T(1,128)} %broadcast_in_dim.19), calls=%async_computation.2 | async-start | bytes 262144 | tf_op jit(solution)/shard_map/all_to_all | solution.py:24
  67.5 0.6 maximum_bitcast_fusion
  68.1 10.8 %all-to-all-done.2 = f32[128,1,256]{2,1,0:T(1,128)S(1)} async-done(((f32[128,1,256]{2,1,0:T(1,128)}), f32[128,1,256]{2,1,0:T(1,128)S(1)}, u32[]{:S(2)}, u32[]{:S(2)}) %all-to-all-start.2) | async-done | bytes 131104 | tf_op jit(solution)/shard_map/all_to_all | solution.py:24
  78.9 0.7 copy.12
  (7 shorter events, 0.1 us)
Async XLA Ops:
  2.6 7.6 %copy-start.2 = (f32[1,2,512]{2,1,0:T(2,128)S(1)}, f32[1,2,512]{2,1,0:T(2,128)}, u32[]{:S(2)}) copy-start(f32[1,2,512]{2,1,0:T(2,128)} %param.7) | copy-start | bytes 12292
  2.6 7.6 %copy-start = (bf16[1,512,128]{2,1,0:T(8,128)(2,1)S(1)}, bf16[1,512,128]{2,1,0:T(8,128)(2,1)}, u32[]{:S(2)}) copy-start(bf16[1,512,128]{2,1,0:T(8,128)(2,1)} %param.4) | copy-start | bytes 393220
  2.6 7.6 %copy-start.1 = (bf16[128,256]{1,0:T(8,128)(2,1)S(1)}, bf16[128,256]{1,0:T(8,128)(2,1)}, u32[]{:S(2)}) copy-start(bf16[128,256]{1,0:T(8,128)(2,1)} %w_ref.1) | copy-start | bytes 196612
  2.6 23.2 %all-to-all-start = ((bf16[8,512,128]{2,1,0:T(8,128)(2,1)}), bf16[8,512,128]{2,1,0:T(8,128)(2,1)S(1)}, u32[]{:S(2)}, u32[]{:S(2)}) async-start(bf16[8,512,128]{2,1,0:T(8,128)(2,1)} %broadcast_in_dim.17), calls=%async_computation | async-start | bytes 2097152 | tf_op jit(solution)/shard_map/all_to_all | solution.py:87
  33.0 2.3 %collective-permute-start = (f32[128,256]{1,0:T(8,128)S(1)}, f32[128,256]{1,0:T(8,128)S(1)}, u32[]{:S(2)}, u32[]{:S(2)}) collective-permute-start(f32[128,256]{1,0:T(8,128)S(1)} %get-tuple-element.5), channel_id=1, source_target_pairs={{0,1},{1,0},{2,3},{3,2},{4,5},{5,4},{6,7},{7,6},{8,9},{9,8},{10,11... | collective-permute-start | bytes 393224 | tf_op jit(solution)/shard_map/ppermute | solution.py:97
  36.2 24.1 %all-to-all-start.1 = ((f32[128,1,256]{2,1,0:T(1,128)}), f32[128,1,256]{2,1,0:T(1,128)S(1)}, u32[]{:S(2)}, u32[]{:S(2)}) async-start(f32[128,1,256]{2,1,0:T(1,128)} %copy.9), calls=%async_computation.1 | async-start | bytes 262144 | tf_op jit(solution)/shard_map/all_to_all | solution.py:22
  61.2 17.8 %all-to-all-start.2 = ((f32[128,1,256]{2,1,0:T(1,128)}), f32[128,1,256]{2,1,0:T(1,128)S(1)}, u32[]{:S(2)}, u32[]{:S(2)}) async-start(f32[128,1,256]{2,1,0:T(1,128)} %broadcast_in_dim.19), calls=%async_computation.2 | async-start | bytes 262144 | tf_op jit(solution)/shard_map/all_to_all | solution.py:24

commit v10 on v9

--- a/solution.py
+++ b/solution.py
@@ -22,6 +22,20 @@
     mine = lax.all_to_all(chunks, axes, 0, 0, tiled=True).sum(axis=0)
     spread = jnp.broadcast_to(mine[None], chunks.shape)
     return lax.all_to_all(spread, axes, 0, 0, tiled=True).reshape(x.shape)
+
+
+def copies_kernel(src_ref, out_ref):
+    out_ref[...] = src_ref[...][None]
+
+
+def copies(x, n):
+    return pl.pallas_call(
+        copies_kernel,
+        grid=(n,),
+        in_specs=[pl.BlockSpec(x.shape, lambda i: (0, 0))],
+        out_specs=pl.BlockSpec((1,) + x.shape, lambda i: (i, 0, 0)),
+        out_shape=jax.ShapeDtypeStruct((n,) + x.shape, x.dtype),
+    )(x)
 
 
 def corr_kernel(ff_ref, qin_ref, kin_ref, w_ref, coord_ref, grad_ref, mean_ref, lg_ref, *, scaling):
@@ -83,7 +97,7 @@
     scaling = channels ** (-0.5)
     blk = lax.axis_index("blk")
 
-    spread = jnp.broadcast_to(second_in[None], (n_blk,) + second_in.shape)
+    spread = copies(second_in, n_blk)
     key_in = lax.all_to_all(spread, "blk", 0, 0, tiled=True).reshape(-1, second_in.shape[1])
     key_col, key_row = coords_of(jnp.arange(key_in.shape[0], dtype=jnp.int32))
     own_col, own_row = coords_of(blk * query_count + jnp.arange(query_count, dtype=jnp.int32))

time: 79.9 us -> 81.5 us (1.020)
  Pallas kernels: 7.17 us -> 10.8 us
  local copies, waits for them, and re-layouts: 4.66 us -> 2.65 us
    pallas_call x0 -> x1, Pallas kernels: none -> 3.61 us  [copies(): pl.pallas_call(copies_kernel, grid=(n,), in_specs=[pl.BlockSpec(x.shape,...]
    broadcast_in_dim x1 -> x0, local copies, waits for them, and re-layouts: 2.01 us -> none  [body(): spread = jnp.broadcast_to(second_in[None], (n_blk,) + second_in.shape)]
where the time goes in v10:
time: 81.5 us; the launch traced here: 81.2 us
  waiting for transfers between devices  38 us (47%)
  starting transfers between devices  27.9 us (34%)
  Pallas kernels  10.8 us (13%)
  local copies, waits for them, and re-layouts  2.65 us (3%)
  other arithmetic  0.93 us (1%)
    all_to_all x1, waiting for transfers between devices, body(): lax.all_to_all(spread, 'blk', 0, 0, tiled=True)  15.1 us
    all_to_all x1, starting transfers between devices, all_sum(): mine = lax.all_to_all(chunks, axes, 0, 0, tiled=True).sum(axis=0)  12.7 us
    all_to_all x1, waiting for transfers between devices, all_sum(): mine = lax.all_to_all(chunks, axes, 0, 0, tiled=True).sum(axis=0)  11.1 us
    all_to_all x1, waiting for transfers between devices, all_sum(): return lax.all_to_all(spread, axes, 0, 0, tiled=True).reshape(x.shape)  10.8 us
    all_to_all x1, starting transfers between devices, body(): lax.all_to_all(spread, 'blk', 0, 0, tiled=True)  7.6 us
    pallas_call x1, Pallas kernels, corr_call(): pl.pallas_call(kernel, grid=(1,), in_specs=[whole(a) for a in operands],...  7.16 us
    all_to_all x1, starting transfers between devices, all_sum(): return lax.all_to_all(spread, axes, 0, 0, tiled=True).reshape(x.shape)  6.34 us
    pallas_call x1, Pallas kernels, copies(): pl.pallas_call(copies_kernel, grid=(n,), in_specs=[pl.BlockSpec(x.shape,...  3.61 us
  transfers between devices with their start and end apart: 4, of which 4 were waited for; matrix products, arithmetic and copies ran while one was open for 2% of the time, Pallas kernels for 0%

profile of v10, /device:TPU:1, one launch (start us, length us, event | category | flops | bytes accessed | tf_op | source)
XLA Modules:
  0.0 81.2 jit_solution(15256842825831750890)
XLA Ops:
  0.6 3.6 %shard_map.59 = bf16[8,512,128]{2,1,0:T(8,128)(2,1)} custom-call(bf16[512,128]{1,0:T(8,128)(2,1)} %bitcast.21), custom_call_target="tpu_custom_call" | custom-call | tf_op jit(solution)/shard_map/pallas_call | solution.py:32
  4.2 0.0 copy-start.2
  4.2 0.0 copy-start
  4.2 7.6 %all-to-all-start = ((bf16[8,512,128]{2,1,0:T(8,128)(2,1)}), bf16[8,512,128]{2,1,0:T(8,128)(2,1)S(1)}, u32[]{:S(2)}, u32[]{:S(2)}) async-start(bf16[8,512,128]{2,1,0:T(8,128)(2,1)} %shard_map.59), calls=%async_computation | async-start | bytes 2097152 | tf_op jit(solution)/shard_map/all_to_all | solution.py:101
  11.8 0.0 copy-done.2
  11.9 0.0 copy-done
  11.9 0.0 copy-done.1
  11.9 0.2 fusion.ff_ref
  12.1 0.1 copy.8.grad_ref
  12.3 0.1 fusion.2
  12.4 15.1 %all-to-all-done = bf16[8,512,128]{2,1,0:T(8,128)(2,1)S(1)} async-done(((bf16[8,512,128]{2,1,0:T(8,128)(2,1)}), bf16[8,512,128]{2,1,0:T(8,128)(2,1)S(1)}, u32[]{:S(2)}, u32[]{:S(2)}) %all-to-all-start) | async-done | bytes 1048608 | tf_op jit(solution)/shard_map/all_to_all | solution.py:101
  27.5 7.2 %shard_map.60 = (f32[512,2]{1,0:T(8,128)S(1)}, f32[128,256]{1,0:T(8,128)S(1)}) custom-call(bf16[512,256]{1,0:T(8,128)(2,1)S(1)} %fusion.ff_ref, bf16[512,128]{1,0:T(8,128)(2,1)S(1)} %bitcast.20, bf16[4096,128]{1,0:T(8,128)(2,1)S(1)} %bitcast.19, bf16[128,256]{1,0:T(8,128)(2,1)S(1)} %copy-done.1, f32[2,4096]{1,0:T(2,128)S(1)} %pad_maximum_fusion.coord_ref, ...), custom_call_target="tpu_custom_call" | custom-call | tf_op jit(solution)/shard_map/pallas_call | solution.py:77
  34.6 1.4 %collective-permute-start = (f32[128,256]{1,0:T(8,128)S(1)}, f32[128,256]{1,0:T(8,128)S(1)}, u32[]{:S(2)}, u32[]{:S(2)}) collective-permute-start(f32[128,256]{1,0:T(8,128)S(1)} %get-tuple-element.5), channel_id=1, source_target_pairs={{0,1},{1,0},{2,3},{3,2},{4,5},{5,4},{6,7},{7,6},{8,9},{9,8},{10,11... | collective-permute-start | bytes 393224 | tf_op jit(solution)/shard_map/ppermute | solution.py:111
  36.0 1.0 %collective-permute-done = f32[128,256]{1,0:T(8,128)S(1)} collective-permute-done((f32[128,256]{1,0:T(8,128)S(1)}, f32[128,256]{1,0:T(8,128)S(1)}, u32[]{:S(2)}, u32[]{:S(2)}) %collective-permute-start) | collective-permute-done | bytes 131104 | tf_op jit(solution)/shard_map/ppermute | solution.py:111
  37.0 0.8 copy.9
  37.8 12.7 %all-to-all-start.1 = ((f32[128,1,256]{2,1,0:T(1,128)}), f32[128,1,256]{2,1,0:T(1,128)S(1)}, u32[]{:S(2)}, u32[]{:S(2)}) async-start(f32[128,1,256]{2,1,0:T(1,128)} %copy.9), calls=%async_computation.1 | async-start | bytes 262144 | tf_op jit(solution)/shard_map/all_to_all | solution.py:22
  50.4 0.3 slice_reduce_fusion.1
  50.8 11.1 %all-to-all-done.1 = f32[128,1,256]{2,1,0:T(1,128)S(1)} async-done(((f32[128,1,256]{2,1,0:T(1,128)}), f32[128,1,256]{2,1,0:T(1,128)S(1)}, u32[]{:S(2)}, u32[]{:S(2)}) %all-to-all-start.1) | async-done | bytes 131104 | tf_op jit(solution)/shard_map/all_to_all | solution.py:22
  61.9 0.2 reduce_sum.9
  62.1 0.7 broadcast_in_dim.10
  62.8 6.3 %all-to-all-start.2 = ((f32[128,1,256]{2,1,0:T(1,128)}), f32[128,1,256]{2,1,0:T(1,128)S(1)}, u32[]{:S(2)}, u32[]{:S(2)}) async-start(f32[128,1,256]{2,1,0:T(1,128)} %broadcast_in_dim.10), calls=%async_computation.2 | async-start | bytes 262144 | tf_op jit(solution)/shard_map/all_to_all | solution.py:24
  69.2 0.6 maximum_bitcast_fusion
  69.8 10.8 %all-to-all-done.2 = f32[128,1,256]{2,1,0:T(1,128)S(1)} async-done(((f32[128,1,256]{2,1,0:T(1,128)}), f32[128,1,256]{2,1,0:T(1,128)S(1)}, u32[]{:S(2)}, u32[]{:S(2)}) %all-to-all-start.2) | async-done | bytes 131104 | tf_op jit(solution)/shard_map/all_to_all | solution.py:24
  80.5 0.7 copy.12
  (7 shorter events, 0.1 us)
Async XLA Ops:
  4.2 7.6 %copy-start.2 = (f32[1,2,512]{2,1,0:T(2,128)S(1)}, f32[1,2,512]{2,1,0:T(2,128)}, u32[]{:S(2)}) copy-start(f32[1,2,512]{2,1,0:T(2,128)} %param.7) | copy-start | bytes 12292
  4.2 7.6 %copy-start = (bf16[1,512,128]{2,1,0:T(8,128)(2,1)S(1)}, bf16[1,512,128]{2,1,0:T(8,128)(2,1)}, u32[]{:S(2)}) copy-start(bf16[1,512,128]{2,1,0:T(8,128)(2,1)} %param.4) | copy-start | bytes 393220
  4.2 7.6 %copy-start.1 = (bf16[128,256]{1,0:T(8,128)(2,1)S(1)}, bf16[128,256]{1,0:T(8,128)(2,1)}, u32[]{:S(2)}) copy-start(bf16[128,256]{1,0:T(8,128)(2,1)} %w_ref.1) | copy-start | bytes 196612
  4.2 23.2 %all-to-all-start = ((bf16[8,512,128]{2,1,0:T(8,128)(2,1)}), bf16[8,512,128]{2,1,0:T(8,128)(2,1)S(1)}, u32[]{:S(2)}, u32[]{:S(2)}) async-start(bf16[8,512,128]{2,1,0:T(8,128)(2,1)} %shard_map.59), calls=%async_computation | async-start | bytes 2097152 | tf_op jit(solution)/shard_map/all_to_all | solution.py:101
  34.6 2.3 %collective-permute-start = (f32[128,256]{1,0:T(8,128)S(1)}, f32[128,256]{1,0:T(8,128)S(1)}, u32[]{:S(2)}, u32[]{:S(2)}) collective-permute-start(f32[128,256]{1,0:T(8,128)S(1)} %get-tuple-element.5), channel_id=1, source_target_pairs={{0,1},{1,0},{2,3},{3,2},{4,5},{5,4},{6,7},{7,6},{8,9},{9,8},{10,11... | collective-permute-start | bytes 393224 | tf_op jit(solution)/shard_map/ppermute | solution.py:111
  37.8 24.1 %all-to-all-start.1 = ((f32[128,1,256]{2,1,0:T(1,128)}), f32[128,1,256]{2,1,0:T(1,128)S(1)}, u32[]{:S(2)}, u32[]{:S(2)}) async-start(f32[128,1,256]{2,1,0:T(1,128)} %copy.9), calls=%async_computation.1 | async-start | bytes 262144 | tf_op jit(solution)/shard_map/all_to_all | solution.py:22
  62.8 17.8 %all-to-all-start.2 = ((f32[128,1,256]{2,1,0:T(1,128)}), f32[128,1,256]{2,1,0:T(1,128)S(1)}, u32[]{:S(2)}, u32[]{:S(2)}) async-start(f32[128,1,256]{2,1,0:T(1,128)} %broadcast_in_dim.10), calls=%async_computation.2 | async-start | bytes 262144 | tf_op jit(solution)/shard_map/all_to_all | solution.py:24

commit v11 on v9

--- a/solution.py
+++ b/solution.py
@@ -94,8 +94,7 @@
     grads = jnp.stack([grad_col, grad_row], axis=1)
     means, local_grad = corr_call(first_feat, first_in, key_in, encoder_weight, coords, grads, scaling)
     flow = jnp.stack([means[:, 0] - own_col, means[:, 1] - own_row])[None]
-    local_grad = local_grad + lax.ppermute(local_grad, "core", [(0, 1), (1, 0)])
-    grad_w = all_sum(local_grad, ("blk", "chip"), n_blk * n_batch // 2)
+    grad_w = all_sum(local_grad, ("blk", "chip", "core"), n_blk * n_batch)
     return (flow, grad_w)
 
 

time: 79.9 us -> 81.4 us (1.019)
  waiting for transfers between devices: 38 us -> 40 us
  starting transfers between devices: 27.9 us -> 26 us
  other arithmetic: 0.93 us -> 2 us
    all_to_all x1, waiting for transfers between devices: 10.8 us -> 12.4 us  [all_sum(): return lax.all_to_all(spread, axes, 0, 0, tiled=True).reshape(x.shape)]
    all_to_all x1, waiting for transfers between devices: 11.1 us -> 12.5 us  [all_sum(): mine = lax.all_to_all(chunks, axes, 0, 0, tiled=True).sum(axis=0)]
    ppermute x1 -> x0, starting transfers between devices: 1.33 us -> none  [body(): local_grad = local_grad + lax.ppermute(local_grad, 'core', [(0, 1), (1, 0)])]
    ppermute x1 -> x0, waiting for transfers between devices: 0.99 us -> none  [body(): local_grad = local_grad + lax.ppermute(local_grad, 'core', [(0, 1), (1, 0)])]
    all_to_all x1, other arithmetic: 0.02 us -> 0.95 us  [all_sum(): return lax.all_to_all(spread, axes, 0, 0, tiled=True).reshape(x.shape)]
  transfers between devices with their start and end apart: 4 -> 3, of which waited for: 4 -> 3; matrix products, arithmetic and copies ran while one was open for 2% -> 2% of each run, Pallas kernels for 0% -> 0%
where the time goes in v11:
time: 81.4 us; the launch traced here: 81.1 us
  waiting for transfers between devices  40 us (49%)
  starting transfers between devices  26 us (32%)
  Pallas kernels  7.16 us (9%)
  local copies, waits for them, and re-layouts  5.08 us (6%)
  other arithmetic  2 us (2%)
    all_to_all x1, waiting for transfers between devices, body(): lax.all_to_all(spread, 'blk', 0, 0, tiled=True)  15.1 us
    all_to_all x1, starting transfers between devices, all_sum(): mine = lax.all_to_all(chunks, axes, 0, 0, tiled=True).sum(axis=0)  12.6 us
    all_to_all x1, waiting for transfers between devices, all_sum(): mine = lax.all_to_all(chunks, axes, 0, 0, tiled=True).sum(axis=0)  12.5 us
    all_to_all x1, waiting for transfers between devices, all_sum(): return lax.all_to_all(spread, axes, 0, 0, tiled=True).reshape(x.shape)  12.4 us
    all_to_all x1, starting transfers between devices, body(): lax.all_to_all(spread, 'blk', 0, 0, tiled=True)  7.6 us
    pallas_call x1, Pallas kernels, corr_call(): pl.pallas_call(kernel, grid=(1,), in_specs=[whole(a) for a in operands],...  7.16 us
    all_to_all x1, starting transfers between devices, all_sum(): return lax.all_to_all(spread, axes, 0, 0, tiled=True).reshape(x.shape)  5.84 us
    broadcast_in_dim x1, local copies, waits for them, and re-layouts, body(): spread = jnp.broadcast_to(second_in[None], (n_blk,) + second_in.shape)  2.02 us
  transfers between devices with their start and end apart: 3, of which 3 were waited for; matrix products, arithmetic and copies ran while one was open for 2% of the time, Pallas kernels for 0%

profile of v11, /device:TPU:1, one launch (start us, length us, event | category | flops | bytes accessed | tf_op | source)
XLA Modules:
  0.0 81.1 jit_solution(2661240994586634341)
XLA Ops:
  0.6 2.0 %broadcast_in_dim.17 = bf16[8,512,128]{2,1,0:T(8,128)(2,1)} broadcast(bf16[512,128]{1,0:T(8,128)(2,1)} %bitcast.17), dimensions={1,2} | broadcast | bytes 1179648 | tf_op jit(solution)/shard_map/broadcast_in_dim | solution.py:86
  2.6 0.0 copy-start.2
  2.6 0.0 copy-start
  2.7 7.6 %all-to-all-start = ((bf16[8,512,128]{2,1,0:T(8,128)(2,1)}), bf16[8,512,128]{2,1,0:T(8,128)(2,1)S(1)}, u32[]{:S(2)}, u32[]{:S(2)}) async-start(bf16[8,512,128]{2,1,0:T(8,128)(2,1)} %broadcast_in_dim.17), calls=%async_computation | async-start | bytes 2097152 | tf_op jit(solution)/shard_map/all_to_all | solution.py:87
  10.3 0.0 copy-done.2
  10.3 0.0 copy-done
  10.3 0.0 copy-done.1
  10.3 0.2 fusion.ff_ref
  10.5 0.1 copy.8.grad_ref
  10.7 0.1 fusion.2
  10.8 15.1 %all-to-all-done = bf16[8,512,128]{2,1,0:T(8,128)(2,1)S(1)} async-done(((bf16[8,512,128]{2,1,0:T(8,128)(2,1)}), bf16[8,512,128]{2,1,0:T(8,128)(2,1)S(1)}, u32[]{:S(2)}, u32[]{:S(2)}) %all-to-all-start) | async-done | bytes 1048608 | tf_op jit(solution)/shard_map/all_to_all | solution.py:87
  25.9 7.2 %shard_map.59 = (f32[512,2]{1,0:T(8,128)S(1)}, f32[128,256]{1,0:T(8,128)S(1)}) custom-call(bf16[512,256]{1,0:T(8,128)(2,1)S(1)} %fusion.ff_ref, bf16[512,128]{1,0:T(8,128)(2,1)S(1)} %bitcast.16, bf16[4096,128]{1,0:T(8,128)(2,1)S(1)} %bitcast.15, bf16[128,256]{1,0:T(8,128)(2,1)S(1)} %copy-done.1, f32[2,4096]{1,0:T(2,128)S(1)} %pad_maximum_fusion.coord_ref, ...), custom_call_target="tpu_custom_call" | custom-call | tf_op jit(solution)/shard_map/pallas_call | solution.py:63
  33.0 0.7 all_to_all.14
  33.7 12.6 %all-to-all-start.1 = ((f32[256,1,128]{2,1,0:T(1,128)}), f32[256,1,128]{2,1,0:T(1,128)S(1)}, u32[]{:S(2)}, u32[]{:S(2)}) async-start(f32[256,1,128]{2,1,0:T(1,128)} %bitcast.6), calls=%async_computation.1 | async-start | bytes 262144 | tf_op jit(solution)/shard_map/all_to_all | solution.py:22
  46.3 0.3 slice_reduce_fusion.1
  46.6 12.5 %all-to-all-done.1 = f32[256,1,128]{2,1,0:T(1,128)S(1)} async-done(((f32[256,1,128]{2,1,0:T(1,128)}), f32[256,1,128]{2,1,0:T(1,128)S(1)}, u32[]{:S(2)}, u32[]{:S(2)}) %all-to-all-start.1) | async-done | bytes 131104 | tf_op jit(solution)/shard_map/all_to_all | solution.py:22
  59.1 0.3 reduce_sum.9
  59.4 0.7 broadcast_in_dim.19
  60.1 5.8 %all-to-all-start.2 = ((f32[256,1,128]{2,1,0:T(1,128)}), f32[256,1,128]{2,1,0:T(1,128)S(1)}, u32[]{:S(2)}, u32[]{:S(2)}) async-start(f32[256,1,128]{2,1,0:T(1,128)} %broadcast_in_dim.19), calls=%async_computation.2 | async-start | bytes 262144 | tf_op jit(solution)/shard_map/all_to_all | solution.py:24
  66.0 0.6 maximum_bitcast_fusion
  66.6 12.4 %all-to-all-done.2 = f32[256,1,128]{2,1,0:T(1,128)S(1)} async-done(((f32[256,1,128]{2,1,0:T(1,128)}), f32[256,1,128]{2,1,0:T(1,128)S(1)}, u32[]{:S(2)}, u32[]{:S(2)}) %all-to-all-start.2) | async-done | bytes 131104 | tf_op jit(solution)/shard_map/all_to_all | solution.py:24
  79.0 0.5 broadcast.171
  79.5 0.9 %reduce.8 = f32[256,128]{1,0:T(8,128)S(1)} reduce(f32[256,1,128]{2,1,0:T(1,128)S(1)} %all-to-all-done.2, f32[]{:T(128)} %broadcast.171), dimensions={1}, to_apply=%all_to_all.16.reduce_sub_computation.3 | reduce | bytes 262148 | tf_op jit(solution)/shard_map/all_to_all | solution.py:24
  80.4 0.7 reshape.157
  (6 shorter events, 0.1 us)
Async XLA Ops:
  2.6 7.6 %copy-start.2 = (f32[1,2,512]{2,1,0:T(2,128)S(1)}, f32[1,2,512]{2,1,0:T(2,128)}, u32[]{:S(2)}) copy-start(f32[1,2,512]{2,1,0:T(2,128)} %param.7) | copy-start | bytes 12292
  2.6 7.6 %copy-start = (bf16[1,512,128]{2,1,0:T(8,128)(2,1)S(1)}, bf16[1,512,128]{2,1,0:T(8,128)(2,1)}, u32[]{:S(2)}) copy-start(bf16[1,512,128]{2,1,0:T(8,128)(2,1)} %param.4) | copy-start | bytes 393220
  2.7 7.6 %copy-start.1 = (bf16[128,256]{1,0:T(8,128)(2,1)S(1)}, bf16[128,256]{1,0:T(8,128)(2,1)}, u32[]{:S(2)}) copy-start(bf16[128,256]{1,0:T(8,128)(2,1)} %w_ref.1) | copy-start | bytes 196612
  2.7 23.2 %all-to-all-start = ((bf16[8,512,128]{2,1,0:T(8,128)(2,1)}), bf16[8,512,128]{2,1,0:T(8,128)(2,1)S(1)}, u32[]{:S(2)}, u32[]{:S(2)}) async-start(bf16[8,512,128]{2,1,0:T(8,128)(2,1)} %broadcast_in_dim.17), calls=%async_computation | async-start | bytes 2097152 | tf_op jit(solution)/shard_map/all_to_all | solution.py:87
  33.7 25.4 %all-to-all-start.1 = ((f32[256,1,128]{2,1,0:T(1,128)}), f32[256,1,128]{2,1,0:T(1,128)S(1)}, u32[]{:S(2)}, u32[]{:S(2)}) async-start(f32[256,1,128]{2,1,0:T(1,128)} %bitcast.6), calls=%async_computation.1 | async-start | bytes 262144 | tf_op jit(solution)/shard_map/all_to_all | solution.py:22
  60.1 18.8 %all-to-all-start.2 = ((f32[256,1,128]{2,1,0:T(1,128)}), f32[256,1,128]{2,1,0:T(1,128)S(1)}, u32[]{:S(2)}, u32[]{:S(2)}) async-start(f32[256,1,128]{2,1,0:T(1,128)} %broadcast_in_dim.19), calls=%async_computation.2 | async-start | bytes 262144 | tf_op jit(solution)/shard_map/all_to_all | solution.py:24

commit v12 on v9

--- a/solution.py
+++ b/solution.py
@@ -20,6 +20,7 @@
 def all_sum(x, axes, n):
     chunks = x.reshape(n, -1)
     mine = lax.all_to_all(chunks, axes, 0, 0, tiled=True).sum(axis=0)
+    mine = mine + lax.ppermute(mine, "core", [(0, 1), (1, 0)])
     spread = jnp.broadcast_to(mine[None], chunks.shape)
     return lax.all_to_all(spread, axes, 0, 0, tiled=True).reshape(x.shape)
 
@@ -94,7 +95,6 @@
     grads = jnp.stack([grad_col, grad_row], axis=1)
     means, local_grad = corr_call(first_feat, first_in, key_in, encoder_weight, coords, grads, scaling)
     flow = jnp.stack([means[:, 0] - own_col, means[:, 1] - own_row])[None]
-    local_grad = local_grad + lax.ppermute(local_grad, "core", [(0, 1), (1, 0)])
     grad_w = all_sum(local_grad, ("blk", "chip"), n_blk * n_batch // 2)
     return (flow, grad_w)
 

time: 79.9 us -> 80.9 us (1.013)
  starting transfers between devices: 27.9 us -> 28.9 us
    ppermute x1, starting transfers between devices: 1.33 us -> 2.35 us  [all_sum(): mine = mine + lax.ppermute(mine, 'core', [(0, 1), (1, 0)])]
where the time goes in v12:
time: 80.9 us; the launch traced here: 80.6 us
  waiting for transfers between devices  38 us (47%)
  starting transfers between devices  28.9 us (36%)
  Pallas kernels  7.17 us (9%)
  local copies, waits for them, and re-layouts  4.66 us (6%)
  other arithmetic  0.92 us (1%)
    all_to_all x1, waiting for transfers between devices, body(): lax.all_to_all(spread, 'blk', 0, 0, tiled=True)  15.1 us
    all_to_all x1, starting transfers between devices, all_sum(): mine = lax.all_to_all(chunks, axes, 0, 0, tiled=True).sum(axis=0)  12.8 us
    all_to_all x1, waiting for transfers between devices, all_sum(): return lax.all_to_all(spread, axes, 0, 0, tiled=True).reshape(x.shape)  11.1 us
    all_to_all x1, waiting for transfers between devices, all_sum(): mine = lax.all_to_all(chunks, axes, 0, 0, tiled=True).sum(axis=0)  11 us
    all_to_all x1, starting transfers between devices, body(): lax.all_to_all(spread, 'blk', 0, 0, tiled=True)  7.6 us
    pallas_call x1, Pallas kernels, corr_call(): pl.pallas_call(kernel, grid=(1,), in_specs=[whole(a) for a in operands],...  7.17 us
    all_to_all x1, starting transfers between devices, all_sum(): return lax.all_to_all(spread, axes, 0, 0, tiled=True).reshape(x.shape)  6.17 us
    ppermute x1, starting transfers between devices, all_sum(): mine = mine + lax.ppermute(mine, 'core', [(0, 1), (1, 0)])  2.35 us
  transfers between devices with their start and end apart: 4, of which 4 were waited for; matrix products, arithmetic and copies ran while one was open for 2% of the time, Pallas kernels for 0%

profile of v12, /device:TPU:1, one launch (start us, length us, event | category | flops | bytes accessed | tf_op | source)
XLA Modules:
  0.0 80.6 jit_solution(9326214907619672750)
XLA Ops:
  0.6 2.0 %broadcast_in_dim.17 = bf16[8,512,128]{2,1,0:T(8,128)(2,1)} broadcast(bf16[512,128]{1,0:T(8,128)(2,1)} %bitcast.21), dimensions={1,2} | broadcast | bytes 1179648 | tf_op jit(solution)/shard_map/broadcast_in_dim | solution.py:87
  2.6 0.0 copy-start.2
  2.6 0.0 copy-start
  2.6 7.6 %all-to-all-start = ((bf16[8,512,128]{2,1,0:T(8,128)(2,1)}), bf16[8,512,128]{2,1,0:T(8,128)(2,1)S(1)}, u32[]{:S(2)}, u32[]{:S(2)}) async-start(bf16[8,512,128]{2,1,0:T(8,128)(2,1)} %broadcast_in_dim.17), calls=%async_computation | async-start | bytes 2097152 | tf_op jit(solution)/shard_map/all_to_all | solution.py:88
  10.3 0.0 copy-done.2
  10.3 0.0 copy-done
  10.3 0.0 copy-done.1
  10.3 0.2 fusion.ff_ref
  10.5 0.1 copy.8.grad_ref
  10.7 0.1 fusion.2
  10.8 15.1 %all-to-all-done = bf16[8,512,128]{2,1,0:T(8,128)(2,1)S(1)} async-done(((bf16[8,512,128]{2,1,0:T(8,128)(2,1)}), bf16[8,512,128]{2,1,0:T(8,128)(2,1)S(1)}, u32[]{:S(2)}, u32[]{:S(2)}) %all-to-all-start) | async-done | bytes 1048608 | tf_op jit(solution)/shard_map/all_to_all | solution.py:88
  25.9 7.2 %shard_map.59 = (f32[512,2]{1,0:T(8,128)S(1)}, f32[128,256]{1,0:T(8,128)S(1)}) custom-call(bf16[512,256]{1,0:T(8,128)(2,1)S(1)} %fusion.ff_ref, bf16[512,128]{1,0:T(8,128)(2,1)S(1)} %bitcast.19, bf16[4096,128]{1,0:T(8,128)(2,1)S(1)} %bitcast.18, bf16[128,256]{1,0:T(8,128)(2,1)S(1)} %copy-done.1, f32[2,4096]{1,0:T(2,128)S(1)} %pad_maximum_fusion.coord_ref, ...), custom_call_target="tpu_custom_call" | custom-call | tf_op jit(solution)/shard_map/pallas_call | solution.py:64
  33.0 0.8 copy.9
  33.8 12.8 %all-to-all-start.1 = ((f32[128,1,256]{2,1,0:T(1,128)}), f32[128,1,256]{2,1,0:T(1,128)S(1)}, u32[]{:S(2)}, u32[]{:S(2)}) async-start(f32[128,1,256]{2,1,0:T(1,128)} %copy.9), calls=%async_computation.1 | async-start | bytes 262144 | tf_op jit(solution)/shard_map/all_to_all | solution.py:22
  46.7 0.3 slice_reduce_fusion.1
  47.0 11.0 %all-to-all-done.1 = f32[128,1,256]{2,1,0:T(1,128)S(1)} async-done(((f32[128,1,256]{2,1,0:T(1,128)}), f32[128,1,256]{2,1,0:T(1,128)S(1)}, u32[]{:S(2)}, u32[]{:S(2)}) %all-to-all-start.1) | async-done | bytes 131104 | tf_op jit(solution)/shard_map/all_to_all | solution.py:22
  58.0 0.2 reduce_sum.9
  58.2 2.3 %collective-permute-start = (f32[256]{0:T(256)S(1)}, f32[256]{0:T(256)S(1)}, u32[]{:S(2)}, u32[]{:S(2)}) collective-permute-start(f32[256]{0:T(256)S(1)} %reduce_sum.9), channel_id=1, source_target_pairs={{0,1},{1,0},{2,3},{3,2},{4,5},{5,4},{6,7},{7,6},{8,9},{9,8},{10,11... | collective-permute-start | bytes 3080 | tf_op jit(solution)/shard_map/ppermute | solution.py:23
  60.5 0.8 collective-permute-done
  61.3 0.7 broadcast_in_dim.19
  62.1 6.2 %all-to-all-start.2 = ((f32[128,1,256]{2,1,0:T(1,128)}), f32[128,1,256]{2,1,0:T(1,128)S(1)}, u32[]{:S(2)}, u32[]{:S(2)}) async-start(f32[128,1,256]{2,1,0:T(1,128)} %broadcast_in_dim.19), calls=%async_computation.2 | async-start | bytes 262144 | tf_op jit(solution)/shard_map/all_to_all | solution.py:25
  68.3 0.6 maximum_bitcast_fusion
  68.9 11.1 %all-to-all-done.2 = f32[128,1,256]{2,1,0:T(1,128)S(1)} async-done(((f32[128,1,256]{2,1,0:T(1,128)}), f32[128,1,256]{2,1,0:T(1,128)S(1)}, u32[]{:S(2)}, u32[]{:S(2)}) %all-to-all-start.2) | async-done | bytes 131104 | tf_op jit(solution)/shard_map/all_to_all | solution.py:25
  80.0 0.7 copy.12
  (7 shorter events, 0.1 us)
Async XLA Ops:
  2.6 7.6 %copy-start.2 = (f32[1,2,512]{2,1,0:T(2,128)S(1)}, f32[1,2,512]{2,1,0:T(2,128)}, u32[]{:S(2)}) copy-start(f32[1,2,512]{2,1,0:T(2,128)} %param.7) | copy-start | bytes 12292
  2.6 7.6 %copy-start = (bf16[1,512,128]{2,1,0:T(8,128)(2,1)S(1)}, bf16[1,512,128]{2,1,0:T(8,128)(2,1)}, u32[]{:S(2)}) copy-start(bf16[1,512,128]{2,1,0:T(8,128)(2,1)} %param.4) | copy-start | bytes 393220
  2.6 7.6 %copy-start.1 = (bf16[128,256]{1,0:T(8,128)(2,1)S(1)}, bf16[128,256]{1,0:T(8,128)(2,1)}, u32[]{:S(2)}) copy-start(bf16[128,256]{1,0:T(8,128)(2,1)} %w_ref.1) | copy-start | bytes 196612
  2.6 23.2 %all-to-all-start = ((bf16[8,512,128]{2,1,0:T(8,128)(2,1)}), bf16[8,512,128]{2,1,0:T(8,128)(2,1)S(1)}, u32[]{:S(2)}, u32[]{:S(2)}) async-start(bf16[8,512,128]{2,1,0:T(8,128)(2,1)} %broadcast_in_dim.17), calls=%async_computation | async-start | bytes 2097152 | tf_op jit(solution)/shard_map/all_to_all | solution.py:88
  33.8 24.2 %all-to-all-start.1 = ((f32[128,1,256]{2,1,0:T(1,128)}), f32[128,1,256]{2,1,0:T(1,128)S(1)}, u32[]{:S(2)}, u32[]{:S(2)}) async-start(f32[128,1,256]{2,1,0:T(1,128)} %copy.9), calls=%async_computation.1 | async-start | bytes 262144 | tf_op jit(solution)/shard_map/all_to_all | solution.py:22
  58.2 3.2 %collective-permute-start = (f32[256]{0:T(256)S(1)}, f32[256]{0:T(256)S(1)}, u32[]{:S(2)}, u32[]{:S(2)}) collective-permute-start(f32[256]{0:T(256)S(1)} %reduce_sum.9), channel_id=1, source_target_pairs={{0,1},{1,0},{2,3},{3,2},{4,5},{5,4},{6,7},{7,6},{8,9},{9,8},{10,11... | collective-permute-start | bytes 3080 | tf_op jit(solution)/shard_map/ppermute | solution.py:23
  62.1 17.9 %all-to-all-start.2 = ((f32[128,1,256]{2,1,0:T(1,128)}), f32[128,1,256]{2,1,0:T(1,128)S(1)}, u32[]{:S(2)}, u32[]{:S(2)}) async-start(f32[128,1,256]{2,1,0:T(1,128)} %broadcast_in_dim.19), calls=%async_computation.2 | async-start | bytes 262144 | tf_op jit(solution)/shard_map/all_to_all | solution.py:25
